TPU v7x, 512 devices: a whole 4x4x16 slice. The times are simulated.
512 devices in a mesh: sec: 4 (over x), tile: 32 (over z, core), lev: 4 (over y).
Axes of the slice: x: 4, y: 4, z: 16, core: 2. Of those that a mesh axis runs over, the one named last changes fastest.
Arguments:
- ocean_conc: float32 [8, 4096, 512], P('lev', ('sec', 'tile')), may hold values from 0.1 to 2.9
- flow_lo: bfloat16 [4096, 512], P(('sec', 'tile')), as said below
- flow_hi: bfloat16 [4096, 512], P(('sec', 'tile')), as said below
- flow_y: bfloat16 [4096, 512], P(('sec', 'tile')), as said below
- open_lo: int32 [4096, 512], P(('sec', 'tile')), may hold values from 0 to 1, as said below
- open_hi: int32 [4096, 512], P(('sec', 'tile')), may hold values from 0 to 1
- open_y: int32 [4096, 512], P(('sec', 'tile')), may hold values from 0 to 1, as said below
- settle_rate: float32 [8], P('lev'), may hold values from 0.01 to 0.1
- critical_stress: float32 [8], P('lev'), may hold values from 0.05 to 0.5
- erosion_rate: float32 [8], P('lev'), may hold values from 0.002 to 0.02
- wave_energy: bfloat16 [768, 65536], P('lev', ('sec', 'tile')), may hold values from 0 to 2
- band_angle: float32 [768], P('lev'), may hold values from -3.140625 to 3.140625
- band_speed: float32 [768], P('lev'), may hold values from 0.2 to 0.3
- band_growth: float32 [768], P('lev'), may hold values from 0.05 to 0.5
- band_orbital: float32 [768], P('lev'), may hold values from 0.01 to 0.1
- neighbors: int32 [4, 65536], P(None, ('sec', 'tile')), may hold values from 0 to 65535, as said below
- facing_angle: float32 [4, 65536], P(None, ('sec', 'tile')), may hold values from -3.140625 to 3.140625
- live_nodes: int32 [65536], P(('sec', 'tile')), may hold values 0 or 1
- remap_owner: int32 [8192, 1], P(('sec', 'tile')), may hold values from 0 to 127; in each aligned block of 64 rows (0 to 63, 64 to 127, ...) at most 2 rows name the same one
- remap_slot: int32 [8192], P(('sec', 'tile')), may hold values from 0 to 7
- remap_cell: int32 [8192], P(('sec', 'tile')), may hold values from 0 to 255
- remap_weight: bfloat16 [8192, 64, 64], P(('sec', 'tile')), may hold values from -0.25 to 0.25
Outputs:
- sediment_out: float32 [8, 4096, 512], P('lev', ('sec', 'tile'))
- waves_out: bfloat16 [768, 65536], P('lev', ('sec', 'tile'))
Inputs may be any that keep to these rules, and one draw needn't show every extreme that they name: open_hi of row r equals open_lo of row r + 1; the lower face of the first row and the upper face of the last row are closed. `open_y`: the face after the last column is closed. flow_lo is zero where open_lo is 0, of magnitude at most 0.150390625; flow_hi of row r equals flow_lo of row r + 1. `flow_hi`: zero where open_hi is 0, of magnitude at most 0.150390625. `flow_y`: zero where open_y is 0, of magnitude at most 0.150390625. `neighbors`: each neighbour's index differs from its node's index by at most 128. `remap_owner`: among the 64 entries of one device at most 2 name the same owner.
All inputs are finite; a program needn't handle non-finite values. No bound on the sum of `live_nodes` on one device may be relied on, other than what follows from the above.
Results may differ from a plain program's by a relative error of at most 0.001.
Values sent between devices are 32-bit elements; how exact they have to be, the bound alone decides.
No kernel may reach another device: no remote copies, remote signals or barrier semaphores. Data moves between devices by JAX's collectives and lax.ppermute only.
A program may use at most 64 MiB of HBM per device.

v0:
```python
import jax
import jax.numpy as jnp
from jax import lax
from jax.sharding import PartitionSpec as P

OSTEPS = 4
WSTEPS = 4
NBRS = 4


KAPPA = 0.07
FORCE_SCALE = 5.0
DRAG = 50.0
TAU_CURRENT = 20.0
TAU_WAVES = 10.0
HIGHEST = lax.Precision.HIGHEST


def with_halo(x, sides, width):
    for axis, dim in sides:
        count, length = (lax.axis_size(axis), x.shape[dim])
        up = [(i, (i + 1) % count) for i in range(count - 1)]
        down = [(j, i) for i, j in up]
        last = lax.slice_in_dim(x, length - width, length, axis=dim)
        first = lax.slice_in_dim(x, 0, width, axis=dim)
        before = lax.ppermute(last, axis, up)
        after = lax.ppermute(first, axis, down)
        x = jnp.concatenate([before, x, after], axis=dim)
    return x


def coupling_fields(flow_lo, flow_hi, flow_y):
    eastward = 0.5 * (flow_lo.astype(jnp.float32) + flow_hi.astype(jnp.float32))
    across = flow_y.astype(jnp.float32)
    earlier = jnp.pad(across, ((0, 0), (1, 0)))[:, :-1]
    northward = 0.5 * (across + earlier)
    current_speed = jnp.sqrt(eastward * eastward + northward * northward)
    forcing = jnp.stack(
        [
            FORCE_SCALE * eastward,
            FORCE_SCALE * northward,
            DRAG * current_speed * eastward,
            DRAG * current_speed * northward,
        ]
    )
    return (forcing, eastward * eastward + northward * northward)


def band_rates(wave_forcing, band_dir, band_pace, growth, facing):
    cosines = jnp.cos(band_dir)[:, None]
    sine_terms = jnp.sin(band_dir)[:, None]
    drift_term = cosines * wave_forcing[0][None, :] + sine_terms * wave_forcing[1][None, :]
    push_term = jnp.maximum(
        cosines * wave_forcing[2][None, :] + sine_terms * wave_forcing[3][None, :], 0.0
    )
    base_rate = 0.5 * band_pace[:, None] * (1.0 + 0.5 * jnp.tanh(drift_term))
    inflow = base_rate[None] * jnp.maximum(
        -jnp.cos(band_dir[None, :, None] - facing[:, None, :]), 0.0
    )
    return (growth[:, None] * push_term, inflow)


def ocean_step(
    sediment,
    above_rows,
    below_rows,
    flow_lo,
    flow_hi,
    flow_y,
    open_lo,
    open_hi,
    open_y,
    settle_rate,
    erosion_gain,
):
    right_cells = jnp.pad(sediment, ((0, 0), (0, 0), (0, 1)))[:, :, 1:]
    flux_lo = (
        jnp.maximum(flow_lo, 0.0) * above_rows
        + jnp.minimum(flow_lo, 0.0) * sediment
        - KAPPA * open_lo * (sediment - above_rows)
    )
    flux_hi = (
        jnp.maximum(flow_hi, 0.0) * sediment
        + jnp.minimum(flow_hi, 0.0) * below_rows
        - KAPPA * open_hi * (below_rows - sediment)
    )
    flux_y = (
        jnp.maximum(flow_y, 0.0) * sediment
        + jnp.minimum(flow_y, 0.0) * right_cells
        - KAPPA * open_y * (right_cells - sediment)
    )
    flux_left = jnp.pad(flux_y, ((0, 0), (0, 0), (1, 0)))[:, :, :-1]
    return (
        sediment
        - (flux_hi - flux_lo)
        - (flux_y - flux_left)
        - settle_rate[:, None, None] * sediment
        + erosion_gain
    )


def entry_rank(owners, peer_count):
    onehot = (owners[:, None] == jnp.arange(peer_count, dtype=jnp.int32)[None, :]).astype(jnp.int32)
    earlier = jnp.cumsum(onehot, axis=0) - onehot
    return jnp.sum(earlier * onehot, axis=1)


def per_device(
    ocean_conc,
    flow_lo,
    flow_hi,
    flow_y,
    open_lo,
    open_hi,
    open_y,
    settle_rate,
    critical_stress,
    erosion_rate,
    wave_energy,
    band_angle,
    band_speed,
    band_growth,
    band_orbital,
    neighbors,
    facing_angle,
    live_nodes,
    remap_owner,
    remap_slot,
    remap_cell,
    remap_weight,
):
    peer_count = lax.axis_size(("sec", "tile"))
    entry_count = remap_cell.shape[0]
    capacity = min(entry_count, max(2, 2 * entry_count // peer_count))
    slot_count = peer_count * capacity
    row_count, column_count = flow_lo.shape
    ocean_count = row_count * column_count // 64
    node_count = wave_energy.shape[1]
    block_count = node_count // 64
    forcing, current_square = coupling_fields(flow_lo, flow_hi, flow_y)
    weights = remap_weight.astype(jnp.float32)
    picked = jnp.transpose(forcing.reshape(4, ocean_count, 64)[:, remap_cell, :], (1, 0, 2))
    pieces = jnp.einsum("eji,eci->ecj", weights, picked, precision=HIGHEST).reshape(
        entry_count, 256
    )
    owners = remap_owner[:, 0]
    ranking = entry_rank(owners, peer_count)
    position = owners * capacity + ranking
    send_rows = jnp.zeros((slot_count, 256), jnp.float32).at[position].set(pieces)
    send_ids = jnp.full((slot_count,), -1, jnp.int32).at[position].set(remap_slot)
    got_rows, got_ids = (
        lax.all_to_all(send_rows, ("sec", "tile"), split_axis=0, concat_axis=0, tiled=True),
        lax.all_to_all(send_ids, ("sec", "tile"), split_axis=0, concat_axis=0, tiled=True),
    )
    block_index = jnp.arange(block_count, dtype=jnp.int32)
    select = (got_ids[None, :] == block_index[:, None]).astype(jnp.float32)
    wave_blocks = jnp.dot(select, got_rows, precision=HIGHEST)
    wave_forcing = jnp.transpose(wave_blocks.reshape(block_count, 4, 64), (1, 0, 2)).reshape(
        4, node_count
    )
    alive_mask = live_nodes.astype(jnp.float32)[None, :]
    source_term, inflow = band_rates(
        wave_forcing, band_angle, band_speed, band_growth, facing_angle
    )
    energy = (wave_energy.astype(jnp.float32) + source_term) * alive_mask
    first_node = lax.axis_index(("sec", "tile")) * node_count
    total_rate = jnp.sum(inflow, axis=0)
    local_index = neighbors - first_node + 128
    for sweep in range(WSTEPS):
        padded = with_halo(energy, ((("sec", "tile"), 1),), 128)
        arriving = jnp.zeros_like(energy)
        for neighbor in range(NBRS):
            arriving = arriving + inflow[neighbor] * jnp.take(padded, local_index[neighbor], axis=1)
        energy = (energy + arriving - total_rate * energy) * alive_mask
    waves_out = energy.astype(jnp.bfloat16)
    coefficient = jnp.stack(
        [band_orbital * jnp.cos(band_angle), band_orbital * jnp.sin(band_angle)]
    )
    orbital = lax.psum(jnp.dot(coefficient, energy, precision=HIGHEST), "lev")
    orbital_blocks = jnp.transpose(orbital.reshape(2, block_count, 64), (1, 0, 2)).reshape(
        block_count, 128
    )
    back_rows = jnp.einsum("ws,wc->sc", select, orbital_blocks, precision=HIGHEST)
    returned = lax.all_to_all(back_rows, ("sec", "tile"), split_axis=0, concat_axis=0, tiled=True)
    mine = returned[position].reshape(entry_count, 2, 64)
    spread = jnp.einsum("eji,ecj->eci", weights, mine, precision=HIGHEST).reshape(entry_count, 128)
    ocean_select = (
        remap_cell[None, :] == jnp.arange(ocean_count, dtype=jnp.int32)[:, None]
    ).astype(jnp.float32)
    ocean_blocks = jnp.dot(ocean_select, spread, precision=HIGHEST)
    ocean_orbital = jnp.transpose(ocean_blocks.reshape(ocean_count, 2, 64), (1, 0, 2)).reshape(
        2, row_count, column_count
    )
    stress = TAU_CURRENT * current_square + TAU_WAVES * (
        ocean_orbital[0] * ocean_orbital[0] + ocean_orbital[1] * ocean_orbital[1]
    )
    erosion_gain = erosion_rate[:, None, None] * jnp.maximum(
        stress[None] / critical_stress[:, None, None] - 1.0, 0.0
    )
    lower_flow = flow_lo.astype(jnp.float32)
    upper_flow = flow_hi.astype(jnp.float32)
    side_flow = flow_y.astype(jnp.float32)
    lower_open = open_lo.astype(jnp.float32)
    upper_open = open_hi.astype(jnp.float32)
    side_open = open_y.astype(jnp.float32)
    sediment = ocean_conc
    for sweep in range(OSTEPS):
        rimmed = with_halo(sediment, ((("sec", "tile"), 1),), 1)
        sediment = ocean_step(
            sediment,
            rimmed[:, :-2],
            rimmed[:, 2:],
            lower_flow,
            upper_flow,
            side_flow,
            lower_open,
            upper_open,
            side_open,
            settle_rate,
            erosion_gain,
        )
    return (sediment, waves_out)


def solution(mesh):
    return jax.shard_map(
        per_device,
        mesh=mesh,
        in_specs=(
            P("lev", ("sec", "tile"), None),
            P(("sec", "tile"), None),
            P(("sec", "tile"), None),
            P(("sec", "tile"), None),
            P(("sec", "tile"), None),
            P(("sec", "tile"), None),
            P(("sec", "tile"), None),
            P("lev"),
            P("lev"),
            P("lev"),
            P("lev", ("sec", "tile")),
            P("lev"),
            P("lev"),
            P("lev"),
            P("lev"),
            P(None, ("sec", "tile")),
            P(None, ("sec", "tile")),
            P(("sec", "tile")),
            P(("sec", "tile"), None),
            P(("sec", "tile")),
            P(("sec", "tile")),
            P(("sec", "tile"), None, None),
        ),
        out_specs=(P("lev", ("sec", "tile"), None), P("lev", ("sec", "tile"))),
        check_vma=False,
    )
```

profile of v0, /device:TPU:2, one launch (start us, length us, event | category | flops | bytes accessed | tf_op | source)
XLA Modules:
  0.0 237.9 jit_solution(6363160017890517381)
XLA Ops:
  4.7 19.5 %all-to-all-start = ((s32[128,2,1]{1,2,0:T(1,128)}), s32[128,2,1]{1,2,0:T(1,128)S(1)}, u32[]{:S(2)}, u32[]{:S(2)}) async-start(s32[128,2,1]{1,2,0:T(1,128)} %bitcast.4), calls=%async_computation | async-start | bytes 131072 | tf_op jit(solution)/shard_map/all_to_all | solution.py:153
  33.9 4.8 %all-to-all-done = s32[128,2,1]{1,2,0:T(1,128)S(1)} async-done(((s32[128,2,1]{1,2,0:T(1,128)}), s32[128,2,1]{1,2,0:T(1,128)S(1)}, u32[]{:S(2)}, u32[]{:S(2)}) %all-to-all-start) | async-done | bytes 1056 | tf_op jit(solution)/shard_map/all_to_all | solution.py:153
  38.7 11.4 %all-to-all-start.1 = ((f32[128,2,256]{2,1,0:T(2,128)}), f32[128,2,256]{2,1,0:T(2,128)S(1)}, u32[]{:S(2)}, u32[]{:S(2)}) async-start(f32[128,2,256]{2,1,0:T(2,128)} %all_to_all.25), calls=%async_computation.1 | async-start | bytes 524288 | tf_op jit(solution)/shard_map/all_to_all | solution.py:152
  52.1 20.8 %all-to-all-done.1 = f32[128,2,256]{2,1,0:T(2,128)S(1)} async-done(((f32[128,2,256]{2,1,0:T(2,128)}), f32[128,2,256]{2,1,0:T(2,128)S(1)}, u32[]{:S(2)}, u32[]{:S(2)}) %all-to-all-start.1) | async-done | bytes 262176 | tf_op jit(solution)/shard_map/all_to_all | solution.py:152
  76.2 5.9 %collective-permute-start.3 = (f32[192,128]{0,1:T(8,128)S(1)}, f32[192,128]{0,1:T(8,128)S(1)}, u32[]{:S(2)}, u32[]{:S(2)}) collective-permute-start(f32[192,128]{0,1:T(8,128)S(1)} %get-tuple-element.22), channel_id=1, source_target_pairs={{4,0},{8,4},{12,8},{16,12},{20,16},{24,20},{28,24},{32,28},{36,32}... | collective-permute-start | bytes 294920 | tf_op jit(solution)/shard_map/ppermute | solution.py:27
  82.1 8.5 %maximum_multiply_fusion = (f32[4,192,512]{1,2,0:T(8,128)}, f32[192,512]{0,1:T(8,128)S(1)}) fusion(f32[4,512]{1,0:T(4,128)S(1)} %copy-done.29, f32[192]{0:T(256)S(1)} %copy-done.34, f32[192,512]{0,1:T(8,128)S(1)} %get-tuple-element.49), kind=kLoop, calls=%fused_computation.20 | loop fusion | flops 1867776 | bytes 2368256 | tf_op jit(solution)/shard_map/mul | solution.py:57
  98.9 2.4 %fusion.21 = f32[192,512]{0,1:T(8,128)S(1)} fusion(f32[512,192]{1,0:T(8,128)} %gather_fusion.5, f32[512,192]{1,0:T(8,128)} %gather_fusion.4, f32[512,192]{1,0:T(8,128)} %gather_fusion.3, f32[512,192]{1,0:T(8,128)S(1)} %gather_fusion.2, f32[192,512]{0,1:T(8,128)S(1)} %get-tuple-element.14, f32[4,192,512]{1,2,0:T(8,128)} %get-tuple-element.13, ...), kind=kLoop, calls=%fused_computation.66 | loop fusion | flops 2260992 | bytes 4139264 | tf_op jit(solution)/shard_map/mul | solution.py:174
  103.3 5.8 %collective-permute-start.5 = (f32[192,128]{0,1:T(8,128)S(1)}, f32[192,128]{0,1:T(8,128)S(1)}, u32[]{:S(2)}, u32[]{:S(2)}) collective-permute-start(f32[192,128]{0,1:T(8,128)S(1)} %get-tuple-element.20), channel_id=1, source_target_pairs={{4,0},{8,4},{12,8},{16,12},{20,16},{24,20},{28,24},{32,28},{36,32}... | collective-permute-start | bytes 294920 | tf_op jit(solution)/shard_map/ppermute | solution.py:27
  112.4 2.4 %collective-permute-start.1 = (f32[2,1,512]{2,1,0:T(1,128)}, f32[2,1,512]{2,1,0:T(1,128)}, u32[]{:S(2)}, u32[]{:S(2)}) collective-permute-start(f32[2,1,512]{2,1,0:T(1,128)} %get-tuple-element.32), channel_id=1, source_target_pairs={{0,4},{4,8},{8,12},{12,16},{16,20},{20,24},{24,28},{28,32},{32,36}... | collective-permute-start | bytes 12296 | tf_op jit(solution)/shard_map/ppermute | solution.py:26
  123.9 2.5 %fusion.15 = f32[192,512]{0,1:T(8,128)S(1)} fusion(f32[192,512]{0,1:T(8,128)S(1)} %fusion.21, f32[512,192]{1,0:T(8,128)} %gather_fusion.9, f32[512,192]{1,0:T(8,128)} %gather_fusion.8, f32[512,192]{1,0:T(8,128)} %gather_fusion.7, f32[512,192]{1,0:T(8,128)} %gather_fusion.6, f32[192,512]{0,1:T(8,128)S(1)} %get-tuple-element.14, ...), kind=kLoop, calls=%fused_computation.56 | loop fusion | flops 1474560 | bytes 4329472 | tf_op jit(solution)/shard_map/mul | solution.py:174
  128.3 5.8 %collective-permute-start.7 = (f32[192,128]{0,1:T(8,128)S(1)}, f32[192,128]{0,1:T(8,128)S(1)}, u32[]{:S(2)}, u32[]{:S(2)}) collective-permute-start(f32[192,128]{0,1:T(8,128)S(1)} %get-tuple-element.18), channel_id=1, source_target_pairs={{4,0},{8,4},{12,8},{16,12},{20,16},{24,20},{28,24},{32,28},{36,32}... | collective-permute-start | bytes 294920 | tf_op jit(solution)/shard_map/ppermute | solution.py:27
  142.7 2.4 gather_fusion.13
  145.1 2.4 %fusion.9 = f32[192,512]{0,1:T(8,128)S(1)} fusion(f32[192,512]{0,1:T(8,128)S(1)} %fusion.15, f32[512,192]{1,0:T(8,128)} %gather_fusion.13, f32[512,192]{1,0:T(8,128)} %gather_fusion.12, f32[512,192]{1,0:T(8,128)} %gather_fusion.11, f32[512,192]{1,0:T(8,128)S(1)} %gather_fusion.10, f32[192,512]{0,1:T(8,128)S(1)} %get-tuple-element.14, ...), kind=kLoop, calls=%fused_computation.46 | loop fusion | flops 1474560 | bytes 4329472 | tf_op jit(solution)/shard_map/mul | solution.py:174
  149.5 6.1 %collective-permute-start.9 = (f32[192,128]{0,1:T(8,128)S(1)}, f32[192,128]{0,1:T(8,128)S(1)}, u32[]{:S(2)}, u32[]{:S(2)}) collective-permute-start(f32[192,128]{0,1:T(8,128)S(1)} %get-tuple-element.16), channel_id=1, source_target_pairs={{4,0},{8,4},{12,8},{16,12},{20,16},{24,20},{28,24},{32,28},{36,32}... | collective-permute-start | bytes 294920 | tf_op jit(solution)/shard_map/ppermute | solution.py:27
  166.3 2.5 %fusion.119 = (bf16[192,512]{0,1:T(8,128)(2,1)S(1)}, f32[192,512]{0,1:T(8,128)S(1)}) fusion(f32[512]{0:T(512)S(1)} %convert_element_type.56, f32[192,512]{0,1:T(8,128)S(1)} %get-tuple-element.14, f32[192,512]{0,1:T(8,128)S(1)} %fusion.9, f32[512,192]{1,0:T(8,128)} %gather_fusion.17, pred[512]{0:T(512)(128)(4,1)S(1)} %copy-done.24, ...), kind=kLoop, calls=%fused_computation.229 | loop fusion | flops 1572864 | bytes 4526080 | tf_op jit(solution)/shard_map/convert_element_type | solution.py:175
  169.5 10.7 %psum.7 = f32[8,128]{1,0:T(8,128)S(1)} all-reduce(f32[8,128]{1,0:T(8,128)S(1)} %reshape.175), channel_id=1, replica_groups=mesh['sec'=4,'tile'=32,'lev'=4] {'lev'}, use_global_device_ids=true, to_apply=%region_5.7 | all-reduce | flops 1024 | bytes 8192 | tf_op jit(solution)/shard_map/psum | solution.py:179
  181.4 6.7 %all-to-all-start.2 = ((f32[128,2,128]{2,1,0:T(2,128)}), f32[128,2,128]{2,1,0:T(2,128)S(1)}, u32[]{:S(2)}, u32[]{:S(2)}) async-start(f32[128,2,128]{2,1,0:T(2,128)} %copy.49), calls=%async_computation.2 | async-start | bytes 262144 | tf_op jit(solution)/shard_map/all_to_all | solution.py:184
  189.1 16.2 %all-to-all-done.2 = f32[128,2,128]{2,1,0:T(2,128)S(1)} async-done(((f32[128,2,128]{2,1,0:T(2,128)}), f32[128,2,128]{2,1,0:T(2,128)S(1)}, u32[]{:S(2)}, u32[]{:S(2)}) %all-to-all-start.2) | async-done | bytes 131104 | tf_op jit(solution)/shard_map/all_to_all | solution.py:184
  208.6 3.2 %collective-permute-start.10 = (f32[2,1,512]{2,1,0:T(1,128)S(1)}, f32[2,1,512]{2,1,0:T(1,128)S(1)}, u32[]{:S(2)}, u32[]{:S(2)}) collective-permute-start(f32[2,1,512]{2,1,0:T(1,128)S(1)} %get-tuple-element.27), channel_id=1, source_target_pairs={{4,0},{8,4},{12,8},{16,12},{20,16},{24,20},{28,24},{32,28},{36,32}... | collective-permute-start | bytes 12296 | tf_op jit(solution)/shard_map/ppermute | solution.py:27
  213.8 5.0 %collective-permute-done.11 = f32[2,1,512]{2,1,0:T(1,128)S(1)} collective-permute-done((f32[2,1,512]{2,1,0:T(1,128)S(1)}, f32[2,1,512]{2,1,0:T(1,128)S(1)}, u32[]{:S(2)}, u32[]{:S(2)}) %collective-permute-start.11) | collective-permute-done | bytes 4128 | tf_op jit(solution)/shard_map/ppermute | solution.py:26
  220.9 2.4 %collective-permute-start.13 = (f32[2,1,512]{2,1,0:T(1,128)S(1)}, f32[2,1,512]{2,1,0:T(1,128)S(1)}, u32[]{:S(2)}, u32[]{:S(2)}) collective-permute-start(f32[2,1,512]{2,1,0:T(1,128)S(1)} %get-tuple-element.26), channel_id=1, source_target_pairs={{0,4},{4,8},{8,12},{12,16},{16,20},{20,24},{24,28},{28,32},{32,36}... | collective-permute-start | bytes 12296 | tf_op jit(solution)/shard_map/ppermute | solution.py:26
  223.5 4.5 %collective-permute-done.13 = f32[2,1,512]{2,1,0:T(1,128)S(1)} collective-permute-done((f32[2,1,512]{2,1,0:T(1,128)S(1)}, f32[2,1,512]{2,1,0:T(1,128)S(1)}, u32[]{:S(2)}, u32[]{:S(2)}) %collective-permute-start.13) | collective-permute-done | bytes 4128 | tf_op jit(solution)/shard_map/ppermute | solution.py:26
  230.0 2.4 %collective-permute-start.15 = (f32[2,1,512]{2,1,0:T(1,128)S(1)}, f32[2,1,512]{2,1,0:T(1,128)S(1)}, u32[]{:S(2)}, u32[]{:S(2)}) collective-permute-start(f32[2,1,512]{2,1,0:T(1,128)S(1)} %get-tuple-element.24), channel_id=1, source_target_pairs={{0,4},{4,8},{8,12},{12,16},{16,20},{20,24},{24,28},{28,32},{32,36}... | collective-permute-start | bytes 12296 | tf_op jit(solution)/shard_map/ppermute | solution.py:26
  232.6 4.5 %collective-permute-done.15 = f32[2,1,512]{2,1,0:T(1,128)S(1)} collective-permute-done((f32[2,1,512]{2,1,0:T(1,128)S(1)}, f32[2,1,512]{2,1,0:T(1,128)S(1)}, u32[]{:S(2)}, u32[]{:S(2)}) %collective-permute-start.15) | collective-permute-done | bytes 4128 | tf_op jit(solution)/shard_map/ppermute | solution.py:26
  (214 shorter events, 77.5 us)
Async XLA Ops:
  4.7 33.9 %all-to-all-start = ((s32[128,2,1]{1,2,0:T(1,128)}), s32[128,2,1]{1,2,0:T(1,128)S(1)}, u32[]{:S(2)}, u32[]{:S(2)}) async-start(s32[128,2,1]{1,2,0:T(1,128)} %bitcast.4), calls=%async_computation | async-start | bytes 131072 | tf_op jit(solution)/shard_map/all_to_all | solution.py:153
  38.7 34.2 %all-to-all-start.1 = ((f32[128,2,256]{2,1,0:T(2,128)}), f32[128,2,256]{2,1,0:T(2,128)S(1)}, u32[]{:S(2)}, u32[]{:S(2)}) async-start(f32[128,2,256]{2,1,0:T(2,128)} %all_to_all.25), calls=%async_computation.1 | async-start | bytes 524288 | tf_op jit(solution)/shard_map/all_to_all | solution.py:152
  50.3 71.3 %copy-start.17 = (s32[1024]{0:T(1024)}, s32[1024]{0:T(1024)S(1)}, u32[]{:S(2)}) copy-start(s32[1024]{0:T(1024)S(1)} %pad_clamp_fusion.1) | copy-start | bytes 12292
  50.4 73.5 %copy-start.23 = (pred[512]{0:T(512)(128)(4,1)}, pred[512]{0:T(512)(128)(4,1)S(1)}, u32[]{:S(2)}) copy-start(pred[512]{0:T(512)(128)(4,1)S(1)} %get-tuple-element.56) | copy-start | bytes 1540
  50.4 73.4 %copy-start.25 = (pred[512]{0:T(512)(128)(4,1)}, pred[512]{0:T(512)(128)(4,1)S(1)}, u32[]{:S(2)}) copy-start(pred[512]{0:T(512)(128)(4,1)S(1)} %get-tuple-element.57) | copy-start | bytes 1540
  50.4 73.4 %copy-start.27 = (pred[512]{0:T(512)(128)(4,1)}, pred[512]{0:T(512)(128)(4,1)S(1)}, u32[]{:S(2)}) copy-start(pred[512]{0:T(512)(128)(4,1)S(1)} %get-tuple-element.58) | copy-start | bytes 1540
  50.4 73.4 %copy-start.28 = (pred[512]{0:T(512)(128)(4,1)}, pred[512]{0:T(512)(128)(4,1)S(1)}, u32[]{:S(2)}) copy-start(pred[512]{0:T(512)(128)(4,1)S(1)} %get-tuple-element.59) | copy-start | bytes 1540
  74.2 16.4 %collective-permute-start.2 = (f32[192,128]{0,1:T(8,128)S(1)}, f32[192,128]{0,1:T(8,128)S(1)}, u32[]{:S(2)}, u32[]{:S(2)}) collective-permute-start(f32[192,128]{0,1:T(8,128)S(1)} %get-tuple-element.21), channel_id=1, source_target_pairs={{0,4},{4,8},{8,12},{12,16},{16,20},{20,24},{24,28},{28,32},{32,36}... | collective-permute-start | bytes 294920 | tf_op jit(solution)/shard_map/ppermute | solution.py:26
  76.2 14.4 %collective-permute-start.3 = (f32[192,128]{0,1:T(8,128)S(1)}, f32[192,128]{0,1:T(8,128)S(1)}, u32[]{:S(2)}, u32[]{:S(2)}) collective-permute-start(f32[192,128]{0,1:T(8,128)S(1)} %get-tuple-element.22), channel_id=1, source_target_pairs={{4,0},{8,4},{12,8},{16,12},{20,16},{24,20},{28,24},{32,28},{36,32}... | collective-permute-start | bytes 294920 | tf_op jit(solution)/shard_map/ppermute | solution.py:27
  101.4 13.4 %collective-permute-start.4 = (f32[192,128]{0,1:T(8,128)S(1)}, f32[192,128]{0,1:T(8,128)S(1)}, u32[]{:S(2)}, u32[]{:S(2)}) collective-permute-start(f32[192,128]{0,1:T(8,128)S(1)} %get-tuple-element.19), channel_id=1, source_target_pairs={{0,4},{4,8},{8,12},{12,16},{16,20},{20,24},{24,28},{28,32},{32,36}... | collective-permute-start | bytes 294920 | tf_op jit(solution)/shard_map/ppermute | solution.py:26
  103.3 11.5 %collective-permute-start.5 = (f32[192,128]{0,1:T(8,128)S(1)}, f32[192,128]{0,1:T(8,128)S(1)}, u32[]{:S(2)}, u32[]{:S(2)}) collective-permute-start(f32[192,128]{0,1:T(8,128)S(1)} %get-tuple-element.20), channel_id=1, source_target_pairs={{4,0},{8,4},{12,8},{16,12},{20,16},{24,20},{28,24},{32,28},{36,32}... | collective-permute-start | bytes 294920 | tf_op jit(solution)/shard_map/ppermute | solution.py:27
  110.4 97.2 %collective-permute-start = (f32[2,1,512]{2,1,0:T(1,128)}, f32[2,1,512]{2,1,0:T(1,128)}, u32[]{:S(2)}, u32[]{:S(2)}) collective-permute-start(f32[2,1,512]{2,1,0:T(1,128)} %get-tuple-element.31), channel_id=1, source_target_pairs={{4,0},{8,4},{12,8},{16,12},{20,16},{24,20},{28,24},{32,28},{36,32}... | collective-permute-start | bytes 12296 | tf_op jit(solution)/shard_map/ppermute | solution.py:27
  112.4 95.3 %collective-permute-start.1 = (f32[2,1,512]{2,1,0:T(1,128)}, f32[2,1,512]{2,1,0:T(1,128)}, u32[]{:S(2)}, u32[]{:S(2)}) collective-permute-start(f32[2,1,512]{2,1,0:T(1,128)} %get-tuple-element.32), channel_id=1, source_target_pairs={{0,4},{4,8},{8,12},{12,16},{16,20},{20,24},{24,28},{28,32},{32,36}... | collective-permute-start | bytes 12296 | tf_op jit(solution)/shard_map/ppermute | solution.py:26
  126.4 8.4 %collective-permute-start.6 = (f32[192,128]{0,1:T(8,128)S(1)}, f32[192,128]{0,1:T(8,128)S(1)}, u32[]{:S(2)}, u32[]{:S(2)}) collective-permute-start(f32[192,128]{0,1:T(8,128)S(1)} %get-tuple-element.17), channel_id=1, source_target_pairs={{0,4},{4,8},{8,12},{12,16},{16,20},{20,24},{24,28},{28,32},{32,36}... | collective-permute-start | bytes 294920 | tf_op jit(solution)/shard_map/ppermute | solution.py:26
  128.3 8.3 %collective-permute-start.7 = (f32[192,128]{0,1:T(8,128)S(1)}, f32[192,128]{0,1:T(8,128)S(1)}, u32[]{:S(2)}, u32[]{:S(2)}) collective-permute-start(f32[192,128]{0,1:T(8,128)S(1)} %get-tuple-element.18), channel_id=1, source_target_pairs={{4,0},{8,4},{12,8},{16,12},{20,16},{24,20},{28,24},{32,28},{36,32}... | collective-permute-start | bytes 294920 | tf_op jit(solution)/shard_map/ppermute | solution.py:27
  147.6 9.3 %collective-permute-start.8 = (f32[192,128]{0,1:T(8,128)S(1)}, f32[192,128]{0,1:T(8,128)S(1)}, u32[]{:S(2)}, u32[]{:S(2)}) collective-permute-start(f32[192,128]{0,1:T(8,128)S(1)} %get-tuple-element.15), channel_id=1, source_target_pairs={{0,4},{4,8},{8,12},{12,16},{16,20},{20,24},{24,28},{28,32},{32,36}... | collective-permute-start | bytes 294920 | tf_op jit(solution)/shard_map/ppermute | solution.py:26
  149.5 8.4 %collective-permute-start.9 = (f32[192,128]{0,1:T(8,128)S(1)}, f32[192,128]{0,1:T(8,128)S(1)}, u32[]{:S(2)}, u32[]{:S(2)}) collective-permute-start(f32[192,128]{0,1:T(8,128)S(1)} %get-tuple-element.16), channel_id=1, source_target_pairs={{4,0},{8,4},{12,8},{16,12},{20,16},{24,20},{28,24},{32,28},{36,32}... | collective-permute-start | bytes 294920 | tf_op jit(solution)/shard_map/ppermute | solution.py:27
  181.4 23.9 %all-to-all-start.2 = ((f32[128,2,128]{2,1,0:T(2,128)}), f32[128,2,128]{2,1,0:T(2,128)S(1)}, u32[]{:S(2)}, u32[]{:S(2)}) async-start(f32[128,2,128]{2,1,0:T(2,128)} %copy.49), calls=%async_computation.2 | async-start | bytes 262144 | tf_op jit(solution)/shard_map/all_to_all | solution.py:184
  208.6 5.2 %collective-permute-start.10 = (f32[2,1,512]{2,1,0:T(1,128)S(1)}, f32[2,1,512]{2,1,0:T(1,128)S(1)}, u32[]{:S(2)}, u32[]{:S(2)}) collective-permute-start(f32[2,1,512]{2,1,0:T(1,128)S(1)} %get-tuple-element.27), channel_id=1, source_target_pairs={{4,0},{8,4},{12,8},{16,12},{20,16},{24,20},{28,24},{32,28},{36,32}... | collective-permute-start | bytes 12296 | tf_op jit(solution)/shard_map/ppermute | solution.py:27
  211.8 7.0 %collective-permute-start.11 = (f32[2,1,512]{2,1,0:T(1,128)S(1)}, f32[2,1,512]{2,1,0:T(1,128)S(1)}, u32[]{:S(2)}, u32[]{:S(2)}) collective-permute-start(f32[2,1,512]{2,1,0:T(1,128)S(1)} %get-tuple-element.28), channel_id=1, source_target_pairs={{0,4},{4,8},{8,12},{12,16},{16,20},{20,24},{24,28},{28,32},{32,36}... | collective-permute-start | bytes 12296 | tf_op jit(solution)/shard_map/ppermute | solution.py:26
  219.0 4.5 %collective-permute-start.12 = (f32[2,1,512]{2,1,0:T(1,128)S(1)}, f32[2,1,512]{2,1,0:T(1,128)S(1)}, u32[]{:S(2)}, u32[]{:S(2)}) collective-permute-start(f32[2,1,512]{2,1,0:T(1,128)S(1)} %get-tuple-element.25), channel_id=1, source_target_pairs={{4,0},{8,4},{12,8},{16,12},{20,16},{24,20},{28,24},{32,28},{36,32}... | collective-permute-start | bytes 12296 | tf_op jit(solution)/shard_map/ppermute | solution.py:27
  220.9 7.0 %collective-permute-start.13 = (f32[2,1,512]{2,1,0:T(1,128)S(1)}, f32[2,1,512]{2,1,0:T(1,128)S(1)}, u32[]{:S(2)}, u32[]{:S(2)}) collective-permute-start(f32[2,1,512]{2,1,0:T(1,128)S(1)} %get-tuple-element.26), channel_id=1, source_target_pairs={{0,4},{4,8},{8,12},{12,16},{16,20},{20,24},{24,28},{28,32},{32,36}... | collective-permute-start | bytes 12296 | tf_op jit(solution)/shard_map/ppermute | solution.py:26
  228.1 4.5 %collective-permute-start.14 = (f32[2,1,512]{2,1,0:T(1,128)S(1)}, f32[2,1,512]{2,1,0:T(1,128)S(1)}, u32[]{:S(2)}, u32[]{:S(2)}) collective-permute-start(f32[2,1,512]{2,1,0:T(1,128)S(1)} %get-tuple-element.23), channel_id=1, source_target_pairs={{4,0},{8,4},{12,8},{16,12},{20,16},{24,20},{28,24},{32,28},{36,32}... | collective-permute-start | bytes 12296 | tf_op jit(solution)/shard_map/ppermute | solution.py:27
  230.0 7.0 %collective-permute-start.15 = (f32[2,1,512]{2,1,0:T(1,128)S(1)}, f32[2,1,512]{2,1,0:T(1,128)S(1)}, u32[]{:S(2)}, u32[]{:S(2)}) collective-permute-start(f32[2,1,512]{2,1,0:T(1,128)S(1)} %get-tuple-element.24), channel_id=1, source_target_pairs={{0,4},{4,8},{8,12},{12,16},{16,20},{20,24},{24,28},{28,32},{32,36}... | collective-permute-start | bytes 12296 | tf_op jit(solution)/shard_map/ppermute | solution.py:26
  (39 other events, 830.7 us)
where the time goes:
time: 239 us; the launch traced here: 238 us
  starting transfers between devices  86.9 us (36%)
  waiting for transfers between devices  58.6 us (25%)
  local copies, waits for them, and re-layouts  45.7 us (19%)
  other arithmetic  30.2 us (13%)
  blocking collectives  10.7 us (4%)
  matrix products  3.97 us (2%)
    gather x16, local copies, waits for them, and re-layouts, per_device(): jnp.take(padded, local_index[neighbor], axis=1)  34 us
    ppermute x8, starting transfers between devices, with_halo(): after = lax.ppermute(first, axis, down)  32.5 us
    all_to_all x1, waiting for transfers between devices, per_device(): lax.all_to_all(send_rows, ('sec', 'tile'), split_axis=0, concat_axis=0, t...  20.8 us
    all_to_all x1, starting transfers between devices, per_device(): lax.all_to_all(send_ids, ('sec', 'tile'), split_axis=0, concat_axis=0, ti...  19.5 us
    ppermute x8, starting transfers between devices, with_halo(): before = lax.ppermute(last, axis, up)  16.8 us
    all_to_all x1, waiting for transfers between devices, per_device(): lax.all_to_all(back_rows, ('sec', 'tile'), split_axis=0, concat_axis=0, t...  16.2 us
    ppermute x8, waiting for transfers between devices, with_halo(): before = lax.ppermute(last, axis, up)  14 us
    all_to_all x1, starting transfers between devices, per_device(): lax.all_to_all(send_rows, ('sec', 'tile'), split_axis=0, concat_axis=0, t...  11.4 us
  transfers between devices with their start and end apart: 19, of which 8 were waited for; matrix products, arithmetic and copies ran while one was open for 25% of the time, Pallas kernels for 0%

commit v1 on v0

--- a/solution.py
+++ b/solution.py
@@ -146,12 +146,11 @@
     owners = remap_owner[:, 0]
     ranking = entry_rank(owners, peer_count)
     position = owners * capacity + ranking
-    send_rows = jnp.zeros((slot_count, 256), jnp.float32).at[position].set(pieces)
-    send_ids = jnp.full((slot_count,), -1, jnp.int32).at[position].set(remap_slot)
-    got_rows, got_ids = (
-        lax.all_to_all(send_rows, ("sec", "tile"), split_axis=0, concat_axis=0, tiled=True),
-        lax.all_to_all(send_ids, ("sec", "tile"), split_axis=0, concat_axis=0, tiled=True),
-    )
+    tagged = jnp.concatenate([pieces, remap_slot.astype(jnp.float32)[:, None]], axis=1)
+    send_rows = jnp.full((slot_count, 257), -1.0, jnp.float32).at[position].set(tagged)
+    got = lax.all_to_all(send_rows, ("sec", "tile"), split_axis=0, concat_axis=0, tiled=True)
+    got_rows = got[:, :256]
+    got_ids = got[:, 256].astype(jnp.int32)
     block_index = jnp.arange(block_count, dtype=jnp.int32)
     select = (got_ids[None, :] == block_index[:, None]).astype(jnp.float32)
     wave_blocks = jnp.dot(select, got_rows, precision=HIGHEST)
@@ -197,19 +196,36 @@
     erosion_gain = erosion_rate[:, None, None] * jnp.maximum(
         stress[None] / critical_stress[:, None, None] - 1.0, 0.0
     )
-    lower_flow = flow_lo.astype(jnp.float32)
-    upper_flow = flow_hi.astype(jnp.float32)
-    side_flow = flow_y.astype(jnp.float32)
-    lower_open = open_lo.astype(jnp.float32)
-    upper_open = open_hi.astype(jnp.float32)
-    side_open = open_y.astype(jnp.float32)
-    sediment = ocean_conc
+    classes = ocean_conc.shape[0]
+    fields = jnp.concatenate(
+        [
+            ocean_conc,
+            erosion_gain,
+            jnp.stack(
+                [
+                    flow_lo.astype(jnp.float32),
+                    flow_hi.astype(jnp.float32),
+                    flow_y.astype(jnp.float32),
+                    open_lo.astype(jnp.float32),
+                    open_hi.astype(jnp.float32),
+                    open_y.astype(jnp.float32),
+                ]
+            ),
+        ]
+    )
+    wide = with_halo(fields, ((("sec", "tile"), 1),), OSTEPS)
+    sediment = wide[:classes]
+    gain = wide[classes : 2 * classes]
+    lower_flow, upper_flow, side_flow, lower_open, upper_open, side_open = (
+        wide[2 * classes + k] for k in range(6)
+    )
     for sweep in range(OSTEPS):
-        rimmed = with_halo(sediment, ((("sec", "tile"), 1),), 1)
+        above_rows = jnp.pad(sediment, ((0, 0), (1, 0), (0, 0)))[:, :-1]
+        below_rows = jnp.pad(sediment, ((0, 0), (0, 1), (0, 0)))[:, 1:]
         sediment = ocean_step(
             sediment,
-            rimmed[:, :-2],
-            rimmed[:, 2:],
+            above_rows,
+            below_rows,
             lower_flow,
             upper_flow,
             side_flow,
@@ -217,8 +233,9 @@
             upper_open,
             side_open,
             settle_rate,
-            erosion_gain,
+            gain,
         )
+    sediment = sediment[:, OSTEPS : OSTEPS + row_count]
     return (sediment, waves_out)
 
 

time: 239 us -> 203 us (0.85)
  the two profiles are of different devices: /device:TPU:2 before, /device:TPU:1 now
where the time goes in v1:
time: 203 us
  starting transfers between devices  61.7 us (30%)
  waiting for transfers between devices  59.4 us (29%)
  local copies, waits for them, and re-layouts  41.6 us (20%)
  other arithmetic  25.7 us (13%)
  blocking collectives  8.71 us (4%)
  matrix products  3.91 us (2%)
    gather x16, local copies, waits for them, and re-layouts, per_device(): jnp.take(padded, local_index[neighbor], axis=1)  35.1 us
    all_to_all x1, waiting for transfers between devices, per_device(): lax.all_to_all(send_rows, ('sec', 'tile'), split_axis=0, concat_axis=0, t...  27.5 us
    all_to_all x1, starting transfers between devices, per_device(): lax.all_to_all(send_rows, ('sec', 'tile'), split_axis=0, concat_axis=0, t...  20.5 us
    all_to_all x1, waiting for transfers between devices, per_device(): lax.all_to_all(back_rows, ('sec', 'tile'), split_axis=0, concat_axis=0, t...  17.3 us
    ppermute x5, starting transfers between devices, with_halo(): before = lax.ppermute(last, axis, up)  15.8 us
    ppermute x5, waiting for transfers between devices, with_halo(): after = lax.ppermute(first, axis, down)  14.7 us
    all_to_all x1, starting transfers between devices, per_device(): lax.all_to_all(back_rows, ('sec', 'tile'), split_axis=0, concat_axis=0, t...  14.6 us
    ppermute x5, starting transfers between devices, with_halo(): after = lax.ppermute(first, axis, down)  10.8 us
  transfers between devices with their start and end apart: 12, of which 6 were waited for; matrix products, arithmetic and copies ran while one was open for 5% of the time, Pallas kernels for 0%

profile of v1, /device:TPU:1, one launch (start us, length us, event | category | flops | bytes accessed | tf_op | source)
XLA Modules:
  0.0 202.6 jit_solution(10572180905489185437)
XLA Ops:
  9.0 20.5 %all-to-all-start = ((f32[128,2,257]{2,1,0:T(2,128)}), f32[128,2,257]{2,1,0:T(2,128)S(1)}, u32[]{:S(2)}, u32[]{:S(2)}) async-start(f32[128,2,257]{2,1,0:T(2,128)} %all_to_all.14), calls=%async_computation | async-start | bytes 786432 | tf_op jit(solution)/shard_map/all_to_all | solution.py:151
  29.9 27.5 %all-to-all-done = f32[128,2,257]{2,1,0:T(2,128)S(1)} async-done(((f32[128,2,257]{2,1,0:T(2,128)}), f32[128,2,257]{2,1,0:T(2,128)S(1)}, u32[]{:S(2)}, u32[]{:S(2)}) %all-to-all-start) | async-done | bytes 263200 | tf_op jit(solution)/shard_map/all_to_all | solution.py:151
  58.9 4.4 %collective-permute-start = (f32[192,128]{0,1:T(8,128)S(1)}, f32[192,128]{0,1:T(8,128)S(1)}, u32[]{:S(2)}, u32[]{:S(2)}) collective-permute-start(f32[192,128]{0,1:T(8,128)S(1)} %get-tuple-element.42), channel_id=1, source_target_pairs={{0,4},{4,8},{8,12},{12,16},{16,20},{20,24},{24,28},{28,32},{32,36}... | collective-permute-start | bytes 294920 | tf_op jit(solution)/shard_map/ppermute | solution.py:26
  65.2 8.5 %maximum_multiply_fusion = (f32[4,192,512]{1,2,0:T(8,128)}, f32[192,512]{0,1:T(8,128)S(1)}) fusion(f32[4,512]{1,0:T(4,128)S(1)} %copy-done.9, f32[192]{0:T(256)S(1)} %copy-done.12, f32[192,512]{0,1:T(8,128)S(1)} %get-tuple-element.57), kind=kLoop, calls=%fused_computation.19 | loop fusion | flops 1867776 | bytes 2368256 | tf_op jit(solution)/shard_map/mul | solution.py:57
  76.0 2.2 %gather_fusion.3 = f32[512,192]{1,0:T(8,128)} fusion(f32[192,768]{0,1:T(8,128)S(1)} %pad_maximum_fusion.1, s32[1024]{0:T(1024)S(1)} %get-tuple-element.64), kind=kCustom, calls=%fused_computation.1.clone | custom fusion | bytes 788480 | tf_op jit(solution)/shard_map/jit(_take)/gather | solution.py:172
  80.5 2.2 %gather_fusion.5 = f32[512,192]{1,0:T(8,128)} fusion(f32[192,768]{0,1:T(8,128)S(1)} %pad_maximum_fusion.1, s32[1024]{0:T(1024)S(1)} %get-tuple-element.62), kind=kCustom, calls=%fused_computation.3.clone | custom fusion | bytes 788480 | tf_op jit(solution)/shard_map/jit(_take)/gather | solution.py:172
  82.7 2.6 %fusion.21 = f32[192,512]{0,1:T(8,128)S(1)} fusion(f32[512,192]{1,0:T(8,128)} %gather_fusion.5, f32[512,192]{1,0:T(8,128)} %gather_fusion.4, f32[512,192]{1,0:T(8,128)} %gather_fusion.3, f32[512,192]{1,0:T(8,128)} %gather_fusion.2, f32[192,512]{0,1:T(8,128)S(1)} %get-tuple-element.35, f32[4,192,512]{1,2,0:T(8,128)} %get-tuple-element.34, ...), kind=kLoop, calls=%fused_computation.65 | loop fusion | flops 2260992 | bytes 4139264 | tf_op jit(solution)/shard_map/mul | solution.py:173
  85.3 3.6 %collective-permute-start.2 = (f32[192,128]{0,1:T(8,128)S(1)}, f32[192,128]{0,1:T(8,128)S(1)}, u32[]{:S(2)}, u32[]{:S(2)}) collective-permute-start(f32[192,128]{0,1:T(8,128)S(1)} %get-tuple-element.40), channel_id=1, source_target_pairs={{0,4},{4,8},{8,12},{12,16},{16,20},{20,24},{24,28},{28,32},{32,36}... | collective-permute-start | bytes 294920 | tf_op jit(solution)/shard_map/ppermute | solution.py:26
  91.1 4.2 %collective-permute-done.3 = f32[192,128]{0,1:T(8,128)S(1)} collective-permute-done((f32[192,128]{0,1:T(8,128)S(1)}, f32[192,128]{0,1:T(8,128)S(1)}, u32[]{:S(2)}, u32[]{:S(2)}) %collective-permute-start.3) | collective-permute-done | bytes 98336 | tf_op jit(solution)/shard_map/ppermute | solution.py:27
  97.5 2.2 %gather_fusion.7 = f32[512,192]{1,0:T(8,128)} fusion(f32[192,768]{0,1:T(8,128)S(1)} %pad_maximum_fusion.2, s32[1024]{0:T(1024)S(1)} %get-tuple-element.64), kind=kCustom, calls=%fused_computation.5.clone | custom fusion | bytes 788480 | tf_op jit(solution)/shard_map/jit(_take)/gather | solution.py:172
  104.3 2.5 %fusion.15 = f32[192,512]{0,1:T(8,128)S(1)} fusion(f32[192,512]{0,1:T(8,128)S(1)} %fusion.21, f32[512,192]{1,0:T(8,128)} %gather_fusion.9, f32[512,192]{1,0:T(8,128)} %gather_fusion.8, f32[512,192]{1,0:T(8,128)} %gather_fusion.7, f32[512,192]{1,0:T(8,128)} %gather_fusion.6, f32[192,512]{0,1:T(8,128)S(1)} %get-tuple-element.35, ...), kind=kLoop, calls=%fused_computation.55 | loop fusion | flops 1474560 | bytes 4329472 | tf_op jit(solution)/shard_map/mul | solution.py:173
  108.7 2.4 %collective-permute-start.5 = (f32[192,128]{0,1:T(8,128)S(1)}, f32[192,128]{0,1:T(8,128)S(1)}, u32[]{:S(2)}, u32[]{:S(2)}) collective-permute-start(f32[192,128]{0,1:T(8,128)S(1)} %get-tuple-element.39), channel_id=1, source_target_pairs={{4,0},{8,4},{12,8},{16,12},{20,16},{24,20},{28,24},{32,28},{36,32}... | collective-permute-start | bytes 294920 | tf_op jit(solution)/shard_map/ppermute | solution.py:27
  111.1 3.9 %collective-permute-done.5 = f32[192,128]{0,1:T(8,128)S(1)} collective-permute-done((f32[192,128]{0,1:T(8,128)S(1)}, f32[192,128]{0,1:T(8,128)S(1)}, u32[]{:S(2)}, u32[]{:S(2)}) %collective-permute-start.5) | collective-permute-done | bytes 98336 | tf_op jit(solution)/shard_map/ppermute | solution.py:27
  117.3 2.2 %gather_fusion.11 = f32[512,192]{1,0:T(8,128)} fusion(f32[192,768]{0,1:T(8,128)S(1)} %pad_maximum_fusion.3, s32[1024]{0:T(1024)S(1)} %get-tuple-element.64), kind=kCustom, calls=%fused_computation.9.clone | custom fusion | bytes 788480 | tf_op jit(solution)/shard_map/jit(_take)/gather | solution.py:172
  124.0 2.5 %fusion.9 = f32[192,512]{0,1:T(8,128)S(1)} fusion(f32[192,512]{0,1:T(8,128)S(1)} %fusion.15, f32[512,192]{1,0:T(8,128)} %gather_fusion.13, f32[512,192]{1,0:T(8,128)} %gather_fusion.12, f32[512,192]{1,0:T(8,128)} %gather_fusion.11, f32[512,192]{1,0:T(8,128)} %gather_fusion.10, f32[192,512]{0,1:T(8,128)S(1)} %get-tuple-element.35, ...), kind=kLoop, calls=%fused_computation.45 | loop fusion | flops 1474560 | bytes 4329472 | tf_op jit(solution)/shard_map/mul | solution.py:173
  128.4 2.4 %collective-permute-start.7 = (f32[192,128]{0,1:T(8,128)S(1)}, f32[192,128]{0,1:T(8,128)S(1)}, u32[]{:S(2)}, u32[]{:S(2)}) collective-permute-start(f32[192,128]{0,1:T(8,128)S(1)} %get-tuple-element.37), channel_id=1, source_target_pairs={{4,0},{8,4},{12,8},{16,12},{20,16},{24,20},{28,24},{32,28},{36,32}... | collective-permute-start | bytes 294920 | tf_op jit(solution)/shard_map/ppermute | solution.py:27
  131.1 3.6 %collective-permute-done.7 = f32[192,128]{0,1:T(8,128)S(1)} collective-permute-done((f32[192,128]{0,1:T(8,128)S(1)}, f32[192,128]{0,1:T(8,128)S(1)}, u32[]{:S(2)}, u32[]{:S(2)}) %collective-permute-start.7) | collective-permute-done | bytes 98336 | tf_op jit(solution)/shard_map/ppermute | solution.py:27
  136.4 2.3 %gather_fusion.15 = f32[512,192]{1,0:T(8,128)} fusion(f32[192,768]{0,1:T(8,128)S(1)} %pad_maximum_fusion.4, s32[1024]{0:T(1024)S(1)} %get-tuple-element.64), kind=kCustom, calls=%fused_computation.13.clone | custom fusion | bytes 788480 | tf_op jit(solution)/shard_map/jit(_take)/gather | solution.py:172
  143.1 2.3 %fusion.79 = (bf16[192,512]{0,1:T(8,128)(2,1)S(1)}, f32[192,512]{0,1:T(8,128)S(1)}) fusion(f32[512]{0:T(512)S(1)} %convert_element_type.84, f32[192,512]{0,1:T(8,128)S(1)} %get-tuple-element.35, f32[192,512]{0,1:T(8,128)S(1)} %fusion.9, f32[512,192]{1,0:T(8,128)} %gather_fusion.17, pred[512]{0:T(512)(128)(4,1)S(1)} %get-tuple-element.67, ...), kind=kLoop, calls=%fused_computation.214 | loop fusion | flops 1572864 | bytes 4526080 | tf_op jit(solution)/shard_map/convert_element_type | solution.py:174
  146.2 8.7 %psum.7 = f32[8,128]{1,0:T(8,128)S(1)} all-reduce(f32[8,128]{1,0:T(8,128)S(1)} %reshape.172), channel_id=1, replica_groups=mesh['sec'=4,'tile'=32,'lev'=4] {'lev'}, use_global_device_ids=true, to_apply=%region_4.6 | all-reduce | flops 1024 | bytes 8192 | tf_op jit(solution)/shard_map/psum | solution.py:178
  156.0 14.6 %all-to-all-start.1 = ((f32[128,2,128]{2,1,0:T(2,128)}), f32[128,2,128]{2,1,0:T(2,128)S(1)}, u32[]{:S(2)}, u32[]{:S(2)}) async-start(f32[128,2,128]{2,1,0:T(2,128)} %copy.49), calls=%async_computation.1 | async-start | bytes 262144 | tf_op jit(solution)/shard_map/all_to_all | solution.py:183
  170.6 17.3 %all-to-all-done.1 = f32[128,2,128]{2,1,0:T(2,128)S(1)} async-done(((f32[128,2,128]{2,1,0:T(2,128)}), f32[128,2,128]{2,1,0:T(2,128)S(1)}, u32[]{:S(2)}, u32[]{:S(2)}) %all-to-all-start.1) | async-done | bytes 131104 | tf_op jit(solution)/shard_map/all_to_all | solution.py:183
  190.6 3.9 %collective-permute-start.8 = (f32[10,4,512]{2,1,0:T(4,128)S(1)}, f32[10,4,512]{2,1,0:T(4,128)S(1)}, u32[]{:S(2)}, u32[]{:S(2)}) collective-permute-start(f32[10,4,512]{2,1,0:T(4,128)S(1)} %get-tuple-element.32), channel_id=1, source_target_pairs={{0,4},{4,8},{8,12},{12,16},{16,20},{20,24},{24,28},{28,32},{32,36}... | collective-permute-start | bytes 245768 | tf_op jit(solution)/shard_map/ppermute | solution.py:26
  197.3 3.0 %collective-permute-done.9 = f32[10,4,512]{2,1,0:T(4,128)S(1)} collective-permute-done((f32[10,4,512]{2,1,0:T(4,128)S(1)}, f32[10,4,512]{2,1,0:T(4,128)S(1)}, u32[]{:S(2)}, u32[]{:S(2)}) %collective-permute-start.9) | collective-permute-done | bytes 81952 | tf_op jit(solution)/shard_map/ppermute | solution.py:27
  (163 shorter events, 51.4 us)
Async XLA Ops:
  6.6 51.8 %copy-start.13 = (f32[192]{0:T(256)S(1)}, f32[192]{0:T(256)}, u32[]{:S(2)}) copy-start(f32[192]{0:T(256)} %param.37) | copy-start | bytes 2308
  9.0 56.2 %copy-start.9 = (f32[4,512]{1,0:T(4,128)S(1)}, f32[4,512]{1,0:T(4,128)}, u32[]{:S(2)}) copy-start(f32[4,512]{1,0:T(4,128)} %param.40) | copy-start | bytes 24580
  9.0 48.4 %all-to-all-start = ((f32[128,2,257]{2,1,0:T(2,128)}), f32[128,2,257]{2,1,0:T(2,128)S(1)}, u32[]{:S(2)}, u32[]{:S(2)}) async-start(f32[128,2,257]{2,1,0:T(2,128)} %all_to_all.14), calls=%async_computation | async-start | bytes 786432 | tf_op jit(solution)/shard_map/all_to_all | solution.py:151
  58.9 14.8 %collective-permute-start = (f32[192,128]{0,1:T(8,128)S(1)}, f32[192,128]{0,1:T(8,128)S(1)}, u32[]{:S(2)}, u32[]{:S(2)}) collective-permute-start(f32[192,128]{0,1:T(8,128)S(1)} %get-tuple-element.42), channel_id=1, source_target_pairs={{0,4},{4,8},{8,12},{12,16},{16,20},{20,24},{24,28},{28,32},{32,36}... | collective-permute-start | bytes 294920 | tf_op jit(solution)/shard_map/ppermute | solution.py:26
  63.3 10.4 %collective-permute-start.1 = (f32[192,128]{0,1:T(8,128)S(1)}, f32[192,128]{0,1:T(8,128)S(1)}, u32[]{:S(2)}, u32[]{:S(2)}) collective-permute-start(f32[192,128]{0,1:T(8,128)S(1)} %get-tuple-element.43), channel_id=1, source_target_pairs={{4,0},{8,4},{12,8},{16,12},{20,16},{24,20},{28,24},{32,28},{36,32}... | collective-permute-start | bytes 294920 | tf_op jit(solution)/shard_map/ppermute | solution.py:27
  85.3 5.8 %collective-permute-start.2 = (f32[192,128]{0,1:T(8,128)S(1)}, f32[192,128]{0,1:T(8,128)S(1)}, u32[]{:S(2)}, u32[]{:S(2)}) collective-permute-start(f32[192,128]{0,1:T(8,128)S(1)} %get-tuple-element.40), channel_id=1, source_target_pairs={{0,4},{4,8},{8,12},{12,16},{16,20},{20,24},{24,28},{28,32},{32,36}... | collective-permute-start | bytes 294920 | tf_op jit(solution)/shard_map/ppermute | solution.py:26
  89.0 6.3 %collective-permute-start.3 = (f32[192,128]{0,1:T(8,128)S(1)}, f32[192,128]{0,1:T(8,128)S(1)}, u32[]{:S(2)}, u32[]{:S(2)}) collective-permute-start(f32[192,128]{0,1:T(8,128)S(1)} %get-tuple-element.41), channel_id=1, source_target_pairs={{4,0},{8,4},{12,8},{16,12},{20,16},{24,20},{28,24},{32,28},{36,32}... | collective-permute-start | bytes 294920 | tf_op jit(solution)/shard_map/ppermute | solution.py:27
  106.8 4.3 %collective-permute-start.4 = (f32[192,128]{0,1:T(8,128)S(1)}, f32[192,128]{0,1:T(8,128)S(1)}, u32[]{:S(2)}, u32[]{:S(2)}) collective-permute-start(f32[192,128]{0,1:T(8,128)S(1)} %get-tuple-element.38), channel_id=1, source_target_pairs={{0,4},{4,8},{8,12},{12,16},{16,20},{20,24},{24,28},{28,32},{32,36}... | collective-permute-start | bytes 294920 | tf_op jit(solution)/shard_map/ppermute | solution.py:26
  108.7 6.3 %collective-permute-start.5 = (f32[192,128]{0,1:T(8,128)S(1)}, f32[192,128]{0,1:T(8,128)S(1)}, u32[]{:S(2)}, u32[]{:S(2)}) collective-permute-start(f32[192,128]{0,1:T(8,128)S(1)} %get-tuple-element.39), channel_id=1, source_target_pairs={{4,0},{8,4},{12,8},{16,12},{20,16},{24,20},{28,24},{32,28},{36,32}... | collective-permute-start | bytes 294920 | tf_op jit(solution)/shard_map/ppermute | solution.py:27
  126.5 4.6 %collective-permute-start.6 = (f32[192,128]{0,1:T(8,128)S(1)}, f32[192,128]{0,1:T(8,128)S(1)}, u32[]{:S(2)}, u32[]{:S(2)}) collective-permute-start(f32[192,128]{0,1:T(8,128)S(1)} %get-tuple-element.36), channel_id=1, source_target_pairs={{0,4},{4,8},{8,12},{12,16},{16,20},{20,24},{24,28},{28,32},{32,36}... | collective-permute-start | bytes 294920 | tf_op jit(solution)/shard_map/ppermute | solution.py:26
  128.4 6.3 %collective-permute-start.7 = (f32[192,128]{0,1:T(8,128)S(1)}, f32[192,128]{0,1:T(8,128)S(1)}, u32[]{:S(2)}, u32[]{:S(2)}) collective-permute-start(f32[192,128]{0,1:T(8,128)S(1)} %get-tuple-element.37), channel_id=1, source_target_pairs={{4,0},{8,4},{12,8},{16,12},{20,16},{24,20},{28,24},{32,28},{36,32}... | collective-permute-start | bytes 294920 | tf_op jit(solution)/shard_map/ppermute | solution.py:27
  143.1 27.5 %copy-start.5 = (f32[2,32,512]{2,1,0:T(8,128)S(1)}, f32[2,32,512]{2,1,0:T(8,128)}, u32[]{:S(2)}) copy-start(f32[2,32,512]{2,1,0:T(8,128)} %param.24) | copy-start | bytes 393220
  145.4 44.3 %copy-start.18 = (s32[64]{0:T(128)S(1)}, s32[64]{0:T(128)}, u32[]{:S(2)}) copy-start(s32[64]{0:T(128)} %param.44) | copy-start | bytes 772
  145.4 44.8 %copy-start.1 = (bf16[32,512]{1,0:T(8,128)(2,1)S(1)}, bf16[32,512]{1,0:T(8,128)(2,1)}, u32[]{:S(2)}) copy-start(bf16[32,512]{1,0:T(8,128)(2,1)} %param.25) | copy-start | bytes 98308
  145.5 44.8 %copy-start.2 = (bf16[32,512]{1,0:T(8,128)(2,1)S(1)}, bf16[32,512]{1,0:T(8,128)(2,1)}, u32[]{:S(2)}) copy-start(bf16[32,512]{1,0:T(8,128)(2,1)} %param.26) | copy-start | bytes 98308
  145.5 44.8 %copy-start.19 = (f32[2]{0:T(128)S(1)}, f32[2]{0:T(128)}, u32[]{:S(2)}) copy-start(f32[2]{0:T(128)} %param.32) | copy-start | bytes 28
  145.5 44.8 %copy-start.20 = (f32[2]{0:T(128)S(1)}, f32[2]{0:T(128)}, u32[]{:S(2)}) copy-start(f32[2]{0:T(128)} %param.33) | copy-start | bytes 28
  146.0 44.4 %copy-start.4 = (bf16[32,512]{1,0:T(8,128)(2,1)S(1)}, bf16[32,512]{1,0:T(8,128)(2,1)}, u32[]{:S(2)}) copy-start(bf16[32,512]{1,0:T(8,128)(2,1)} %param.27) | copy-start | bytes 98308
  154.9 35.6 %copy-start.6 = (s32[32,512]{1,0:T(8,128)S(1)}, s32[32,512]{1,0:T(8,128)}, u32[]{:S(2)}) copy-start(s32[32,512]{1,0:T(8,128)} %param.28) | copy-start | bytes 196612
  155.2 35.3 %copy-start.7 = (s32[32,512]{1,0:T(8,128)S(1)}, s32[32,512]{1,0:T(8,128)}, u32[]{:S(2)}) copy-start(s32[32,512]{1,0:T(8,128)} %param.29) | copy-start | bytes 196612
  156.0 34.6 %copy-start.8 = (s32[32,512]{1,0:T(8,128)S(1)}, s32[32,512]{1,0:T(8,128)}, u32[]{:S(2)}) copy-start(s32[32,512]{1,0:T(8,128)} %param.30) | copy-start | bytes 196612
  156.0 31.9 %all-to-all-start.1 = ((f32[128,2,128]{2,1,0:T(2,128)}), f32[128,2,128]{2,1,0:T(2,128)S(1)}, u32[]{:S(2)}, u32[]{:S(2)}) async-start(f32[128,2,128]{2,1,0:T(2,128)} %copy.49), calls=%async_computation.1 | async-start | bytes 262144 | tf_op jit(solution)/shard_map/all_to_all | solution.py:183
  190.6 6.7 %collective-permute-start.8 = (f32[10,4,512]{2,1,0:T(4,128)S(1)}, f32[10,4,512]{2,1,0:T(4,128)S(1)}, u32[]{:S(2)}, u32[]{:S(2)}) collective-permute-start(f32[10,4,512]{2,1,0:T(4,128)S(1)} %get-tuple-element.32), channel_id=1, source_target_pairs={{0,4},{4,8},{8,12},{12,16},{16,20},{20,24},{24,28},{28,32},{32,36}... | collective-permute-start | bytes 245768 | tf_op jit(solution)/shard_map/ppermute | solution.py:26
  194.5 5.8 %collective-permute-start.9 = (f32[10,4,512]{2,1,0:T(4,128)S(1)}, f32[10,4,512]{2,1,0:T(4,128)S(1)}, u32[]{:S(2)}, u32[]{:S(2)}) collective-permute-start(f32[10,4,512]{2,1,0:T(4,128)S(1)} %get-tuple-element.33), channel_id=1, source_target_pairs={{4,0},{8,4},{12,8},{16,12},{20,16},{24,20},{28,24},{32,28},{36,32}... | collective-permute-start | bytes 245768 | tf_op jit(solution)/shard_map/ppermute | solution.py:27
  (10 other events, 152.1 us)

commit v2 on v1

--- a/solution.py
+++ b/solution.py
@@ -1,6 +1,8 @@
 import jax
 import jax.numpy as jnp
 from jax import lax
+from jax.experimental import pallas as pl
+from jax.experimental.pallas import tpu as pltpu
 from jax.sharding import PartitionSpec as P
 
 OSTEPS = 4
@@ -54,10 +56,69 @@
         cosines * wave_forcing[2][None, :] + sine_terms * wave_forcing[3][None, :], 0.0
     )
     base_rate = 0.5 * band_pace[:, None] * (1.0 + 0.5 * jnp.tanh(drift_term))
-    inflow = base_rate[None] * jnp.maximum(
-        -jnp.cos(band_dir[None, :, None] - facing[:, None, :]), 0.0
-    )
+    facing_cos = jnp.cos(facing)[:, None, :]
+    facing_sin = jnp.sin(facing)[:, None, :]
+    along = cosines[None] * facing_cos + sine_terms[None] * facing_sin
+    inflow = base_rate[None] * jnp.maximum(-along, 0.0)
     return (growth[:, None] * push_term, inflow)
+
+
+def split3(x):
+    hi = lax.reduce_precision(x, exponent_bits=8, mantissa_bits=7)
+    rest = x - hi
+    mid = lax.reduce_precision(rest, exponent_bits=8, mantissa_bits=7)
+    lo = rest - mid
+    return hi.astype(jnp.bfloat16), mid.astype(jnp.bfloat16), lo.astype(jnp.bfloat16)
+
+
+def sweep_kernel(padded_ref, sel_ref, inflow_ref, rate_ref, alive_ref, out_ref):
+    bands = out_ref.shape[0]
+    for t in range(sel_ref.shape[0]):
+        window = padded_ref[:, 128 * t : 128 * t + 384]
+        parts = jnp.concatenate(split3(window), axis=0)
+        picked = jnp.dot(parts, sel_ref[t], preferred_element_type=jnp.float32)
+        gathered = picked[:bands] + picked[bands : 2 * bands] + picked[2 * bands :]
+        cols = slice(128 * t, 128 * t + 128)
+        energy = padded_ref[:, 128 * t + 128 : 128 * t + 256]
+        arriving = inflow_ref[0, :, cols] * gathered[:, 0:128]
+        for k in range(1, NBRS):
+            arriving = arriving + inflow_ref[k, :, cols] * gathered[:, 128 * k : 128 * k + 128]
+        out_ref[:, cols] = (energy + arriving - rate_ref[:, cols] * energy) * alive_ref[:, cols]
+
+
+def wave_sweep(padded, sel, inflow, rate, alive):
+    bands, nodes = rate.shape
+    vmem = pl.BlockSpec(memory_space=pltpu.VMEM)
+    flops = 2 * 3 * bands * 384 * nodes * NBRS
+    moved = 4 * (padded.size + inflow.size + 2 * rate.size) + 2 * sel.size
+    return pl.pallas_call(
+        sweep_kernel,
+        out_shape=jax.ShapeDtypeStruct((bands, nodes), jnp.float32),
+        in_specs=[vmem] * 5,
+        out_specs=vmem,
+        cost_estimate=pl.CostEstimate(flops=flops, bytes_accessed=moved, transcendentals=0),
+    )(padded, sel, inflow, rate, alive)
+
+
+def selection(local_index):
+    nbrs, nodes = local_index.shape
+    tiles = nodes // 128
+    start = 128 * jnp.arange(tiles, dtype=jnp.int32)
+    idx = local_index.reshape(nbrs, tiles, 128) - start[None, :, None]
+    rows = jnp.arange(384, dtype=jnp.int32)
+    sel = idx.transpose(1, 0, 2)[:, None, :, :] == rows[None, :, None, None]
+    return sel.reshape(tiles, 384, nbrs * 128).astype(jnp.bfloat16)
+
+
+def lev_sum(x):
+    count = lax.axis_size("lev")
+    if count & (count - 1):
+        return lax.psum(x, "lev")
+    step = 1
+    while step < count:
+        x = x + lax.ppermute(x, "lev", [(i, i ^ step) for i in range(count)])
+        step *= 2
+    return x
 
 
 def ocean_step(
@@ -165,17 +226,15 @@
     first_node = lax.axis_index(("sec", "tile")) * node_count
     total_rate = jnp.sum(inflow, axis=0)
     local_index = neighbors - first_node + 128
+    sel = selection(local_index)
     for sweep in range(WSTEPS):
         padded = with_halo(energy, ((("sec", "tile"), 1),), 128)
-        arriving = jnp.zeros_like(energy)
-        for neighbor in range(NBRS):
-            arriving = arriving + inflow[neighbor] * jnp.take(padded, local_index[neighbor], axis=1)
-        energy = (energy + arriving - total_rate * energy) * alive_mask
+        energy = wave_sweep(padded, sel, inflow, total_rate, alive_mask)
     waves_out = energy.astype(jnp.bfloat16)
     coefficient = jnp.stack(
         [band_orbital * jnp.cos(band_angle), band_orbital * jnp.sin(band_angle)]
     )
-    orbital = lax.psum(jnp.dot(coefficient, energy, precision=HIGHEST), "lev")
+    orbital = lev_sum(jnp.dot(coefficient, energy, precision=HIGHEST))
     orbital_blocks = jnp.transpose(orbital.reshape(2, block_count, 64), (1, 0, 2)).reshape(
         block_count, 128
     )

time: 203 us -> 180 us (0.89)
  local copies, waits for them, and re-layouts: 41.6 us -> 8.72 us
  Pallas kernels: 0 us -> 17.6 us
  blocking collectives: 8.71 us -> 0 us
  other arithmetic: 25.7 us -> 18.2 us
  starting transfers between devices: 61.7 us -> 68.7 us
    gather x16 -> x0, local copies, waits for them, and re-layouts: 35.1 us -> none  [per_device(): jnp.take(padded, local_index[neighbor], axis=1)]
    pallas_call x0 -> x4, Pallas kernels: none -> 17.6 us  [wave_sweep(): pl.pallas_call(sweep_kernel, out_shape=jax.ShapeDtypeStruct((bands, nodes...]
    mul x5 -> x2, other arithmetic: 16.4 us -> 0.29 us  [the longest x1 0.28 us: band_rates(): base_rate = 0.5 * band_pace[:, None] * (1.0 + 0.5 * jnp.tanh(drift_term))]
    psum x1 -> x0, blocking collectives: 8.71 us -> none  [per_device(): orbital = lax.psum(jnp.dot(coefficient, energy, precision=HIGHEST), 'lev')]
    ppermute x0 -> x2, starting transfers between devices: none -> 8.01 us  [lev_sum(): x = x + lax.ppermute(x, 'lev', [(i, i ^ step) for i in range(count)])]
    concatenate x5, other arithmetic: 0.35 us -> 6.55 us  [with_halo(): x = jnp.concatenate([before, x, after], axis=dim)]
    slice x5, local copies, waits for them, and re-layouts: 0.11 us -> 2.91 us  [with_halo(): last = lax.slice_in_dim(x, length - width, length, axis=dim)]
    reduce_sum x0 -> x1, other arithmetic: none -> 2.34 us  [per_device(): total_rate = jnp.sum(inflow, axis=0)]
  transfers between devices with their start and end apart: 12 -> 14, of which waited for: 6 -> 9; matrix products, arithmetic and copies ran while one was open for 5% -> 3% of each run, Pallas kernels for 0% -> 0%
where the time goes in v2:
time: 180 us; the launch traced here: 179 us
  starting transfers between devices  68.7 us (38%)
  waiting for transfers between devices  60.1 us (33%)
  other arithmetic  18.2 us (10%)
  Pallas kernels  17.6 us (10%)
  local copies, waits for them, and re-layouts  8.72 us (5%)
  matrix products  4.72 us (3%)
    all_to_all x1, waiting for transfers between devices, per_device(): lax.all_to_all(send_rows, ('sec', 'tile'), split_axis=0, concat_axis=0, t...  25.8 us
    all_to_all x1, starting transfers between devices, per_device(): lax.all_to_all(send_rows, ('sec', 'tile'), split_axis=0, concat_axis=0, t...  20.4 us
    pallas_call x4, Pallas kernels, wave_sweep(): pl.pallas_call(sweep_kernel, out_shape=jax.ShapeDtypeStruct((bands, nodes...  17.6 us
    all_to_all x1, waiting for transfers between devices, per_device(): lax.all_to_all(back_rows, ('sec', 'tile'), split_axis=0, concat_axis=0, t...  17.2 us
    ppermute x5, waiting for transfers between devices, with_halo(): after = lax.ppermute(first, axis, down)  15.2 us
    all_to_all x1, starting transfers between devices, per_device(): lax.all_to_all(back_rows, ('sec', 'tile'), split_axis=0, concat_axis=0, t...  14.9 us
    ppermute x5, starting transfers between devices, with_halo(): before = lax.ppermute(last, axis, up)  14.1 us
    ppermute x5, starting transfers between devices, with_halo(): after = lax.ppermute(first, axis, down)  11.2 us
  transfers between devices with their start and end apart: 14, of which 9 were waited for; matrix products, arithmetic and copies ran while one was open for 3% of the time, Pallas kernels for 0%

profile of v2, /device:TPU:1, one launch (start us, length us, event | category | flops | bytes accessed | tf_op | source)
XLA Modules:
  0.0 179.5 jit_solution(6623663080276121758)
XLA Ops:
  9.0 20.4 %all-to-all-start = ((f32[128,2,257]{2,1,0:T(2,128)}), f32[128,2,257]{2,1,0:T(2,128)S(1)}, u32[]{:S(2)}, u32[]{:S(2)}) async-start(f32[128,2,257]{2,1,0:T(2,128)} %all_to_all.14), calls=%async_computation | async-start | bytes 786432 | tf_op jit(solution)/shard_map/all_to_all | solution.py:212
  31.5 25.8 %all-to-all-done = f32[128,2,257]{2,1,0:T(2,128)S(1)} async-done(((f32[128,2,257]{2,1,0:T(2,128)}), f32[128,2,257]{2,1,0:T(2,128)S(1)}, u32[]{:S(2)}, u32[]{:S(2)}) %all-to-all-start) | async-done | bytes 263200 | tf_op jit(solution)/shard_map/all_to_all | solution.py:212
  58.6 4.4 %collective-permute-start = (f32[192,128]{1,0:T(8,128)S(1)}, f32[192,128]{1,0:T(8,128)S(1)}, u32[]{:S(2)}, u32[]{:S(2)}) collective-permute-start(f32[192,128]{1,0:T(8,128)S(1)} %get-tuple-element.33), channel_id=1, source_target_pairs={{0,4},{4,8},{8,12},{12,16},{16,20},{20,24},{24,28},{28,32},{32,36}... | collective-permute-start | bytes 294920 | tf_op jit(solution)/shard_map/ppermute | solution.py:28
  63.0 1.9 %collective-permute-start.1 = (f32[192,128]{1,0:T(8,128)S(1)}, f32[192,128]{1,0:T(8,128)S(1)}, u32[]{:S(2)}, u32[]{:S(2)}) collective-permute-start(f32[192,128]{1,0:T(8,128)S(1)} %get-tuple-element.34), channel_id=1, source_target_pairs={{4,0},{8,4},{12,8},{16,12},{20,16},{24,20},{28,24},{32,28},{36,32}... | collective-permute-start | bytes 294920 | tf_op jit(solution)/shard_map/ppermute | solution.py:29
  64.9 2.3 %fusion.43 = (f32[192,512]{1,0:T(8,128)}, f32[4,192,512]{2,1,0:T(8,128)}) fusion(f32[4,512]{1,0:T(4,128)S(1)} %get-tuple-element.44, f32[192]{0:T(256)S(1)} %get-tuple-element.50, f32[4,512]{1,0:T(4,128)S(1)} %get-tuple-element.43, f32[192]{0:T(256)S(1)} %get-tuple-element.49, f32[192,512]{1,0:T(8,128)S(1)} %get-tuple-element.45), kind=kLoop, calls=%fused_computation.117 | loop fusion | flops 2654208 | bytes 2377216 | tf_op jit(solution)/shard_map/reduce_sum | solution.py:227
  69.8 4.4 %shard_map.221 = f32[192,512]{1,0:T(8,128)} custom-call(f32[192,768]{1,0:T(8,128)} %pad_maximum_fusion.1.padded_ref, bf16[4,384,512]{2,1,0:T(8,128)(2,1)} %fusion.sel_ref, f32[4,192,512]{2,1,0:T(8,128)} %get-tuple-element.26.inflow_ref, f32[192,512]{1,0:T(8,128)} %get-tuple-element.25.rate_ref, f32[1,512]{1,0:T(1,128)} %bitcast.81), custom_call_target="tpu_custom_call" | custom-call | flops 905969664 | bytes 4521984 | tf_op jit(solution)/shard_map/pallas_call | solution.py:94
  75.2 2.0 %collective-permute-start.2 = (f32[192,128]{1,0:T(8,128)S(1)}, f32[192,128]{1,0:T(8,128)S(1)}, u32[]{:S(2)}, u32[]{:S(2)}) collective-permute-start(f32[192,128]{1,0:T(8,128)S(1)} %get-tuple-element.31), channel_id=1, source_target_pairs={{0,4},{4,8},{8,12},{12,16},{16,20},{20,24},{24,28},{28,32},{32,36}... | collective-permute-start | bytes 294920 | tf_op jit(solution)/shard_map/ppermute | solution.py:28
  77.1 2.3 %collective-permute-start.3 = (f32[192,128]{1,0:T(8,128)S(1)}, f32[192,128]{1,0:T(8,128)S(1)}, u32[]{:S(2)}, u32[]{:S(2)}) collective-permute-start(f32[192,128]{1,0:T(8,128)S(1)} %get-tuple-element.32), channel_id=1, source_target_pairs={{4,0},{8,4},{12,8},{16,12},{20,16},{24,20},{28,24},{32,28},{36,32}... | collective-permute-start | bytes 294920 | tf_op jit(solution)/shard_map/ppermute | solution.py:29
  79.5 3.6 %collective-permute-done.3 = f32[192,128]{1,0:T(8,128)S(1)} collective-permute-done((f32[192,128]{1,0:T(8,128)S(1)}, f32[192,128]{1,0:T(8,128)S(1)}, u32[]{:S(2)}, u32[]{:S(2)}) %collective-permute-start.3) | collective-permute-done | bytes 98336 | tf_op jit(solution)/shard_map/ppermute | solution.py:29
  84.9 4.4 %shard_map.222 = f32[192,512]{1,0:T(8,128)} custom-call(f32[192,768]{1,0:T(8,128)} %pad_maximum_fusion.2.padded_ref, bf16[4,384,512]{2,1,0:T(8,128)(2,1)} %fusion.sel_ref, f32[4,192,512]{2,1,0:T(8,128)} %get-tuple-element.26.inflow_ref, f32[192,512]{1,0:T(8,128)} %get-tuple-element.25.rate_ref, f32[1,512]{1,0:T(1,128)} %bitcast.82), custom_call_target="tpu_custom_call" | custom-call | flops 905969664 | bytes 4521984 | tf_op jit(solution)/shard_map/pallas_call | solution.py:94
  92.2 2.4 %collective-permute-start.5 = (f32[192,128]{1,0:T(8,128)S(1)}, f32[192,128]{1,0:T(8,128)S(1)}, u32[]{:S(2)}, u32[]{:S(2)}) collective-permute-start(f32[192,128]{1,0:T(8,128)S(1)} %get-tuple-element.30), channel_id=1, source_target_pairs={{4,0},{8,4},{12,8},{16,12},{20,16},{24,20},{28,24},{32,28},{36,32}... | collective-permute-start | bytes 294920 | tf_op jit(solution)/shard_map/ppermute | solution.py:29
  94.6 3.5 %collective-permute-done.5 = f32[192,128]{1,0:T(8,128)S(1)} collective-permute-done((f32[192,128]{1,0:T(8,128)S(1)}, f32[192,128]{1,0:T(8,128)S(1)}, u32[]{:S(2)}, u32[]{:S(2)}) %collective-permute-start.5) | collective-permute-done | bytes 98336 | tf_op jit(solution)/shard_map/ppermute | solution.py:29
  100.0 4.4 %shard_map.223 = f32[192,512]{1,0:T(8,128)} custom-call(f32[192,768]{1,0:T(8,128)} %pad_maximum_fusion.3.padded_ref, bf16[4,384,512]{2,1,0:T(8,128)(2,1)} %fusion.sel_ref, f32[4,192,512]{2,1,0:T(8,128)} %get-tuple-element.26.inflow_ref, f32[192,512]{1,0:T(8,128)} %get-tuple-element.25.rate_ref, f32[1,512]{1,0:T(1,128)} %bitcast.83), custom_call_target="tpu_custom_call" | custom-call | flops 905969664 | bytes 4521984 | tf_op jit(solution)/shard_map/pallas_call | solution.py:94
  105.3 1.9 %collective-permute-start.6 = (f32[192,128]{1,0:T(8,128)S(1)}, f32[192,128]{1,0:T(8,128)S(1)}, u32[]{:S(2)}, u32[]{:S(2)}) collective-permute-start(f32[192,128]{1,0:T(8,128)S(1)} %get-tuple-element.27), channel_id=1, source_target_pairs={{0,4},{4,8},{8,12},{12,16},{16,20},{20,24},{24,28},{28,32},{32,36}... | collective-permute-start | bytes 294920 | tf_op jit(solution)/shard_map/ppermute | solution.py:28
  107.3 2.6 %collective-permute-start.7 = (f32[192,128]{1,0:T(8,128)S(1)}, f32[192,128]{1,0:T(8,128)S(1)}, u32[]{:S(2)}, u32[]{:S(2)}) collective-permute-start(f32[192,128]{1,0:T(8,128)S(1)} %get-tuple-element.28), channel_id=1, source_target_pairs={{4,0},{8,4},{12,8},{16,12},{20,16},{24,20},{28,24},{32,28},{36,32}... | collective-permute-start | bytes 294920 | tf_op jit(solution)/shard_map/ppermute | solution.py:29
  109.9 3.3 %collective-permute-done.7 = f32[192,128]{1,0:T(8,128)S(1)} collective-permute-done((f32[192,128]{1,0:T(8,128)S(1)}, f32[192,128]{1,0:T(8,128)S(1)}, u32[]{:S(2)}, u32[]{:S(2)}) %collective-permute-start.7) | collective-permute-done | bytes 98336 | tf_op jit(solution)/shard_map/ppermute | solution.py:29
  115.1 4.4 %shard_map.224 = f32[192,512]{1,0:T(8,128)} custom-call(f32[192,768]{1,0:T(8,128)} %pad_maximum_fusion.4.padded_ref, bf16[4,384,512]{2,1,0:T(8,128)(2,1)} %fusion.sel_ref, f32[4,192,512]{2,1,0:T(8,128)} %get-tuple-element.26.inflow_ref, f32[192,512]{1,0:T(8,128)} %get-tuple-element.25.rate_ref, f32[1,512]{1,0:T(1,128)} %bitcast.84), custom_call_target="tpu_custom_call" | custom-call | flops 905969664 | bytes 4521984 | tf_op jit(solution)/shard_map/pallas_call | solution.py:94
  120.8 3.2 %collective-permute-start.8 = (f32[2,512]{1,0:T(2,128)S(1)}, f32[2,512]{1,0:T(2,128)S(1)}, u32[]{:S(2)}, u32[]{:S(2)}) collective-permute-start(f32[2,512]{1,0:T(2,128)S(1)} %fusion.49), channel_id=1, source_target_pairs={{0,1},{1,0},{2,3},{3,2},{4,5},{5,4},{6,7},{7,6},{8,9},{9,8},{10,11... | collective-permute-start | bytes 12296 | tf_op jit(solution)/shard_map/ppermute | solution.py:119
  125.2 4.8 %collective-permute-start.9 = (f32[2,512]{1,0:T(2,128)S(1)}, f32[2,512]{1,0:T(2,128)S(1)}, u32[]{:S(2)}, u32[]{:S(2)}) collective-permute-start(f32[2,512]{1,0:T(2,128)S(1)} %add.168), channel_id=1, source_target_pairs={{0,2},{1,3},{2,0},{3,1},{4,6},{5,7},{6,4},{7,5},{8,10},{9,11},{10,... | collective-permute-start | bytes 12296 | tf_op jit(solution)/shard_map/ppermute | solution.py:119
  132.2 14.9 %all-to-all-start.1 = ((f32[128,2,128]{2,1,0:T(2,128)}), f32[128,2,128]{2,1,0:T(2,128)S(1)}, u32[]{:S(2)}, u32[]{:S(2)}) async-start(f32[128,2,128]{2,1,0:T(2,128)} %copy.44), calls=%async_computation.1 | async-start | bytes 262144 | tf_op jit(solution)/shard_map/all_to_all | solution.py:242
  147.3 17.2 %all-to-all-done.1 = f32[128,2,128]{2,1,0:T(2,128)S(1)} async-done(((f32[128,2,128]{2,1,0:T(2,128)}), f32[128,2,128]{2,1,0:T(2,128)S(1)}, u32[]{:S(2)}, u32[]{:S(2)}) %all-to-all-start.1) | async-done | bytes 131104 | tf_op jit(solution)/shard_map/all_to_all | solution.py:242
  167.2 3.9 %collective-permute-start.10 = (f32[10,4,512]{2,1,0:T(4,128)S(1)}, f32[10,4,512]{2,1,0:T(4,128)S(1)}, u32[]{:S(2)}, u32[]{:S(2)}) collective-permute-start(f32[10,4,512]{2,1,0:T(4,128)S(1)} %get-tuple-element.23), channel_id=1, source_target_pairs={{0,4},{4,8},{8,12},{12,16},{16,20},{20,24},{24,28},{28,32},{32,36}... | collective-permute-start | bytes 245768 | tf_op jit(solution)/shard_map/ppermute | solution.py:28
  171.2 1.9 %collective-permute-start.11 = (f32[10,4,512]{2,1,0:T(4,128)S(1)}, f32[10,4,512]{2,1,0:T(4,128)S(1)}, u32[]{:S(2)}, u32[]{:S(2)}) collective-permute-start(f32[10,4,512]{2,1,0:T(4,128)S(1)} %get-tuple-element.24), channel_id=1, source_target_pairs={{4,0},{8,4},{12,8},{16,12},{20,16},{24,20},{28,24},{32,28},{36,32}... | collective-permute-start | bytes 245768 | tf_op jit(solution)/shard_map/ppermute | solution.py:29
  173.8 3.1 %collective-permute-done.11 = f32[10,4,512]{2,1,0:T(4,128)S(1)} collective-permute-done((f32[10,4,512]{2,1,0:T(4,128)S(1)}, f32[10,4,512]{2,1,0:T(4,128)S(1)}, u32[]{:S(2)}, u32[]{:S(2)}) %collective-permute-start.11) | collective-permute-done | bytes 81952 | tf_op jit(solution)/shard_map/ppermute | solution.py:29
  (151 shorter events, 34.9 us)
Async XLA Ops:
  4.7 24.7 %copy-start.15 = (s32[512]{0:T(512)S(1)}, s32[512]{0:T(512)}, u32[]{:S(2)}) copy-start(s32[512]{0:T(512)} %param.39) | copy-start | bytes 6148
  4.7 24.8 %copy-start.13 = (s32[4,512]{1,0:T(4,128)S(1)}, s32[4,512]{1,0:T(4,128)}, u32[]{:S(2)}) copy-start(s32[4,512]{1,0:T(4,128)} %param.37) | copy-start | bytes 24580
  6.5 23.2 %copy-start.12 = (f32[4,512]{1,0:T(4,128)S(1)}, f32[4,512]{1,0:T(4,128)}, u32[]{:S(2)}) copy-start(f32[4,512]{1,0:T(4,128)} %param.38) | copy-start | bytes 24580
  9.0 48.2 %all-to-all-start = ((f32[128,2,257]{2,1,0:T(2,128)}), f32[128,2,257]{2,1,0:T(2,128)S(1)}, u32[]{:S(2)}, u32[]{:S(2)}) async-start(f32[128,2,257]{2,1,0:T(2,128)} %all_to_all.14), calls=%async_computation | async-start | bytes 786432 | tf_op jit(solution)/shard_map/all_to_all | solution.py:212
  29.4 28.9 %copy-start.4 = (bf16[192,512]{1,0:T(8,128)(2,1)S(1)}, bf16[192,512]{1,0:T(8,128)(2,1)}, u32[]{:S(2)}) copy-start(bf16[192,512]{1,0:T(8,128)(2,1)} %param.32) | copy-start | bytes 589828
  29.4 28.9 %copy-start.19 = (f32[192]{0:T(256)S(1)}, f32[192]{0:T(256)}, u32[]{:S(2)}) copy-start(f32[192]{0:T(256)} %param.35) | copy-start | bytes 2308
  29.5 29.1 %copy-start.7 = (f32[512]{0:T(512)}, f32[512]{0:T(512)S(1)}, u32[]{:S(2)}) copy-start(f32[512]{0:T(512)S(1)} %convert_element_type.87) | copy-start | bytes 6148
  58.6 8.7 %collective-permute-start = (f32[192,128]{1,0:T(8,128)S(1)}, f32[192,128]{1,0:T(8,128)S(1)}, u32[]{:S(2)}, u32[]{:S(2)}) collective-permute-start(f32[192,128]{1,0:T(8,128)S(1)} %get-tuple-element.33), channel_id=1, source_target_pairs={{0,4},{4,8},{8,12},{12,16},{16,20},{20,24},{24,28},{28,32},{32,36}... | collective-permute-start | bytes 294920 | tf_op jit(solution)/shard_map/ppermute | solution.py:28
  63.0 5.9 %collective-permute-start.1 = (f32[192,128]{1,0:T(8,128)S(1)}, f32[192,128]{1,0:T(8,128)S(1)}, u32[]{:S(2)}, u32[]{:S(2)}) collective-permute-start(f32[192,128]{1,0:T(8,128)S(1)} %get-tuple-element.34), channel_id=1, source_target_pairs={{4,0},{8,4},{12,8},{16,12},{20,16},{24,20},{28,24},{32,28},{36,32}... | collective-permute-start | bytes 294920 | tf_op jit(solution)/shard_map/ppermute | solution.py:29
  75.2 4.3 %collective-permute-start.2 = (f32[192,128]{1,0:T(8,128)S(1)}, f32[192,128]{1,0:T(8,128)S(1)}, u32[]{:S(2)}, u32[]{:S(2)}) collective-permute-start(f32[192,128]{1,0:T(8,128)S(1)} %get-tuple-element.31), channel_id=1, source_target_pairs={{0,4},{4,8},{8,12},{12,16},{16,20},{20,24},{24,28},{28,32},{32,36}... | collective-permute-start | bytes 294920 | tf_op jit(solution)/shard_map/ppermute | solution.py:28
  77.1 5.9 %collective-permute-start.3 = (f32[192,128]{1,0:T(8,128)S(1)}, f32[192,128]{1,0:T(8,128)S(1)}, u32[]{:S(2)}, u32[]{:S(2)}) collective-permute-start(f32[192,128]{1,0:T(8,128)S(1)} %get-tuple-element.32), channel_id=1, source_target_pairs={{4,0},{8,4},{12,8},{16,12},{20,16},{24,20},{28,24},{32,28},{36,32}... | collective-permute-start | bytes 294920 | tf_op jit(solution)/shard_map/ppermute | solution.py:29
  90.3 4.3 %collective-permute-start.4 = (f32[192,128]{1,0:T(8,128)S(1)}, f32[192,128]{1,0:T(8,128)S(1)}, u32[]{:S(2)}, u32[]{:S(2)}) collective-permute-start(f32[192,128]{1,0:T(8,128)S(1)} %get-tuple-element.29), channel_id=1, source_target_pairs={{0,4},{4,8},{8,12},{12,16},{16,20},{20,24},{24,28},{28,32},{32,36}... | collective-permute-start | bytes 294920 | tf_op jit(solution)/shard_map/ppermute | solution.py:28
  92.2 5.9 %collective-permute-start.5 = (f32[192,128]{1,0:T(8,128)S(1)}, f32[192,128]{1,0:T(8,128)S(1)}, u32[]{:S(2)}, u32[]{:S(2)}) collective-permute-start(f32[192,128]{1,0:T(8,128)S(1)} %get-tuple-element.30), channel_id=1, source_target_pairs={{4,0},{8,4},{12,8},{16,12},{20,16},{24,20},{28,24},{32,28},{36,32}... | collective-permute-start | bytes 294920 | tf_op jit(solution)/shard_map/ppermute | solution.py:29
  105.3 4.6 %collective-permute-start.6 = (f32[192,128]{1,0:T(8,128)S(1)}, f32[192,128]{1,0:T(8,128)S(1)}, u32[]{:S(2)}, u32[]{:S(2)}) collective-permute-start(f32[192,128]{1,0:T(8,128)S(1)} %get-tuple-element.27), channel_id=1, source_target_pairs={{0,4},{4,8},{8,12},{12,16},{16,20},{20,24},{24,28},{28,32},{32,36}... | collective-permute-start | bytes 294920 | tf_op jit(solution)/shard_map/ppermute | solution.py:28
  107.3 5.9 %collective-permute-start.7 = (f32[192,128]{1,0:T(8,128)S(1)}, f32[192,128]{1,0:T(8,128)S(1)}, u32[]{:S(2)}, u32[]{:S(2)}) collective-permute-start(f32[192,128]{1,0:T(8,128)S(1)} %get-tuple-element.28), channel_id=1, source_target_pairs={{4,0},{8,4},{12,8},{16,12},{20,16},{24,20},{28,24},{32,28},{36,32}... | collective-permute-start | bytes 294920 | tf_op jit(solution)/shard_map/ppermute | solution.py:29
  115.1 32.2 %copy-start.6 = (f32[2,32,512]{2,1,0:T(8,128)S(1)}, f32[2,32,512]{2,1,0:T(8,128)}, u32[]{:S(2)}) copy-start(f32[2,32,512]{2,1,0:T(8,128)} %param.22) | copy-start | bytes 393220
  119.5 46.9 %copy-start.20 = (s32[64]{0:T(128)S(1)}, s32[64]{0:T(128)}, u32[]{:S(2)}) copy-start(s32[64]{0:T(128)} %param.42) | copy-start | bytes 772
  120.8 4.3 %collective-permute-start.8 = (f32[2,512]{1,0:T(2,128)S(1)}, f32[2,512]{1,0:T(2,128)S(1)}, u32[]{:S(2)}, u32[]{:S(2)}) collective-permute-start(f32[2,512]{1,0:T(2,128)S(1)} %fusion.49), channel_id=1, source_target_pairs={{0,1},{1,0},{2,3},{3,2},{4,5},{5,4},{6,7},{7,6},{8,9},{9,8},{10,11... | collective-permute-start | bytes 12296 | tf_op jit(solution)/shard_map/ppermute | solution.py:119
  125.2 5.8 %collective-permute-start.9 = (f32[2,512]{1,0:T(2,128)S(1)}, f32[2,512]{1,0:T(2,128)S(1)}, u32[]{:S(2)}, u32[]{:S(2)}) collective-permute-start(f32[2,512]{1,0:T(2,128)S(1)} %add.168), channel_id=1, source_target_pairs={{0,2},{1,3},{2,0},{3,1},{4,6},{5,7},{6,4},{7,5},{8,10},{9,11},{10,... | collective-permute-start | bytes 12296 | tf_op jit(solution)/shard_map/ppermute | solution.py:119
  132.2 34.6 %copy-start.2 = (bf16[32,512]{1,0:T(8,128)(2,1)S(1)}, bf16[32,512]{1,0:T(8,128)(2,1)}, u32[]{:S(2)}) copy-start(bf16[32,512]{1,0:T(8,128)(2,1)} %param.23) | copy-start | bytes 98308
  132.2 34.6 %copy-start.3 = (bf16[32,512]{1,0:T(8,128)(2,1)S(1)}, bf16[32,512]{1,0:T(8,128)(2,1)}, u32[]{:S(2)}) copy-start(bf16[32,512]{1,0:T(8,128)(2,1)} %param.24) | copy-start | bytes 98308
  132.2 32.3 %all-to-all-start.1 = ((f32[128,2,128]{2,1,0:T(2,128)}), f32[128,2,128]{2,1,0:T(2,128)S(1)}, u32[]{:S(2)}, u32[]{:S(2)}) async-start(f32[128,2,128]{2,1,0:T(2,128)} %copy.44), calls=%async_computation.1 | async-start | bytes 262144 | tf_op jit(solution)/shard_map/all_to_all | solution.py:242
  167.2 6.6 %collective-permute-start.10 = (f32[10,4,512]{2,1,0:T(4,128)S(1)}, f32[10,4,512]{2,1,0:T(4,128)S(1)}, u32[]{:S(2)}, u32[]{:S(2)}) collective-permute-start(f32[10,4,512]{2,1,0:T(4,128)S(1)} %get-tuple-element.23), channel_id=1, source_target_pairs={{0,4},{4,8},{8,12},{12,16},{16,20},{20,24},{24,28},{28,32},{32,36}... | collective-permute-start | bytes 245768 | tf_op jit(solution)/shard_map/ppermute | solution.py:28
  171.2 5.8 %collective-permute-start.11 = (f32[10,4,512]{2,1,0:T(4,128)S(1)}, f32[10,4,512]{2,1,0:T(4,128)S(1)}, u32[]{:S(2)}, u32[]{:S(2)}) collective-permute-start(f32[10,4,512]{2,1,0:T(4,128)S(1)} %get-tuple-element.24), channel_id=1, source_target_pairs={{4,0},{8,4},{12,8},{16,12},{20,16},{24,20},{28,24},{32,28},{36,32}... | collective-permute-start | bytes 245768 | tf_op jit(solution)/shard_map/ppermute | solution.py:29
  (14 other events, 124.9 us)

commit v3 on v2

--- a/solution.py
+++ b/solution.py
@@ -71,33 +71,47 @@
     return hi.astype(jnp.bfloat16), mid.astype(jnp.bfloat16), lo.astype(jnp.bfloat16)
 
 
-def sweep_kernel(padded_ref, sel_ref, inflow_ref, rate_ref, alive_ref, out_ref):
+def sweep_kernel(
+    left_ref, energy_ref, right_ref, sel_ref, inflow_ref, rate_ref, alive_ref, out_ref, first_ref, last_ref
+):
     bands = out_ref.shape[0]
-    for t in range(sel_ref.shape[0]):
-        window = padded_ref[:, 128 * t : 128 * t + 384]
+    tiles = sel_ref.shape[0]
+    blocks = (
+        [left_ref[...]]
+        + [energy_ref[:, 128 * t : 128 * t + 128] for t in range(tiles)]
+        + [right_ref[...]]
+    )
+    for t in range(tiles):
+        window = jnp.concatenate(blocks[t : t + 3], axis=1)
         parts = jnp.concatenate(split3(window), axis=0)
         picked = jnp.dot(parts, sel_ref[t], preferred_element_type=jnp.float32)
         gathered = picked[:bands] + picked[bands : 2 * bands] + picked[2 * bands :]
         cols = slice(128 * t, 128 * t + 128)
-        energy = padded_ref[:, 128 * t + 128 : 128 * t + 256]
+        energy = blocks[t + 1]
         arriving = inflow_ref[0, :, cols] * gathered[:, 0:128]
         for k in range(1, NBRS):
             arriving = arriving + inflow_ref[k, :, cols] * gathered[:, 128 * k : 128 * k + 128]
-        out_ref[:, cols] = (energy + arriving - rate_ref[:, cols] * energy) * alive_ref[:, cols]
-
-
-def wave_sweep(padded, sel, inflow, rate, alive):
+        fresh = (energy + arriving - rate_ref[:, cols] * energy) * alive_ref[:, cols]
+        out_ref[:, cols] = fresh
+        if t == 0:
+            first_ref[...] = fresh
+        if t == tiles - 1:
+            last_ref[...] = fresh
+
+
+def wave_sweep(left, energy, right, sel, inflow, rate, alive):
     bands, nodes = rate.shape
     vmem = pl.BlockSpec(memory_space=pltpu.VMEM)
     flops = 2 * 3 * bands * 384 * nodes * NBRS
-    moved = 4 * (padded.size + inflow.size + 2 * rate.size) + 2 * sel.size
+    moved = 4 * (2 * left.size + inflow.size + 3 * rate.size) + 2 * sel.size
+    edge = jax.ShapeDtypeStruct((bands, 128), jnp.float32)
     return pl.pallas_call(
         sweep_kernel,
-        out_shape=jax.ShapeDtypeStruct((bands, nodes), jnp.float32),
-        in_specs=[vmem] * 5,
-        out_specs=vmem,
+        out_shape=(jax.ShapeDtypeStruct((bands, nodes), jnp.float32), edge, edge),
+        in_specs=[vmem] * 7,
+        out_specs=(vmem, vmem, vmem),
         cost_estimate=pl.CostEstimate(flops=flops, bytes_accessed=moved, transcendentals=0),
-    )(padded, sel, inflow, rate, alive)
+    )(left, energy, right, sel, inflow, rate, alive)
 
 
 def selection(local_index):
@@ -108,17 +122,6 @@
     rows = jnp.arange(384, dtype=jnp.int32)
     sel = idx.transpose(1, 0, 2)[:, None, :, :] == rows[None, :, None, None]
     return sel.reshape(tiles, 384, nbrs * 128).astype(jnp.bfloat16)
-
-
-def lev_sum(x):
-    count = lax.axis_size("lev")
-    if count & (count - 1):
-        return lax.psum(x, "lev")
-    step = 1
-    while step < count:
-        x = x + lax.ppermute(x, "lev", [(i, i ^ step) for i in range(count)])
-        step *= 2
-    return x
 
 
 def ocean_step(
@@ -227,14 +230,19 @@
     total_rate = jnp.sum(inflow, axis=0)
     local_index = neighbors - first_node + 128
     sel = selection(local_index)
+    wave_axis = ("sec", "tile")
+    up = [(i, i + 1) for i in range(lax.axis_size(wave_axis) - 1)]
+    down = [(j, i) for i, j in up]
+    first, last = energy[:, :128], energy[:, -128:]
     for sweep in range(WSTEPS):
-        padded = with_halo(energy, ((("sec", "tile"), 1),), 128)
-        energy = wave_sweep(padded, sel, inflow, total_rate, alive_mask)
+        left = lax.ppermute(last, wave_axis, up)
+        right = lax.ppermute(first, wave_axis, down)
+        energy, first, last = wave_sweep(left, energy, right, sel, inflow, total_rate, alive_mask)
     waves_out = energy.astype(jnp.bfloat16)
     coefficient = jnp.stack(
         [band_orbital * jnp.cos(band_angle), band_orbital * jnp.sin(band_angle)]
     )
-    orbital = lev_sum(jnp.dot(coefficient, energy, precision=HIGHEST))
+    orbital = lax.psum(jnp.dot(coefficient, energy, precision=HIGHEST), "lev")
     orbital_blocks = jnp.transpose(orbital.reshape(2, block_count, 64), (1, 0, 2)).reshape(
         block_count, 128
     )

time: 180 us -> 173 us (0.961)
  blocking collectives: 0 us -> 8.85 us
  starting transfers between devices: 68.7 us -> 60.3 us
  other arithmetic: 18.2 us -> 11.8 us
    ppermute x5 -> x1, waiting for transfers between devices: 15.2 us -> 3.12 us  [with_halo(): after = lax.ppermute(first, axis, down)]
    ppermute x2 -> x8, starting transfers between devices: 8.01 us -> 19.2 us  [the longest x4 10.2 us: per_device(): left = lax.ppermute(last, wave_axis, up)]
    ppermute x2 -> x8, waiting for transfers between devices: 1.96 us -> 12.7 us  [the longest x4 12.7 us: per_device(): right = lax.ppermute(first, wave_axis, down)]
    ppermute x5 -> x1, starting transfers between devices: 14.1 us -> 3.94 us  [with_halo(): before = lax.ppermute(last, axis, up)]
    ppermute x5 -> x1, starting transfers between devices: 11.2 us -> 1.92 us  [with_halo(): after = lax.ppermute(first, axis, down)]
    psum x0 -> x1, blocking collectives: none -> 8.85 us  [per_device(): orbital = lax.psum(jnp.dot(coefficient, energy, precision=HIGHEST), 'lev')]
    concatenate x5 -> x1, other arithmetic: 6.55 us -> 0.14 us  [with_halo(): x = jnp.concatenate([before, x, after], axis=dim)]
    slice x5 -> x1, local copies, waits for them, and re-layouts: 2.91 us -> 0.03 us  [with_halo(): last = lax.slice_in_dim(x, length - width, length, axis=dim)]
  transfers between devices with their start and end apart: 14 -> 12, of which waited for: 9 -> 7; matrix products, arithmetic and copies ran while one was open for 3% -> 3% of each run, Pallas kernels for 0% -> 0%
where the time goes in v3:
time: 173 us
  starting transfers between devices  60.3 us (35%)
  waiting for transfers between devices  58.8 us (34%)
  Pallas kernels  18.3 us (11%)
  other arithmetic  11.8 us (7%)
  blocking collectives  8.85 us (5%)
  local copies, waits for them, and re-layouts  8.38 us (5%)
  matrix products  4.73 us (3%)
    all_to_all x1, waiting for transfers between devices, per_device(): lax.all_to_all(send_rows, ('sec', 'tile'), split_axis=0, concat_axis=0, t...  25.8 us
    all_to_all x1, starting transfers between devices, per_device(): lax.all_to_all(send_rows, ('sec', 'tile'), split_axis=0, concat_axis=0, t...  20.4 us
    pallas_call x4, Pallas kernels, wave_sweep(): pl.pallas_call(sweep_kernel, out_shape=(jax.ShapeDtypeStruct((bands, node...  18.3 us
    all_to_all x1, waiting for transfers between devices, per_device(): lax.all_to_all(back_rows, ('sec', 'tile'), split_axis=0, concat_axis=0, t...  17.2 us
    all_to_all x1, starting transfers between devices, per_device(): lax.all_to_all(back_rows, ('sec', 'tile'), split_axis=0, concat_axis=0, t...  14.8 us
    ppermute x4, waiting for transfers between devices, per_device(): right = lax.ppermute(first, wave_axis, down)  12.7 us
    ppermute x4, starting transfers between devices, per_device(): left = lax.ppermute(last, wave_axis, up)  10.2 us
    ppermute x4, starting transfers between devices, per_device(): right = lax.ppermute(first, wave_axis, down)  9.02 us
  transfers between devices with their start and end apart: 12, of which 7 were waited for; matrix products, arithmetic and copies ran while one was open for 3% of the time, Pallas kernels for 0%

profile of v3, /device:TPU:1, one launch (start us, length us, event | category | flops | bytes accessed | tf_op | source)
XLA Modules:
  0.0 172.6 jit_solution(8197794535939311387)
XLA Ops:
  9.0 20.4 %all-to-all-start = ((f32[128,2,257]{2,1,0:T(2,128)}), f32[128,2,257]{2,1,0:T(2,128)S(1)}, u32[]{:S(2)}, u32[]{:S(2)}) async-start(f32[128,2,257]{2,1,0:T(2,128)} %all_to_all.14), calls=%async_computation | async-start | bytes 786432 | tf_op jit(solution)/shard_map/all_to_all | solution.py:215
  31.4 25.8 %all-to-all-done = f32[128,2,257]{2,1,0:T(2,128)S(1)} async-done(((f32[128,2,257]{2,1,0:T(2,128)}), f32[128,2,257]{2,1,0:T(2,128)S(1)}, u32[]{:S(2)}, u32[]{:S(2)}) %all-to-all-start) | async-done | bytes 263200 | tf_op jit(solution)/shard_map/all_to_all | solution.py:215
  58.6 4.4 %collective-permute-start = (f32[192,128]{1,0:T(8,128)S(1)}, f32[192,128]{1,0:T(8,128)S(1)}, u32[]{:S(2)}, u32[]{:S(2)}) collective-permute-start(f32[192,128]{1,0:T(8,128)S(1)} %get-tuple-element.48), channel_id=1, source_target_pairs={{0,4},{4,8},{8,12},{12,16},{16,20},{20,24},{24,28},{28,32},{32,36}... | collective-permute-start | bytes 294920 | tf_op jit(solution)/shard_map/ppermute | solution.py:238
  63.0 1.9 %collective-permute-start.1 = (f32[192,128]{1,0:T(8,128)S(1)}, f32[192,128]{1,0:T(8,128)S(1)}, u32[]{:S(2)}, u32[]{:S(2)}) collective-permute-start(f32[192,128]{1,0:T(8,128)S(1)} %get-tuple-element.47), channel_id=1, source_target_pairs={{4,0},{8,4},{12,8},{16,12},{20,16},{24,20},{28,24},{32,28},{36,32}... | collective-permute-start | bytes 294920 | tf_op jit(solution)/shard_map/ppermute | solution.py:239
  64.9 2.4 %fusion.43 = (f32[192,512]{1,0:T(8,128)}, f32[4,192,512]{2,1,0:T(8,128)}) fusion(f32[4,512]{1,0:T(4,128)S(1)} %get-tuple-element.58, f32[192]{0:T(256)S(1)} %get-tuple-element.64, f32[4,512]{1,0:T(4,128)S(1)} %get-tuple-element.57, f32[192]{0:T(256)S(1)} %get-tuple-element.63, f32[192,512]{1,0:T(8,128)S(1)} %get-tuple-element.59), kind=kLoop, calls=%fused_computation.113 | loop fusion | flops 2654208 | bytes 2377216 | tf_op jit(solution)/shard_map/reduce_sum | solution.py:230
  69.6 4.5 %shard_map.221 = (f32[192,512]{1,0:T(8,128)}, f32[192,128]{1,0:T(8,128)}, f32[192,128]{1,0:T(8,128)}) custom-call(f32[192,128]{1,0:T(8,128)} %copy-done.10, f32[192,512]{1,0:T(8,128)} %copy-done.1, f32[192,128]{1,0:T(8,128)} %copy-done.11, bf16[4,384,512]{2,1,0:T(8,128)(2,1)} %fusion.sel_ref, f32[4,192,512]{2,1,0:T(8,128)} %get-tuple-element.46.inflow_ref, ...), custom_call_target="tpu_custom_call" | custom-call | flops 905969664 | bytes 4521984 | tf_op jit(solution)/shard_map/pallas_call | solution.py:108
  74.1 2.0 %collective-permute-start.2 = (f32[192,128]{1,0:T(8,128)}, f32[192,128]{1,0:T(8,128)S(1)}, u32[]{:S(2)}, u32[]{:S(2)}) collective-permute-start(f32[192,128]{1,0:T(8,128)} %get-tuple-element.12), channel_id=1, source_target_pairs={{0,4},{4,8},{8,12},{12,16},{16,20},{20,24},{24,28},{28,32},{32,36}... | collective-permute-start | bytes 294920 | tf_op jit(solution)/shard_map/ppermute | solution.py:238
  76.1 2.3 %collective-permute-start.3 = (f32[192,128]{1,0:T(8,128)}, f32[192,128]{1,0:T(8,128)S(1)}, u32[]{:S(2)}, u32[]{:S(2)}) collective-permute-start(f32[192,128]{1,0:T(8,128)} %get-tuple-element.14), channel_id=1, source_target_pairs={{4,0},{8,4},{12,8},{16,12},{20,16},{24,20},{28,24},{32,28},{36,32}... | collective-permute-start | bytes 294920 | tf_op jit(solution)/shard_map/ppermute | solution.py:239
  78.5 3.8 %collective-permute-done.3.right_ref = f32[192,128]{1,0:T(8,128)S(1)} collective-permute-done((f32[192,128]{1,0:T(8,128)}, f32[192,128]{1,0:T(8,128)S(1)}, u32[]{:S(2)}, u32[]{:S(2)}) %collective-permute-start.3) | collective-permute-done | bytes 98336 | tf_op jit(solution)/shard_map/ppermute | solution.py:239
  82.9 4.6 %shard_map.222 = (f32[192,512]{1,0:T(8,128)}, f32[192,128]{1,0:T(8,128)}, f32[192,128]{1,0:T(8,128)}) custom-call(f32[192,128]{1,0:T(8,128)} %copy-done.12, f32[192,512]{1,0:T(8,128)} %get-tuple-element.13.energy_ref, f32[192,128]{1,0:T(8,128)} %copy-done.14, bf16[4,384,512]{2,1,0:T(8,128)(2,1)} %fusion.sel_ref, ...), custom_call_target="tpu_custom_call" | custom-call | flops 905969664 | bytes 4521984 | tf_op jit(solution)/shard_map/pallas_call | solution.py:108
  87.5 1.9 %collective-permute-start.4 = (f32[192,128]{1,0:T(8,128)}, f32[192,128]{1,0:T(8,128)S(1)}, u32[]{:S(2)}, u32[]{:S(2)}) collective-permute-start(f32[192,128]{1,0:T(8,128)} %get-tuple-element.15), channel_id=1, source_target_pairs={{0,4},{4,8},{8,12},{12,16},{16,20},{20,24},{24,28},{28,32},{32,36}... | collective-permute-start | bytes 294920 | tf_op jit(solution)/shard_map/ppermute | solution.py:238
  89.4 2.4 %collective-permute-start.5 = (f32[192,128]{1,0:T(8,128)}, f32[192,128]{1,0:T(8,128)S(1)}, u32[]{:S(2)}, u32[]{:S(2)}) collective-permute-start(f32[192,128]{1,0:T(8,128)} %get-tuple-element.17), channel_id=1, source_target_pairs={{4,0},{8,4},{12,8},{16,12},{20,16},{24,20},{28,24},{32,28},{36,32}... | collective-permute-start | bytes 294920 | tf_op jit(solution)/shard_map/ppermute | solution.py:239
  91.8 3.7 %collective-permute-done.5.right_ref = f32[192,128]{1,0:T(8,128)S(1)} collective-permute-done((f32[192,128]{1,0:T(8,128)}, f32[192,128]{1,0:T(8,128)S(1)}, u32[]{:S(2)}, u32[]{:S(2)}) %collective-permute-start.5) | collective-permute-done | bytes 98336 | tf_op jit(solution)/shard_map/ppermute | solution.py:239
  96.2 4.6 %shard_map.223 = (f32[192,512]{1,0:T(8,128)}, f32[192,128]{1,0:T(8,128)}, f32[192,128]{1,0:T(8,128)}) custom-call(f32[192,128]{1,0:T(8,128)} %copy-done.13, f32[192,512]{1,0:T(8,128)} %get-tuple-element.16.energy_ref, f32[192,128]{1,0:T(8,128)} %copy-done.15, bf16[4,384,512]{2,1,0:T(8,128)(2,1)} %fusion.sel_ref, ...), custom_call_target="tpu_custom_call" | custom-call | flops 905969664 | bytes 4521984 | tf_op jit(solution)/shard_map/pallas_call | solution.py:108
  100.8 1.9 %collective-permute-start.6 = (f32[192,128]{1,0:T(8,128)}, f32[192,128]{1,0:T(8,128)S(1)}, u32[]{:S(2)}, u32[]{:S(2)}) collective-permute-start(f32[192,128]{1,0:T(8,128)} %get-tuple-element.18), channel_id=1, source_target_pairs={{0,4},{4,8},{8,12},{12,16},{16,20},{20,24},{24,28},{28,32},{32,36}... | collective-permute-start | bytes 294920 | tf_op jit(solution)/shard_map/ppermute | solution.py:238
  102.7 2.4 %collective-permute-start.7 = (f32[192,128]{1,0:T(8,128)}, f32[192,128]{1,0:T(8,128)S(1)}, u32[]{:S(2)}, u32[]{:S(2)}) collective-permute-start(f32[192,128]{1,0:T(8,128)} %get-tuple-element.20), channel_id=1, source_target_pairs={{4,0},{8,4},{12,8},{16,12},{20,16},{24,20},{28,24},{32,28},{36,32}... | collective-permute-start | bytes 294920 | tf_op jit(solution)/shard_map/ppermute | solution.py:239
  105.3 3.5 %collective-permute-done.7.right_ref = f32[192,128]{1,0:T(8,128)S(1)} collective-permute-done((f32[192,128]{1,0:T(8,128)}, f32[192,128]{1,0:T(8,128)S(1)}, u32[]{:S(2)}, u32[]{:S(2)}) %collective-permute-start.7) | collective-permute-done | bytes 98336 | tf_op jit(solution)/shard_map/ppermute | solution.py:239
  109.5 4.6 %shard_map.224 = (f32[192,512]{1,0:T(8,128)}, f32[192,128]{1,0:T(8,128)}, f32[192,128]{1,0:T(8,128)}) custom-call(f32[192,128]{1,0:T(8,128)} %copy-done.8, f32[192,512]{1,0:T(8,128)} %get-tuple-element.19.energy_ref, f32[192,128]{1,0:T(8,128)} %copy-done.9, bf16[4,384,512]{2,1,0:T(8,128)(2,1)} %fusion.sel_ref, f32[4,192,512]{2,1,0:T(8,128)} %get-tuple-element.46.inflow_ref, ...), custom_call_target="tpu_custom_call" | custom-call | flops 905969664 | bytes 4521984 | tf_op jit(solution)/shard_map/pallas_call | solution.py:108
  115.6 8.8 %psum.7 = f32[8,128]{1,0:T(8,128)S(1)} all-reduce(f32[8,128]{1,0:T(8,128)S(1)} %reshape.181), channel_id=1, replica_groups=mesh['sec'=4,'tile'=32,'lev'=4] {'lev'}, use_global_device_ids=true, to_apply=%region_4.5 | all-reduce | flops 1024 | bytes 8192 | tf_op jit(solution)/shard_map/psum | solution.py:245
  125.5 14.8 %all-to-all-start.1 = ((f32[128,2,128]{2,1,0:T(2,128)}), f32[128,2,128]{2,1,0:T(2,128)S(1)}, u32[]{:S(2)}, u32[]{:S(2)}) async-start(f32[128,2,128]{2,1,0:T(2,128)} %copy.44), calls=%async_computation.1 | async-start | bytes 262144 | tf_op jit(solution)/shard_map/all_to_all | solution.py:250
  140.3 17.2 %all-to-all-done.1 = f32[128,2,128]{2,1,0:T(2,128)S(1)} async-done(((f32[128,2,128]{2,1,0:T(2,128)}), f32[128,2,128]{2,1,0:T(2,128)S(1)}, u32[]{:S(2)}, u32[]{:S(2)}) %all-to-all-start.1) | async-done | bytes 131104 | tf_op jit(solution)/shard_map/all_to_all | solution.py:250
  160.3 3.9 %collective-permute-start.8 = (f32[10,4,512]{2,1,0:T(4,128)S(1)}, f32[10,4,512]{2,1,0:T(4,128)S(1)}, u32[]{:S(2)}, u32[]{:S(2)}) collective-permute-start(f32[10,4,512]{2,1,0:T(4,128)S(1)} %get-tuple-element.43), channel_id=1, source_target_pairs={{0,4},{4,8},{8,12},{12,16},{16,20},{20,24},{24,28},{28,32},{32,36}... | collective-permute-start | bytes 245768 | tf_op jit(solution)/shard_map/ppermute | solution.py:28
  164.2 1.9 %collective-permute-start.9 = (f32[10,4,512]{2,1,0:T(4,128)S(1)}, f32[10,4,512]{2,1,0:T(4,128)S(1)}, u32[]{:S(2)}, u32[]{:S(2)}) collective-permute-start(f32[10,4,512]{2,1,0:T(4,128)S(1)} %get-tuple-element.44), channel_id=1, source_target_pairs={{4,0},{8,4},{12,8},{16,12},{20,16},{24,20},{28,24},{32,28},{36,32}... | collective-permute-start | bytes 245768 | tf_op jit(solution)/shard_map/ppermute | solution.py:29
  166.9 3.1 %collective-permute-done.9 = f32[10,4,512]{2,1,0:T(4,128)S(1)} collective-permute-done((f32[10,4,512]{2,1,0:T(4,128)S(1)}, f32[10,4,512]{2,1,0:T(4,128)S(1)}, u32[]{:S(2)}, u32[]{:S(2)}) %collective-permute-start.9) | collective-permute-done | bytes 81952 | tf_op jit(solution)/shard_map/ppermute | solution.py:29
  (157 shorter events, 24.2 us)
Async XLA Ops:
  4.7 24.7 %copy-start.24 = (s32[512]{0:T(512)S(1)}, s32[512]{0:T(512)}, u32[]{:S(2)}) copy-start(s32[512]{0:T(512)} %param.39) | copy-start | bytes 6148
  4.7 24.7 %copy-start.22 = (s32[4,512]{1,0:T(4,128)S(1)}, s32[4,512]{1,0:T(4,128)}, u32[]{:S(2)}) copy-start(s32[4,512]{1,0:T(4,128)} %param.37) | copy-start | bytes 24580
  6.5 23.0 %copy-start.25 = (f32[192]{0:T(256)S(1)}, f32[192]{0:T(256)}, u32[]{:S(2)}) copy-start(f32[192]{0:T(256)} %param.33) | copy-start | bytes 2308
  6.5 23.0 %copy-start.26 = (f32[192]{0:T(256)S(1)}, f32[192]{0:T(256)}, u32[]{:S(2)}) copy-start(f32[192]{0:T(256)} %param.34) | copy-start | bytes 2308
  6.5 23.2 %copy-start.21 = (f32[4,512]{1,0:T(4,128)S(1)}, f32[4,512]{1,0:T(4,128)}, u32[]{:S(2)}) copy-start(f32[4,512]{1,0:T(4,128)} %param.38) | copy-start | bytes 24580
  9.0 48.2 %all-to-all-start = ((f32[128,2,257]{2,1,0:T(2,128)}), f32[128,2,257]{2,1,0:T(2,128)S(1)}, u32[]{:S(2)}, u32[]{:S(2)}) async-start(f32[128,2,257]{2,1,0:T(2,128)} %all_to_all.14), calls=%async_computation | async-start | bytes 786432 | tf_op jit(solution)/shard_map/all_to_all | solution.py:215
  29.4 28.9 %copy-start.5 = (bf16[192,512]{1,0:T(8,128)(2,1)S(1)}, bf16[192,512]{1,0:T(8,128)(2,1)}, u32[]{:S(2)}) copy-start(bf16[192,512]{1,0:T(8,128)(2,1)} %param.32) | copy-start | bytes 589828
  29.4 28.9 %copy-start.28 = (f32[192]{0:T(256)S(1)}, f32[192]{0:T(256)}, u32[]{:S(2)}) copy-start(f32[192]{0:T(256)} %param.35) | copy-start | bytes 2308
  29.4 29.1 %copy-start.16 = (f32[512]{0:T(512)}, f32[512]{0:T(512)S(1)}, u32[]{:S(2)}) copy-start(f32[512]{0:T(512)S(1)} %convert_element_type.87) | copy-start | bytes 6148
  58.6 8.7 %collective-permute-start = (f32[192,128]{1,0:T(8,128)S(1)}, f32[192,128]{1,0:T(8,128)S(1)}, u32[]{:S(2)}, u32[]{:S(2)}) collective-permute-start(f32[192,128]{1,0:T(8,128)S(1)} %get-tuple-element.48), channel_id=1, source_target_pairs={{0,4},{4,8},{8,12},{12,16},{16,20},{20,24},{24,28},{28,32},{32,36}... | collective-permute-start | bytes 294920 | tf_op jit(solution)/shard_map/ppermute | solution.py:238
  63.0 5.9 %collective-permute-start.1 = (f32[192,128]{1,0:T(8,128)S(1)}, f32[192,128]{1,0:T(8,128)S(1)}, u32[]{:S(2)}, u32[]{:S(2)}) collective-permute-start(f32[192,128]{1,0:T(8,128)S(1)} %get-tuple-element.47), channel_id=1, source_target_pairs={{4,0},{8,4},{12,8},{16,12},{20,16},{24,20},{28,24},{32,28},{36,32}... | collective-permute-start | bytes 294920 | tf_op jit(solution)/shard_map/ppermute | solution.py:239
  74.1 4.3 %collective-permute-start.2 = (f32[192,128]{1,0:T(8,128)}, f32[192,128]{1,0:T(8,128)S(1)}, u32[]{:S(2)}, u32[]{:S(2)}) collective-permute-start(f32[192,128]{1,0:T(8,128)} %get-tuple-element.12), channel_id=1, source_target_pairs={{0,4},{4,8},{8,12},{12,16},{16,20},{20,24},{24,28},{28,32},{32,36}... | collective-permute-start | bytes 294920 | tf_op jit(solution)/shard_map/ppermute | solution.py:238
  76.1 6.1 %collective-permute-start.3 = (f32[192,128]{1,0:T(8,128)}, f32[192,128]{1,0:T(8,128)S(1)}, u32[]{:S(2)}, u32[]{:S(2)}) collective-permute-start(f32[192,128]{1,0:T(8,128)} %get-tuple-element.14), channel_id=1, source_target_pairs={{4,0},{8,4},{12,8},{16,12},{20,16},{24,20},{28,24},{32,28},{36,32}... | collective-permute-start | bytes 294920 | tf_op jit(solution)/shard_map/ppermute | solution.py:239
  87.5 4.3 %collective-permute-start.4 = (f32[192,128]{1,0:T(8,128)}, f32[192,128]{1,0:T(8,128)S(1)}, u32[]{:S(2)}, u32[]{:S(2)}) collective-permute-start(f32[192,128]{1,0:T(8,128)} %get-tuple-element.15), channel_id=1, source_target_pairs={{0,4},{4,8},{8,12},{12,16},{16,20},{20,24},{24,28},{28,32},{32,36}... | collective-permute-start | bytes 294920 | tf_op jit(solution)/shard_map/ppermute | solution.py:238
  89.4 6.1 %collective-permute-start.5 = (f32[192,128]{1,0:T(8,128)}, f32[192,128]{1,0:T(8,128)S(1)}, u32[]{:S(2)}, u32[]{:S(2)}) collective-permute-start(f32[192,128]{1,0:T(8,128)} %get-tuple-element.17), channel_id=1, source_target_pairs={{4,0},{8,4},{12,8},{16,12},{20,16},{24,20},{28,24},{32,28},{36,32}... | collective-permute-start | bytes 294920 | tf_op jit(solution)/shard_map/ppermute | solution.py:239
  100.8 4.6 %collective-permute-start.6 = (f32[192,128]{1,0:T(8,128)}, f32[192,128]{1,0:T(8,128)S(1)}, u32[]{:S(2)}, u32[]{:S(2)}) collective-permute-start(f32[192,128]{1,0:T(8,128)} %get-tuple-element.18), channel_id=1, source_target_pairs={{0,4},{4,8},{8,12},{12,16},{16,20},{20,24},{24,28},{28,32},{32,36}... | collective-permute-start | bytes 294920 | tf_op jit(solution)/shard_map/ppermute | solution.py:238
  102.7 6.1 %collective-permute-start.7 = (f32[192,128]{1,0:T(8,128)}, f32[192,128]{1,0:T(8,128)S(1)}, u32[]{:S(2)}, u32[]{:S(2)}) collective-permute-start(f32[192,128]{1,0:T(8,128)} %get-tuple-element.20), channel_id=1, source_target_pairs={{4,0},{8,4},{12,8},{16,12},{20,16},{24,20},{28,24},{32,28},{36,32}... | collective-permute-start | bytes 294920 | tf_op jit(solution)/shard_map/ppermute | solution.py:239
  109.5 30.8 %copy-start.7 = (f32[2,32,512]{2,1,0:T(8,128)S(1)}, f32[2,32,512]{2,1,0:T(8,128)}, u32[]{:S(2)}) copy-start(f32[2,32,512]{2,1,0:T(8,128)} %param.22) | copy-start | bytes 393220
  114.1 45.4 %copy-start.29 = (s32[64]{0:T(128)S(1)}, s32[64]{0:T(128)}, u32[]{:S(2)}) copy-start(s32[64]{0:T(128)} %param.42) | copy-start | bytes 772
  125.5 34.5 %copy-start.3 = (bf16[32,512]{1,0:T(8,128)(2,1)S(1)}, bf16[32,512]{1,0:T(8,128)(2,1)}, u32[]{:S(2)}) copy-start(bf16[32,512]{1,0:T(8,128)(2,1)} %param.23) | copy-start | bytes 98308
  125.5 34.5 %copy-start.4 = (bf16[32,512]{1,0:T(8,128)(2,1)S(1)}, bf16[32,512]{1,0:T(8,128)(2,1)}, u32[]{:S(2)}) copy-start(bf16[32,512]{1,0:T(8,128)(2,1)} %param.24) | copy-start | bytes 98308
  125.5 32.1 %all-to-all-start.1 = ((f32[128,2,128]{2,1,0:T(2,128)}), f32[128,2,128]{2,1,0:T(2,128)S(1)}, u32[]{:S(2)}, u32[]{:S(2)}) async-start(f32[128,2,128]{2,1,0:T(2,128)} %copy.44), calls=%async_computation.1 | async-start | bytes 262144 | tf_op jit(solution)/shard_map/all_to_all | solution.py:250
  160.3 6.6 %collective-permute-start.8 = (f32[10,4,512]{2,1,0:T(4,128)S(1)}, f32[10,4,512]{2,1,0:T(4,128)S(1)}, u32[]{:S(2)}, u32[]{:S(2)}) collective-permute-start(f32[10,4,512]{2,1,0:T(4,128)S(1)} %get-tuple-element.43), channel_id=1, source_target_pairs={{0,4},{4,8},{8,12},{12,16},{16,20},{20,24},{24,28},{28,32},{32,36}... | collective-permute-start | bytes 245768 | tf_op jit(solution)/shard_map/ppermute | solution.py:28
  164.2 5.8 %collective-permute-start.9 = (f32[10,4,512]{2,1,0:T(4,128)S(1)}, f32[10,4,512]{2,1,0:T(4,128)S(1)}, u32[]{:S(2)}, u32[]{:S(2)}) collective-permute-start(f32[10,4,512]{2,1,0:T(4,128)S(1)} %get-tuple-element.44), channel_id=1, source_target_pairs={{4,0},{8,4},{12,8},{16,12},{20,16},{24,20},{28,24},{32,28},{36,32}... | collective-permute-start | bytes 245768 | tf_op jit(solution)/shard_map/ppermute | solution.py:29
  (21 other events, 103.5 us)

commit v4 on v3

--- a/solution.py
+++ b/solution.py
@@ -81,9 +81,12 @@
         + [energy_ref[:, 128 * t : 128 * t + 128] for t in range(tiles)]
         + [right_ref[...]]
     )
+    pieces = [split3(block) for block in blocks]
     for t in range(tiles):
-        window = jnp.concatenate(blocks[t : t + 3], axis=1)
-        parts = jnp.concatenate(split3(window), axis=0)
+        parts = jnp.concatenate(
+            [jnp.concatenate([pieces[t + b][p] for b in range(3)], axis=1) for p in range(3)],
+            axis=0,
+        )
         picked = jnp.dot(parts, sel_ref[t], preferred_element_type=jnp.float32)
         gathered = picked[:bands] + picked[bands : 2 * bands] + picked[2 * bands :]
         cols = slice(128 * t, 128 * t + 128)

time: 173 us -> 173 us (level)
  no operation moved by 1% of the time
where the time goes in v4:
time: 173 us
  starting transfers between devices  60.3 us (35%)
  waiting for transfers between devices  58.9 us (34%)
  Pallas kernels  18.2 us (11%)
  other arithmetic  11.8 us (7%)
  blocking collectives  8.85 us (5%)
  local copies, waits for them, and re-layouts  8.38 us (5%)
  matrix products  4.73 us (3%)
    all_to_all x1, waiting for transfers between devices, per_device(): lax.all_to_all(send_rows, ('sec', 'tile'), split_axis=0, concat_axis=0, t...  25.8 us
    all_to_all x1, starting transfers between devices, per_device(): lax.all_to_all(send_rows, ('sec', 'tile'), split_axis=0, concat_axis=0, t...  20.4 us
    pallas_call x4, Pallas kernels, wave_sweep(): pl.pallas_call(sweep_kernel, out_shape=(jax.ShapeDtypeStruct((bands, node...  18.2 us
    all_to_all x1, waiting for transfers between devices, per_device(): lax.all_to_all(back_rows, ('sec', 'tile'), split_axis=0, concat_axis=0, t...  17.2 us
    all_to_all x1, starting transfers between devices, per_device(): lax.all_to_all(back_rows, ('sec', 'tile'), split_axis=0, concat_axis=0, t...  14.8 us
    ppermute x4, waiting for transfers between devices, per_device(): right = lax.ppermute(first, wave_axis, down)  12.7 us
    ppermute x4, starting transfers between devices, per_device(): left = lax.ppermute(last, wave_axis, up)  10.2 us
    ppermute x4, starting transfers between devices, per_device(): right = lax.ppermute(first, wave_axis, down)  9.01 us
  transfers between devices with their start and end apart: 12, of which 7 were waited for; matrix products, arithmetic and copies ran while one was open for 3% of the time, Pallas kernels for 0%

profile of v4, /device:TPU:1, one launch (start us, length us, event | category | flops | bytes accessed | tf_op | source)
XLA Modules:
  0.0 172.6 jit_solution(8197794535939311387)
XLA Ops:
  9.0 20.4 %all-to-all-start = ((f32[128,2,257]{2,1,0:T(2,128)}), f32[128,2,257]{2,1,0:T(2,128)S(1)}, u32[]{:S(2)}, u32[]{:S(2)}) async-start(f32[128,2,257]{2,1,0:T(2,128)} %all_to_all.14), calls=%async_computation | async-start | bytes 786432 | tf_op jit(solution)/shard_map/all_to_all | solution.py:218
  31.4 25.8 %all-to-all-done = f32[128,2,257]{2,1,0:T(2,128)S(1)} async-done(((f32[128,2,257]{2,1,0:T(2,128)}), f32[128,2,257]{2,1,0:T(2,128)S(1)}, u32[]{:S(2)}, u32[]{:S(2)}) %all-to-all-start) | async-done | bytes 263200 | tf_op jit(solution)/shard_map/all_to_all | solution.py:218
  58.6 4.4 %collective-permute-start = (f32[192,128]{1,0:T(8,128)S(1)}, f32[192,128]{1,0:T(8,128)S(1)}, u32[]{:S(2)}, u32[]{:S(2)}) collective-permute-start(f32[192,128]{1,0:T(8,128)S(1)} %get-tuple-element.48), channel_id=1, source_target_pairs={{0,4},{4,8},{8,12},{12,16},{16,20},{20,24},{24,28},{28,32},{32,36}... | collective-permute-start | bytes 294920 | tf_op jit(solution)/shard_map/ppermute | solution.py:241
  63.0 1.9 %collective-permute-start.1 = (f32[192,128]{1,0:T(8,128)S(1)}, f32[192,128]{1,0:T(8,128)S(1)}, u32[]{:S(2)}, u32[]{:S(2)}) collective-permute-start(f32[192,128]{1,0:T(8,128)S(1)} %get-tuple-element.47), channel_id=1, source_target_pairs={{4,0},{8,4},{12,8},{16,12},{20,16},{24,20},{28,24},{32,28},{36,32}... | collective-permute-start | bytes 294920 | tf_op jit(solution)/shard_map/ppermute | solution.py:242
  64.9 2.4 %fusion.43 = (f32[192,512]{1,0:T(8,128)}, f32[4,192,512]{2,1,0:T(8,128)}) fusion(f32[4,512]{1,0:T(4,128)S(1)} %get-tuple-element.58, f32[192]{0:T(256)S(1)} %get-tuple-element.64, f32[4,512]{1,0:T(4,128)S(1)} %get-tuple-element.57, f32[192]{0:T(256)S(1)} %get-tuple-element.63, f32[192,512]{1,0:T(8,128)S(1)} %get-tuple-element.59), kind=kLoop, calls=%fused_computation.113 | loop fusion | flops 2654208 | bytes 2377216 | tf_op jit(solution)/shard_map/reduce_sum | solution.py:233
  69.6 4.5 %shard_map.221 = (f32[192,512]{1,0:T(8,128)}, f32[192,128]{1,0:T(8,128)}, f32[192,128]{1,0:T(8,128)}) custom-call(f32[192,128]{1,0:T(8,128)} %copy-done.10, f32[192,512]{1,0:T(8,128)} %copy-done.1, f32[192,128]{1,0:T(8,128)} %copy-done.11, bf16[4,384,512]{2,1,0:T(8,128)(2,1)} %fusion.sel_ref, f32[4,192,512]{2,1,0:T(8,128)} %get-tuple-element.46.inflow_ref, ...), custom_call_target="tpu_custom_call" | custom-call | flops 905969664 | bytes 4521984 | tf_op jit(solution)/shard_map/pallas_call | solution.py:111
  74.1 2.0 %collective-permute-start.2 = (f32[192,128]{1,0:T(8,128)}, f32[192,128]{1,0:T(8,128)S(1)}, u32[]{:S(2)}, u32[]{:S(2)}) collective-permute-start(f32[192,128]{1,0:T(8,128)} %get-tuple-element.12), channel_id=1, source_target_pairs={{0,4},{4,8},{8,12},{12,16},{16,20},{20,24},{24,28},{28,32},{32,36}... | collective-permute-start | bytes 294920 | tf_op jit(solution)/shard_map/ppermute | solution.py:241
  76.1 2.3 %collective-permute-start.3 = (f32[192,128]{1,0:T(8,128)}, f32[192,128]{1,0:T(8,128)S(1)}, u32[]{:S(2)}, u32[]{:S(2)}) collective-permute-start(f32[192,128]{1,0:T(8,128)} %get-tuple-element.14), channel_id=1, source_target_pairs={{4,0},{8,4},{12,8},{16,12},{20,16},{24,20},{28,24},{32,28},{36,32}... | collective-permute-start | bytes 294920 | tf_op jit(solution)/shard_map/ppermute | solution.py:242
  78.5 3.8 %collective-permute-done.3.right_ref = f32[192,128]{1,0:T(8,128)S(1)} collective-permute-done((f32[192,128]{1,0:T(8,128)}, f32[192,128]{1,0:T(8,128)S(1)}, u32[]{:S(2)}, u32[]{:S(2)}) %collective-permute-start.3) | collective-permute-done | bytes 98336 | tf_op jit(solution)/shard_map/ppermute | solution.py:242
  82.9 4.6 %shard_map.222 = (f32[192,512]{1,0:T(8,128)}, f32[192,128]{1,0:T(8,128)}, f32[192,128]{1,0:T(8,128)}) custom-call(f32[192,128]{1,0:T(8,128)} %copy-done.12, f32[192,512]{1,0:T(8,128)} %get-tuple-element.13.energy_ref, f32[192,128]{1,0:T(8,128)} %copy-done.14, bf16[4,384,512]{2,1,0:T(8,128)(2,1)} %fusion.sel_ref, ...), custom_call_target="tpu_custom_call" | custom-call | flops 905969664 | bytes 4521984 | tf_op jit(solution)/shard_map/pallas_call | solution.py:111
  87.5 1.9 %collective-permute-start.4 = (f32[192,128]{1,0:T(8,128)}, f32[192,128]{1,0:T(8,128)S(1)}, u32[]{:S(2)}, u32[]{:S(2)}) collective-permute-start(f32[192,128]{1,0:T(8,128)} %get-tuple-element.15), channel_id=1, source_target_pairs={{0,4},{4,8},{8,12},{12,16},{16,20},{20,24},{24,28},{28,32},{32,36}... | collective-permute-start | bytes 294920 | tf_op jit(solution)/shard_map/ppermute | solution.py:241
  89.4 2.4 %collective-permute-start.5 = (f32[192,128]{1,0:T(8,128)}, f32[192,128]{1,0:T(8,128)S(1)}, u32[]{:S(2)}, u32[]{:S(2)}) collective-permute-start(f32[192,128]{1,0:T(8,128)} %get-tuple-element.17), channel_id=1, source_target_pairs={{4,0},{8,4},{12,8},{16,12},{20,16},{24,20},{28,24},{32,28},{36,32}... | collective-permute-start | bytes 294920 | tf_op jit(solution)/shard_map/ppermute | solution.py:242
  91.8 3.7 %collective-permute-done.5.right_ref = f32[192,128]{1,0:T(8,128)S(1)} collective-permute-done((f32[192,128]{1,0:T(8,128)}, f32[192,128]{1,0:T(8,128)S(1)}, u32[]{:S(2)}, u32[]{:S(2)}) %collective-permute-start.5) | collective-permute-done | bytes 98336 | tf_op jit(solution)/shard_map/ppermute | solution.py:242
  96.2 4.6 %shard_map.223 = (f32[192,512]{1,0:T(8,128)}, f32[192,128]{1,0:T(8,128)}, f32[192,128]{1,0:T(8,128)}) custom-call(f32[192,128]{1,0:T(8,128)} %copy-done.13, f32[192,512]{1,0:T(8,128)} %get-tuple-element.16.energy_ref, f32[192,128]{1,0:T(8,128)} %copy-done.15, bf16[4,384,512]{2,1,0:T(8,128)(2,1)} %fusion.sel_ref, ...), custom_call_target="tpu_custom_call" | custom-call | flops 905969664 | bytes 4521984 | tf_op jit(solution)/shard_map/pallas_call | solution.py:111
  100.8 1.9 %collective-permute-start.6 = (f32[192,128]{1,0:T(8,128)}, f32[192,128]{1,0:T(8,128)S(1)}, u32[]{:S(2)}, u32[]{:S(2)}) collective-permute-start(f32[192,128]{1,0:T(8,128)} %get-tuple-element.18), channel_id=1, source_target_pairs={{0,4},{4,8},{8,12},{12,16},{16,20},{20,24},{24,28},{28,32},{32,36}... | collective-permute-start | bytes 294920 | tf_op jit(solution)/shard_map/ppermute | solution.py:241
  102.7 2.4 %collective-permute-start.7 = (f32[192,128]{1,0:T(8,128)}, f32[192,128]{1,0:T(8,128)S(1)}, u32[]{:S(2)}, u32[]{:S(2)}) collective-permute-start(f32[192,128]{1,0:T(8,128)} %get-tuple-element.20), channel_id=1, source_target_pairs={{4,0},{8,4},{12,8},{16,12},{20,16},{24,20},{28,24},{32,28},{36,32}... | collective-permute-start | bytes 294920 | tf_op jit(solution)/shard_map/ppermute | solution.py:242
  105.3 3.5 %collective-permute-done.7.right_ref = f32[192,128]{1,0:T(8,128)S(1)} collective-permute-done((f32[192,128]{1,0:T(8,128)}, f32[192,128]{1,0:T(8,128)S(1)}, u32[]{:S(2)}, u32[]{:S(2)}) %collective-permute-start.7) | collective-permute-done | bytes 98336 | tf_op jit(solution)/shard_map/ppermute | solution.py:242
  109.5 4.6 %shard_map.224 = (f32[192,512]{1,0:T(8,128)}, f32[192,128]{1,0:T(8,128)}, f32[192,128]{1,0:T(8,128)}) custom-call(f32[192,128]{1,0:T(8,128)} %copy-done.8, f32[192,512]{1,0:T(8,128)} %get-tuple-element.19.energy_ref, f32[192,128]{1,0:T(8,128)} %copy-done.9, bf16[4,384,512]{2,1,0:T(8,128)(2,1)} %fusion.sel_ref, f32[4,192,512]{2,1,0:T(8,128)} %get-tuple-element.46.inflow_ref, ...), custom_call_target="tpu_custom_call" | custom-call | flops 905969664 | bytes 4521984 | tf_op jit(solution)/shard_map/pallas_call | solution.py:111
  115.6 8.8 %psum.7 = f32[8,128]{1,0:T(8,128)S(1)} all-reduce(f32[8,128]{1,0:T(8,128)S(1)} %reshape.181), channel_id=1, replica_groups=mesh['sec'=4,'tile'=32,'lev'=4] {'lev'}, use_global_device_ids=true, to_apply=%region_4.5 | all-reduce | flops 1024 | bytes 8192 | tf_op jit(solution)/shard_map/psum | solution.py:248
  125.5 14.8 %all-to-all-start.1 = ((f32[128,2,128]{2,1,0:T(2,128)}), f32[128,2,128]{2,1,0:T(2,128)S(1)}, u32[]{:S(2)}, u32[]{:S(2)}) async-start(f32[128,2,128]{2,1,0:T(2,128)} %copy.44), calls=%async_computation.1 | async-start | bytes 262144 | tf_op jit(solution)/shard_map/all_to_all | solution.py:253
  140.3 17.2 %all-to-all-done.1 = f32[128,2,128]{2,1,0:T(2,128)S(1)} async-done(((f32[128,2,128]{2,1,0:T(2,128)}), f32[128,2,128]{2,1,0:T(2,128)S(1)}, u32[]{:S(2)}, u32[]{:S(2)}) %all-to-all-start.1) | async-done | bytes 131104 | tf_op jit(solution)/shard_map/all_to_all | solution.py:253
  160.3 3.9 %collective-permute-start.8 = (f32[10,4,512]{2,1,0:T(4,128)S(1)}, f32[10,4,512]{2,1,0:T(4,128)S(1)}, u32[]{:S(2)}, u32[]{:S(2)}) collective-permute-start(f32[10,4,512]{2,1,0:T(4,128)S(1)} %get-tuple-element.43), channel_id=1, source_target_pairs={{0,4},{4,8},{8,12},{12,16},{16,20},{20,24},{24,28},{28,32},{32,36}... | collective-permute-start | bytes 245768 | tf_op jit(solution)/shard_map/ppermute | solution.py:28
  164.2 1.9 %collective-permute-start.9 = (f32[10,4,512]{2,1,0:T(4,128)S(1)}, f32[10,4,512]{2,1,0:T(4,128)S(1)}, u32[]{:S(2)}, u32[]{:S(2)}) collective-permute-start(f32[10,4,512]{2,1,0:T(4,128)S(1)} %get-tuple-element.44), channel_id=1, source_target_pairs={{4,0},{8,4},{12,8},{16,12},{20,16},{24,20},{28,24},{32,28},{36,32}... | collective-permute-start | bytes 245768 | tf_op jit(solution)/shard_map/ppermute | solution.py:29
  166.9 3.1 %collective-permute-done.9 = f32[10,4,512]{2,1,0:T(4,128)S(1)} collective-permute-done((f32[10,4,512]{2,1,0:T(4,128)S(1)}, f32[10,4,512]{2,1,0:T(4,128)S(1)}, u32[]{:S(2)}, u32[]{:S(2)}) %collective-permute-start.9) | collective-permute-done | bytes 81952 | tf_op jit(solution)/shard_map/ppermute | solution.py:29
  (157 shorter events, 24.2 us)
Async XLA Ops:
  4.7 24.7 %copy-start.24 = (s32[512]{0:T(512)S(1)}, s32[512]{0:T(512)}, u32[]{:S(2)}) copy-start(s32[512]{0:T(512)} %param.39) | copy-start | bytes 6148
  4.7 24.7 %copy-start.22 = (s32[4,512]{1,0:T(4,128)S(1)}, s32[4,512]{1,0:T(4,128)}, u32[]{:S(2)}) copy-start(s32[4,512]{1,0:T(4,128)} %param.37) | copy-start | bytes 24580
  6.5 23.0 %copy-start.25 = (f32[192]{0:T(256)S(1)}, f32[192]{0:T(256)}, u32[]{:S(2)}) copy-start(f32[192]{0:T(256)} %param.33) | copy-start | bytes 2308
  6.5 23.0 %copy-start.26 = (f32[192]{0:T(256)S(1)}, f32[192]{0:T(256)}, u32[]{:S(2)}) copy-start(f32[192]{0:T(256)} %param.34) | copy-start | bytes 2308
  6.5 23.2 %copy-start.21 = (f32[4,512]{1,0:T(4,128)S(1)}, f32[4,512]{1,0:T(4,128)}, u32[]{:S(2)}) copy-start(f32[4,512]{1,0:T(4,128)} %param.38) | copy-start | bytes 24580
  9.0 48.2 %all-to-all-start = ((f32[128,2,257]{2,1,0:T(2,128)}), f32[128,2,257]{2,1,0:T(2,128)S(1)}, u32[]{:S(2)}, u32[]{:S(2)}) async-start(f32[128,2,257]{2,1,0:T(2,128)} %all_to_all.14), calls=%async_computation | async-start | bytes 786432 | tf_op jit(solution)/shard_map/all_to_all | solution.py:218
  29.4 28.9 %copy-start.5 = (bf16[192,512]{1,0:T(8,128)(2,1)S(1)}, bf16[192,512]{1,0:T(8,128)(2,1)}, u32[]{:S(2)}) copy-start(bf16[192,512]{1,0:T(8,128)(2,1)} %param.32) | copy-start | bytes 589828
  29.4 28.9 %copy-start.28 = (f32[192]{0:T(256)S(1)}, f32[192]{0:T(256)}, u32[]{:S(2)}) copy-start(f32[192]{0:T(256)} %param.35) | copy-start | bytes 2308
  29.4 29.1 %copy-start.16 = (f32[512]{0:T(512)}, f32[512]{0:T(512)S(1)}, u32[]{:S(2)}) copy-start(f32[512]{0:T(512)S(1)} %convert_element_type.87) | copy-start | bytes 6148
  58.6 8.7 %collective-permute-start = (f32[192,128]{1,0:T(8,128)S(1)}, f32[192,128]{1,0:T(8,128)S(1)}, u32[]{:S(2)}, u32[]{:S(2)}) collective-permute-start(f32[192,128]{1,0:T(8,128)S(1)} %get-tuple-element.48), channel_id=1, source_target_pairs={{0,4},{4,8},{8,12},{12,16},{16,20},{20,24},{24,28},{28,32},{32,36}... | collective-permute-start | bytes 294920 | tf_op jit(solution)/shard_map/ppermute | solution.py:241
  63.0 5.9 %collective-permute-start.1 = (f32[192,128]{1,0:T(8,128)S(1)}, f32[192,128]{1,0:T(8,128)S(1)}, u32[]{:S(2)}, u32[]{:S(2)}) collective-permute-start(f32[192,128]{1,0:T(8,128)S(1)} %get-tuple-element.47), channel_id=1, source_target_pairs={{4,0},{8,4},{12,8},{16,12},{20,16},{24,20},{28,24},{32,28},{36,32}... | collective-permute-start | bytes 294920 | tf_op jit(solution)/shard_map/ppermute | solution.py:242
  74.1 4.3 %collective-permute-start.2 = (f32[192,128]{1,0:T(8,128)}, f32[192,128]{1,0:T(8,128)S(1)}, u32[]{:S(2)}, u32[]{:S(2)}) collective-permute-start(f32[192,128]{1,0:T(8,128)} %get-tuple-element.12), channel_id=1, source_target_pairs={{0,4},{4,8},{8,12},{12,16},{16,20},{20,24},{24,28},{28,32},{32,36}... | collective-permute-start | bytes 294920 | tf_op jit(solution)/shard_map/ppermute | solution.py:241
  76.1 6.1 %collective-permute-start.3 = (f32[192,128]{1,0:T(8,128)}, f32[192,128]{1,0:T(8,128)S(1)}, u32[]{:S(2)}, u32[]{:S(2)}) collective-permute-start(f32[192,128]{1,0:T(8,128)} %get-tuple-element.14), channel_id=1, source_target_pairs={{4,0},{8,4},{12,8},{16,12},{20,16},{24,20},{28,24},{32,28},{36,32}... | collective-permute-start | bytes 294920 | tf_op jit(solution)/shard_map/ppermute | solution.py:242
  87.5 4.3 %collective-permute-start.4 = (f32[192,128]{1,0:T(8,128)}, f32[192,128]{1,0:T(8,128)S(1)}, u32[]{:S(2)}, u32[]{:S(2)}) collective-permute-start(f32[192,128]{1,0:T(8,128)} %get-tuple-element.15), channel_id=1, source_target_pairs={{0,4},{4,8},{8,12},{12,16},{16,20},{20,24},{24,28},{28,32},{32,36}... | collective-permute-start | bytes 294920 | tf_op jit(solution)/shard_map/ppermute | solution.py:241
  89.4 6.1 %collective-permute-start.5 = (f32[192,128]{1,0:T(8,128)}, f32[192,128]{1,0:T(8,128)S(1)}, u32[]{:S(2)}, u32[]{:S(2)}) collective-permute-start(f32[192,128]{1,0:T(8,128)} %get-tuple-element.17), channel_id=1, source_target_pairs={{4,0},{8,4},{12,8},{16,12},{20,16},{24,20},{28,24},{32,28},{36,32}... | collective-permute-start | bytes 294920 | tf_op jit(solution)/shard_map/ppermute | solution.py:242
  100.8 4.6 %collective-permute-start.6 = (f32[192,128]{1,0:T(8,128)}, f32[192,128]{1,0:T(8,128)S(1)}, u32[]{:S(2)}, u32[]{:S(2)}) collective-permute-start(f32[192,128]{1,0:T(8,128)} %get-tuple-element.18), channel_id=1, source_target_pairs={{0,4},{4,8},{8,12},{12,16},{16,20},{20,24},{24,28},{28,32},{32,36}... | collective-permute-start | bytes 294920 | tf_op jit(solution)/shard_map/ppermute | solution.py:241
  102.7 6.1 %collective-permute-start.7 = (f32[192,128]{1,0:T(8,128)}, f32[192,128]{1,0:T(8,128)S(1)}, u32[]{:S(2)}, u32[]{:S(2)}) collective-permute-start(f32[192,128]{1,0:T(8,128)} %get-tuple-element.20), channel_id=1, source_target_pairs={{4,0},{8,4},{12,8},{16,12},{20,16},{24,20},{28,24},{32,28},{36,32}... | collective-permute-start | bytes 294920 | tf_op jit(solution)/shard_map/ppermute | solution.py:242
  109.5 30.8 %copy-start.7 = (f32[2,32,512]{2,1,0:T(8,128)S(1)}, f32[2,32,512]{2,1,0:T(8,128)}, u32[]{:S(2)}) copy-start(f32[2,32,512]{2,1,0:T(8,128)} %param.22) | copy-start | bytes 393220
  114.1 45.4 %copy-start.29 = (s32[64]{0:T(128)S(1)}, s32[64]{0:T(128)}, u32[]{:S(2)}) copy-start(s32[64]{0:T(128)} %param.42) | copy-start | bytes 772
  125.5 34.5 %copy-start.3 = (bf16[32,512]{1,0:T(8,128)(2,1)S(1)}, bf16[32,512]{1,0:T(8,128)(2,1)}, u32[]{:S(2)}) copy-start(bf16[32,512]{1,0:T(8,128)(2,1)} %param.23) | copy-start | bytes 98308
  125.5 34.5 %copy-start.4 = (bf16[32,512]{1,0:T(8,128)(2,1)S(1)}, bf16[32,512]{1,0:T(8,128)(2,1)}, u32[]{:S(2)}) copy-start(bf16[32,512]{1,0:T(8,128)(2,1)} %param.24) | copy-start | bytes 98308
  125.5 32.1 %all-to-all-start.1 = ((f32[128,2,128]{2,1,0:T(2,128)}), f32[128,2,128]{2,1,0:T(2,128)S(1)}, u32[]{:S(2)}, u32[]{:S(2)}) async-start(f32[128,2,128]{2,1,0:T(2,128)} %copy.44), calls=%async_computation.1 | async-start | bytes 262144 | tf_op jit(solution)/shard_map/all_to_all | solution.py:253
  160.3 6.6 %collective-permute-start.8 = (f32[10,4,512]{2,1,0:T(4,128)S(1)}, f32[10,4,512]{2,1,0:T(4,128)S(1)}, u32[]{:S(2)}, u32[]{:S(2)}) collective-permute-start(f32[10,4,512]{2,1,0:T(4,128)S(1)} %get-tuple-element.43), channel_id=1, source_target_pairs={{0,4},{4,8},{8,12},{12,16},{16,20},{20,24},{24,28},{28,32},{32,36}... | collective-permute-start | bytes 245768 | tf_op jit(solution)/shard_map/ppermute | solution.py:28
  164.2 5.8 %collective-permute-start.9 = (f32[10,4,512]{2,1,0:T(4,128)S(1)}, f32[10,4,512]{2,1,0:T(4,128)S(1)}, u32[]{:S(2)}, u32[]{:S(2)}) collective-permute-start(f32[10,4,512]{2,1,0:T(4,128)S(1)} %get-tuple-element.44), channel_id=1, source_target_pairs={{4,0},{8,4},{12,8},{16,12},{20,16},{24,20},{28,24},{32,28},{36,32}... | collective-permute-start | bytes 245768 | tf_op jit(solution)/shard_map/ppermute | solution.py:29
  (21 other events, 103.5 us)

commit v5 on v3

--- a/solution.py
+++ b/solution.py
@@ -72,44 +72,77 @@
 
 
 def sweep_kernel(
-    left_ref, energy_ref, right_ref, sel_ref, inflow_ref, rate_ref, alive_ref, out_ref, first_ref, last_ref
+    left_ref,
+    energy_ref,
+    right_ref,
+    sel_ref,
+    inflow_ref,
+    rate_ref,
+    alive_ref,
+    out_ref,
+    first_ref,
+    last_ref,
+    ext_ref,
 ):
     bands = out_ref.shape[0]
-    tiles = sel_ref.shape[0]
-    blocks = (
-        [left_ref[...]]
-        + [energy_ref[:, 128 * t : 128 * t + 128] for t in range(tiles)]
-        + [right_ref[...]]
-    )
-    for t in range(tiles):
-        window = jnp.concatenate(blocks[t : t + 3], axis=1)
-        parts = jnp.concatenate(split3(window), axis=0)
-        picked = jnp.dot(parts, sel_ref[t], preferred_element_type=jnp.float32)
-        gathered = picked[:bands] + picked[bands : 2 * bands] + picked[2 * bands :]
-        cols = slice(128 * t, 128 * t + 128)
-        energy = blocks[t + 1]
-        arriving = inflow_ref[0, :, cols] * gathered[:, 0:128]
-        for k in range(1, NBRS):
-            arriving = arriving + inflow_ref[k, :, cols] * gathered[:, 128 * k : 128 * k + 128]
-        fresh = (energy + arriving - rate_ref[:, cols] * energy) * alive_ref[:, cols]
-        out_ref[:, cols] = fresh
-        if t == 0:
-            first_ref[...] = fresh
-        if t == tiles - 1:
-            last_ref[...] = fresh
+    t = pl.program_id(0)
+    tiles = pl.num_programs(0)
+    nodes = energy_ref.shape[1]
+
+    @pl.when(t == 0)
+    def _():
+        ext_ref[:, 0:128] = left_ref[...]
+        ext_ref[:, 128 : 128 + nodes] = energy_ref[...]
+        ext_ref[:, 128 + nodes : 256 + nodes] = right_ref[...]
+
+    start = pl.multiple_of(t * 128, 128)
+    window = ext_ref[:, pl.ds(start, 384)]
+    parts = jnp.concatenate(split3(window), axis=0)
+    picked = jnp.dot(parts, sel_ref[0], preferred_element_type=jnp.float32)
+    gathered = picked[:bands] + picked[bands : 2 * bands] + picked[2 * bands :]
+    energy = window[:, 128:256]
+    arriving = inflow_ref[0] * gathered[:, 0:128]
+    for k in range(1, NBRS):
+        arriving = arriving + inflow_ref[k] * gathered[:, 128 * k : 128 * k + 128]
+    fresh = (energy + arriving - rate_ref[...] * energy) * alive_ref[...]
+    out_ref[...] = fresh
+
+    @pl.when(t == 0)
+    def _():
+        first_ref[...] = fresh
+
+    @pl.when(t == tiles - 1)
+    def _():
+        last_ref[...] = fresh
 
 
 def wave_sweep(left, energy, right, sel, inflow, rate, alive):
     bands, nodes = rate.shape
-    vmem = pl.BlockSpec(memory_space=pltpu.VMEM)
+    tiles = nodes // 128
     flops = 2 * 3 * bands * 384 * nodes * NBRS
     moved = 4 * (2 * left.size + inflow.size + 3 * rate.size) + 2 * sel.size
     edge = jax.ShapeDtypeStruct((bands, 128), jnp.float32)
+    whole = lambda shape: pl.BlockSpec(shape, lambda t: (0,) * len(shape))
     return pl.pallas_call(
         sweep_kernel,
+        grid=(tiles,),
         out_shape=(jax.ShapeDtypeStruct((bands, nodes), jnp.float32), edge, edge),
-        in_specs=[vmem] * 7,
-        out_specs=(vmem, vmem, vmem),
+        in_specs=[
+            whole((bands, 128)),
+            whole((bands, nodes)),
+            whole((bands, 128)),
+            pl.BlockSpec((1, 384, NBRS * 128), lambda t: (t, 0, 0)),
+            pl.BlockSpec((NBRS, bands, 128), lambda t: (0, 0, t)),
+            pl.BlockSpec((bands, 128), lambda t: (0, t)),
+            pl.BlockSpec((1, 128), lambda t: (0, t)),
+        ],
+        out_specs=(
+            pl.BlockSpec((bands, 128), lambda t: (0, t)),
+            whole((bands, 128)),
+            whole((bands, 128)),
+        ),
+        scratch_shapes=[pltpu.VMEM((bands, nodes + 256), jnp.float32)],
+        compiler_params=pltpu.CompilerParams(dimension_semantics=("arbitrary",)),
         cost_estimate=pl.CostEstimate(flops=flops, bytes_accessed=moved, transcendentals=0),
     )(left, energy, right, sel, inflow, rate, alive)
 

time: 173 us -> 176 us (1.017)
  Pallas kernels: 18.3 us -> 20.5 us
    pallas_call x4, Pallas kernels: 18.3 us -> 20.5 us  [wave_sweep(): pl.pallas_call(sweep_kernel, grid=(tiles,), out_shape=(jax.ShapeDtypeStru...]
where the time goes in v5:
time: 176 us; the launch traced here: 175 us
  starting transfers between devices  60.3 us (34%)
  waiting for transfers between devices  58.9 us (33%)
  Pallas kernels  20.5 us (12%)
  other arithmetic  11.8 us (7%)
  blocking collectives  8.7 us (5%)
  local copies, waits for them, and re-layouts  8.39 us (5%)
  matrix products  4.72 us (3%)
    all_to_all x1, waiting for transfers between devices, per_device(): lax.all_to_all(send_rows, ('sec', 'tile'), split_axis=0, concat_axis=0, t...  25.8 us
    pallas_call x4, Pallas kernels, wave_sweep(): pl.pallas_call(sweep_kernel, grid=(tiles,), out_shape=(jax.ShapeDtypeStru...  20.5 us
    all_to_all x1, starting transfers between devices, per_device(): lax.all_to_all(send_rows, ('sec', 'tile'), split_axis=0, concat_axis=0, t...  20.4 us
    all_to_all x1, waiting for transfers between devices, per_device(): lax.all_to_all(back_rows, ('sec', 'tile'), split_axis=0, concat_axis=0, t...  17.2 us
    all_to_all x1, starting transfers between devices, per_device(): lax.all_to_all(back_rows, ('sec', 'tile'), split_axis=0, concat_axis=0, t...  14.8 us
    ppermute x4, waiting for transfers between devices, per_device(): right = lax.ppermute(first, wave_axis, down)  12.7 us
    ppermute x4, starting transfers between devices, per_device(): left = lax.ppermute(last, wave_axis, up)  10.3 us
    ppermute x4, starting transfers between devices, per_device(): right = lax.ppermute(first, wave_axis, down)  9 us
  transfers between devices with their start and end apart: 12, of which 7 were waited for; matrix products, arithmetic and copies ran while one was open for 3% of the time, Pallas kernels for 0%

profile of v5, /device:TPU:1, one launch (start us, length us, event | category | flops | bytes accessed | tf_op | source)
XLA Modules:
  0.0 174.6 jit_solution(1094356938649412592)
XLA Ops:
  9.0 20.4 %all-to-all-start = ((f32[128,2,257]{2,1,0:T(2,128)}), f32[128,2,257]{2,1,0:T(2,128)S(1)}, u32[]{:S(2)}, u32[]{:S(2)}) async-start(f32[128,2,257]{2,1,0:T(2,128)} %all_to_all.14), calls=%async_computation | async-start | bytes 786432 | tf_op jit(solution)/shard_map/all_to_all | solution.py:248
  31.4 25.8 %all-to-all-done = f32[128,2,257]{2,1,0:T(2,128)S(1)} async-done(((f32[128,2,257]{2,1,0:T(2,128)}), f32[128,2,257]{2,1,0:T(2,128)S(1)}, u32[]{:S(2)}, u32[]{:S(2)}) %all-to-all-start) | async-done | bytes 263200 | tf_op jit(solution)/shard_map/all_to_all | solution.py:248
  58.6 4.4 %collective-permute-start = (f32[192,128]{1,0:T(8,128)S(1)}, f32[192,128]{1,0:T(8,128)S(1)}, u32[]{:S(2)}, u32[]{:S(2)}) collective-permute-start(f32[192,128]{1,0:T(8,128)S(1)} %get-tuple-element.48), channel_id=1, source_target_pairs={{0,4},{4,8},{8,12},{12,16},{16,20},{20,24},{24,28},{28,32},{32,36}... | collective-permute-start | bytes 294920 | tf_op jit(solution)/shard_map/ppermute | solution.py:271
  63.0 1.9 %collective-permute-start.1 = (f32[192,128]{1,0:T(8,128)S(1)}, f32[192,128]{1,0:T(8,128)S(1)}, u32[]{:S(2)}, u32[]{:S(2)}) collective-permute-start(f32[192,128]{1,0:T(8,128)S(1)} %get-tuple-element.47), channel_id=1, source_target_pairs={{4,0},{8,4},{12,8},{16,12},{20,16},{24,20},{28,24},{32,28},{36,32}... | collective-permute-start | bytes 294920 | tf_op jit(solution)/shard_map/ppermute | solution.py:272
  64.9 2.4 %fusion.43 = (f32[192,512]{1,0:T(8,128)}, f32[4,192,512]{2,1,0:T(8,128)}) fusion(f32[4,512]{1,0:T(4,128)S(1)} %get-tuple-element.58, f32[192]{0:T(256)S(1)} %get-tuple-element.64, f32[4,512]{1,0:T(4,128)S(1)} %get-tuple-element.57, f32[192]{0:T(256)S(1)} %get-tuple-element.63, f32[192,512]{1,0:T(8,128)S(1)} %get-tuple-element.59), kind=kLoop, calls=%fused_computation.113 | loop fusion | flops 2654208 | bytes 2377216 | tf_op jit(solution)/shard_map/reduce_sum | solution.py:263
  69.6 5.1 %shard_map.221 = (f32[192,512]{1,0:T(8,128)}, f32[192,128]{1,0:T(8,128)}, f32[192,128]{1,0:T(8,128)}) custom-call(f32[192,128]{1,0:T(8,128)} %copy-done.10, f32[192,512]{1,0:T(8,128)} %copy-done.1, f32[192,128]{1,0:T(8,128)} %copy-done.11, bf16[4,384,512]{2,1,0:T(8,128)(2,1)} %fusion.sel_ref, f32[4,192,512]{2,1,0:T(8,128)} %get-tuple-element.46.inflow_ref, ...), custom_call_target="tpu_custom_call" | custom-call | flops 905969664 | bytes 4521984 | tf_op jit(solution)/shard_map/pallas_call | solution.py:126
  74.7 2.0 %collective-permute-start.2 = (f32[192,128]{1,0:T(8,128)}, f32[192,128]{1,0:T(8,128)S(1)}, u32[]{:S(2)}, u32[]{:S(2)}) collective-permute-start(f32[192,128]{1,0:T(8,128)} %get-tuple-element.12), channel_id=1, source_target_pairs={{0,4},{4,8},{8,12},{12,16},{16,20},{20,24},{24,28},{28,32},{32,36}... | collective-permute-start | bytes 294920 | tf_op jit(solution)/shard_map/ppermute | solution.py:271
  76.7 2.3 %collective-permute-start.3 = (f32[192,128]{1,0:T(8,128)}, f32[192,128]{1,0:T(8,128)S(1)}, u32[]{:S(2)}, u32[]{:S(2)}) collective-permute-start(f32[192,128]{1,0:T(8,128)} %get-tuple-element.14), channel_id=1, source_target_pairs={{4,0},{8,4},{12,8},{16,12},{20,16},{24,20},{28,24},{32,28},{36,32}... | collective-permute-start | bytes 294920 | tf_op jit(solution)/shard_map/ppermute | solution.py:272
  79.0 3.8 %collective-permute-done.3.right_ref = f32[192,128]{1,0:T(8,128)S(1)} collective-permute-done((f32[192,128]{1,0:T(8,128)}, f32[192,128]{1,0:T(8,128)S(1)}, u32[]{:S(2)}, u32[]{:S(2)}) %collective-permute-start.3) | collective-permute-done | bytes 98336 | tf_op jit(solution)/shard_map/ppermute | solution.py:272
  83.5 5.1 %shard_map.222 = (f32[192,512]{1,0:T(8,128)}, f32[192,128]{1,0:T(8,128)}, f32[192,128]{1,0:T(8,128)}) custom-call(f32[192,128]{1,0:T(8,128)} %copy-done.12, f32[192,512]{1,0:T(8,128)} %get-tuple-element.13.energy_ref, f32[192,128]{1,0:T(8,128)} %copy-done.14, bf16[4,384,512]{2,1,0:T(8,128)(2,1)} %fusion.sel_ref, ...), custom_call_target="tpu_custom_call" | custom-call | flops 905969664 | bytes 4521984 | tf_op jit(solution)/shard_map/pallas_call | solution.py:126
  88.6 1.9 %collective-permute-start.4 = (f32[192,128]{1,0:T(8,128)}, f32[192,128]{1,0:T(8,128)S(1)}, u32[]{:S(2)}, u32[]{:S(2)}) collective-permute-start(f32[192,128]{1,0:T(8,128)} %get-tuple-element.15), channel_id=1, source_target_pairs={{0,4},{4,8},{8,12},{12,16},{16,20},{20,24},{24,28},{28,32},{32,36}... | collective-permute-start | bytes 294920 | tf_op jit(solution)/shard_map/ppermute | solution.py:271
  90.5 2.4 %collective-permute-start.5 = (f32[192,128]{1,0:T(8,128)}, f32[192,128]{1,0:T(8,128)S(1)}, u32[]{:S(2)}, u32[]{:S(2)}) collective-permute-start(f32[192,128]{1,0:T(8,128)} %get-tuple-element.17), channel_id=1, source_target_pairs={{4,0},{8,4},{12,8},{16,12},{20,16},{24,20},{28,24},{32,28},{36,32}... | collective-permute-start | bytes 294920 | tf_op jit(solution)/shard_map/ppermute | solution.py:272
  93.0 3.7 %collective-permute-done.5.right_ref = f32[192,128]{1,0:T(8,128)S(1)} collective-permute-done((f32[192,128]{1,0:T(8,128)}, f32[192,128]{1,0:T(8,128)S(1)}, u32[]{:S(2)}, u32[]{:S(2)}) %collective-permute-start.5) | collective-permute-done | bytes 98336 | tf_op jit(solution)/shard_map/ppermute | solution.py:272
  97.3 5.1 %shard_map.223 = (f32[192,512]{1,0:T(8,128)}, f32[192,128]{1,0:T(8,128)}, f32[192,128]{1,0:T(8,128)}) custom-call(f32[192,128]{1,0:T(8,128)} %copy-done.13, f32[192,512]{1,0:T(8,128)} %get-tuple-element.16.energy_ref, f32[192,128]{1,0:T(8,128)} %copy-done.15, bf16[4,384,512]{2,1,0:T(8,128)(2,1)} %fusion.sel_ref, ...), custom_call_target="tpu_custom_call" | custom-call | flops 905969664 | bytes 4521984 | tf_op jit(solution)/shard_map/pallas_call | solution.py:126
  102.5 1.9 %collective-permute-start.6 = (f32[192,128]{1,0:T(8,128)}, f32[192,128]{1,0:T(8,128)S(1)}, u32[]{:S(2)}, u32[]{:S(2)}) collective-permute-start(f32[192,128]{1,0:T(8,128)} %get-tuple-element.18), channel_id=1, source_target_pairs={{0,4},{4,8},{8,12},{12,16},{16,20},{20,24},{24,28},{28,32},{32,36}... | collective-permute-start | bytes 294920 | tf_op jit(solution)/shard_map/ppermute | solution.py:271
  104.4 2.4 %collective-permute-start.7 = (f32[192,128]{1,0:T(8,128)}, f32[192,128]{1,0:T(8,128)S(1)}, u32[]{:S(2)}, u32[]{:S(2)}) collective-permute-start(f32[192,128]{1,0:T(8,128)} %get-tuple-element.20), channel_id=1, source_target_pairs={{4,0},{8,4},{12,8},{16,12},{20,16},{24,20},{28,24},{32,28},{36,32}... | collective-permute-start | bytes 294920 | tf_op jit(solution)/shard_map/ppermute | solution.py:272
  107.0 3.5 %collective-permute-done.7.right_ref = f32[192,128]{1,0:T(8,128)S(1)} collective-permute-done((f32[192,128]{1,0:T(8,128)}, f32[192,128]{1,0:T(8,128)S(1)}, u32[]{:S(2)}, u32[]{:S(2)}) %collective-permute-start.7) | collective-permute-done | bytes 98336 | tf_op jit(solution)/shard_map/ppermute | solution.py:272
  111.2 5.1 %shard_map.224 = (f32[192,512]{1,0:T(8,128)}, f32[192,128]{1,0:T(8,128)}, f32[192,128]{1,0:T(8,128)}) custom-call(f32[192,128]{1,0:T(8,128)} %copy-done.8, f32[192,512]{1,0:T(8,128)} %get-tuple-element.19.energy_ref, f32[192,128]{1,0:T(8,128)} %copy-done.9, bf16[4,384,512]{2,1,0:T(8,128)(2,1)} %fusion.sel_ref, f32[4,192,512]{2,1,0:T(8,128)} %get-tuple-element.46.inflow_ref, ...), custom_call_target="tpu_custom_call" | custom-call | flops 905969664 | bytes 4521984 | tf_op jit(solution)/shard_map/pallas_call | solution.py:126
  117.8 8.7 %psum.7 = f32[8,128]{1,0:T(8,128)S(1)} all-reduce(f32[8,128]{1,0:T(8,128)S(1)} %reshape.181), channel_id=1, replica_groups=mesh['sec'=4,'tile'=32,'lev'=4] {'lev'}, use_global_device_ids=true, to_apply=%region_4.5 | all-reduce | flops 1024 | bytes 8192 | tf_op jit(solution)/shard_map/psum | solution.py:278
  127.6 14.8 %all-to-all-start.1 = ((f32[128,2,128]{2,1,0:T(2,128)}), f32[128,2,128]{2,1,0:T(2,128)S(1)}, u32[]{:S(2)}, u32[]{:S(2)}) async-start(f32[128,2,128]{2,1,0:T(2,128)} %copy.44), calls=%async_computation.1 | async-start | bytes 262144 | tf_op jit(solution)/shard_map/all_to_all | solution.py:283
  142.4 17.2 %all-to-all-done.1 = f32[128,2,128]{2,1,0:T(2,128)S(1)} async-done(((f32[128,2,128]{2,1,0:T(2,128)}), f32[128,2,128]{2,1,0:T(2,128)S(1)}, u32[]{:S(2)}, u32[]{:S(2)}) %all-to-all-start.1) | async-done | bytes 131104 | tf_op jit(solution)/shard_map/all_to_all | solution.py:283
  162.4 3.9 %collective-permute-start.8 = (f32[10,4,512]{2,1,0:T(4,128)S(1)}, f32[10,4,512]{2,1,0:T(4,128)S(1)}, u32[]{:S(2)}, u32[]{:S(2)}) collective-permute-start(f32[10,4,512]{2,1,0:T(4,128)S(1)} %get-tuple-element.43), channel_id=1, source_target_pairs={{0,4},{4,8},{8,12},{12,16},{16,20},{20,24},{24,28},{28,32},{32,36}... | collective-permute-start | bytes 245768 | tf_op jit(solution)/shard_map/ppermute | solution.py:28
  166.3 1.9 %collective-permute-start.9 = (f32[10,4,512]{2,1,0:T(4,128)S(1)}, f32[10,4,512]{2,1,0:T(4,128)S(1)}, u32[]{:S(2)}, u32[]{:S(2)}) collective-permute-start(f32[10,4,512]{2,1,0:T(4,128)S(1)} %get-tuple-element.44), channel_id=1, source_target_pairs={{4,0},{8,4},{12,8},{16,12},{20,16},{24,20},{28,24},{32,28},{36,32}... | collective-permute-start | bytes 245768 | tf_op jit(solution)/shard_map/ppermute | solution.py:29
  168.9 3.1 %collective-permute-done.9 = f32[10,4,512]{2,1,0:T(4,128)S(1)} collective-permute-done((f32[10,4,512]{2,1,0:T(4,128)S(1)}, f32[10,4,512]{2,1,0:T(4,128)S(1)}, u32[]{:S(2)}, u32[]{:S(2)}) %collective-permute-start.9) | collective-permute-done | bytes 81952 | tf_op jit(solution)/shard_map/ppermute | solution.py:29
  (157 shorter events, 24.2 us)
Async XLA Ops:
  4.7 24.7 %copy-start.24 = (s32[512]{0:T(512)S(1)}, s32[512]{0:T(512)}, u32[]{:S(2)}) copy-start(s32[512]{0:T(512)} %param.39) | copy-start | bytes 6148
  4.7 24.7 %copy-start.22 = (s32[4,512]{1,0:T(4,128)S(1)}, s32[4,512]{1,0:T(4,128)}, u32[]{:S(2)}) copy-start(s32[4,512]{1,0:T(4,128)} %param.37) | copy-start | bytes 24580
  6.5 23.0 %copy-start.25 = (f32[192]{0:T(256)S(1)}, f32[192]{0:T(256)}, u32[]{:S(2)}) copy-start(f32[192]{0:T(256)} %param.33) | copy-start | bytes 2308
  6.5 23.0 %copy-start.26 = (f32[192]{0:T(256)S(1)}, f32[192]{0:T(256)}, u32[]{:S(2)}) copy-start(f32[192]{0:T(256)} %param.34) | copy-start | bytes 2308
  6.5 23.2 %copy-start.21 = (f32[4,512]{1,0:T(4,128)S(1)}, f32[4,512]{1,0:T(4,128)}, u32[]{:S(2)}) copy-start(f32[4,512]{1,0:T(4,128)} %param.38) | copy-start | bytes 24580
  9.0 48.2 %all-to-all-start = ((f32[128,2,257]{2,1,0:T(2,128)}), f32[128,2,257]{2,1,0:T(2,128)S(1)}, u32[]{:S(2)}, u32[]{:S(2)}) async-start(f32[128,2,257]{2,1,0:T(2,128)} %all_to_all.14), calls=%async_computation | async-start | bytes 786432 | tf_op jit(solution)/shard_map/all_to_all | solution.py:248
  29.4 28.9 %copy-start.5 = (bf16[192,512]{1,0:T(8,128)(2,1)S(1)}, bf16[192,512]{1,0:T(8,128)(2,1)}, u32[]{:S(2)}) copy-start(bf16[192,512]{1,0:T(8,128)(2,1)} %param.32) | copy-start | bytes 589828
  29.4 28.9 %copy-start.28 = (f32[192]{0:T(256)S(1)}, f32[192]{0:T(256)}, u32[]{:S(2)}) copy-start(f32[192]{0:T(256)} %param.35) | copy-start | bytes 2308
  29.4 29.1 %copy-start.16 = (f32[512]{0:T(512)}, f32[512]{0:T(512)S(1)}, u32[]{:S(2)}) copy-start(f32[512]{0:T(512)S(1)} %convert_element_type.87) | copy-start | bytes 6148
  58.6 8.7 %collective-permute-start = (f32[192,128]{1,0:T(8,128)S(1)}, f32[192,128]{1,0:T(8,128)S(1)}, u32[]{:S(2)}, u32[]{:S(2)}) collective-permute-start(f32[192,128]{1,0:T(8,128)S(1)} %get-tuple-element.48), channel_id=1, source_target_pairs={{0,4},{4,8},{8,12},{12,16},{16,20},{20,24},{24,28},{28,32},{32,36}... | collective-permute-start | bytes 294920 | tf_op jit(solution)/shard_map/ppermute | solution.py:271
  63.0 5.9 %collective-permute-start.1 = (f32[192,128]{1,0:T(8,128)S(1)}, f32[192,128]{1,0:T(8,128)S(1)}, u32[]{:S(2)}, u32[]{:S(2)}) collective-permute-start(f32[192,128]{1,0:T(8,128)S(1)} %get-tuple-element.47), channel_id=1, source_target_pairs={{4,0},{8,4},{12,8},{16,12},{20,16},{24,20},{28,24},{32,28},{36,32}... | collective-permute-start | bytes 294920 | tf_op jit(solution)/shard_map/ppermute | solution.py:272
  74.7 4.3 %collective-permute-start.2 = (f32[192,128]{1,0:T(8,128)}, f32[192,128]{1,0:T(8,128)S(1)}, u32[]{:S(2)}, u32[]{:S(2)}) collective-permute-start(f32[192,128]{1,0:T(8,128)} %get-tuple-element.12), channel_id=1, source_target_pairs={{0,4},{4,8},{8,12},{12,16},{16,20},{20,24},{24,28},{28,32},{32,36}... | collective-permute-start | bytes 294920 | tf_op jit(solution)/shard_map/ppermute | solution.py:271
  76.7 6.1 %collective-permute-start.3 = (f32[192,128]{1,0:T(8,128)}, f32[192,128]{1,0:T(8,128)S(1)}, u32[]{:S(2)}, u32[]{:S(2)}) collective-permute-start(f32[192,128]{1,0:T(8,128)} %get-tuple-element.14), channel_id=1, source_target_pairs={{4,0},{8,4},{12,8},{16,12},{20,16},{24,20},{28,24},{32,28},{36,32}... | collective-permute-start | bytes 294920 | tf_op jit(solution)/shard_map/ppermute | solution.py:272
  88.6 4.3 %collective-permute-start.4 = (f32[192,128]{1,0:T(8,128)}, f32[192,128]{1,0:T(8,128)S(1)}, u32[]{:S(2)}, u32[]{:S(2)}) collective-permute-start(f32[192,128]{1,0:T(8,128)} %get-tuple-element.15), channel_id=1, source_target_pairs={{0,4},{4,8},{8,12},{12,16},{16,20},{20,24},{24,28},{28,32},{32,36}... | collective-permute-start | bytes 294920 | tf_op jit(solution)/shard_map/ppermute | solution.py:271
  90.5 6.1 %collective-permute-start.5 = (f32[192,128]{1,0:T(8,128)}, f32[192,128]{1,0:T(8,128)S(1)}, u32[]{:S(2)}, u32[]{:S(2)}) collective-permute-start(f32[192,128]{1,0:T(8,128)} %get-tuple-element.17), channel_id=1, source_target_pairs={{4,0},{8,4},{12,8},{16,12},{20,16},{24,20},{28,24},{32,28},{36,32}... | collective-permute-start | bytes 294920 | tf_op jit(solution)/shard_map/ppermute | solution.py:272
  102.5 4.6 %collective-permute-start.6 = (f32[192,128]{1,0:T(8,128)}, f32[192,128]{1,0:T(8,128)S(1)}, u32[]{:S(2)}, u32[]{:S(2)}) collective-permute-start(f32[192,128]{1,0:T(8,128)} %get-tuple-element.18), channel_id=1, source_target_pairs={{0,4},{4,8},{8,12},{12,16},{16,20},{20,24},{24,28},{28,32},{32,36}... | collective-permute-start | bytes 294920 | tf_op jit(solution)/shard_map/ppermute | solution.py:271
  104.4 6.1 %collective-permute-start.7 = (f32[192,128]{1,0:T(8,128)}, f32[192,128]{1,0:T(8,128)S(1)}, u32[]{:S(2)}, u32[]{:S(2)}) collective-permute-start(f32[192,128]{1,0:T(8,128)} %get-tuple-element.20), channel_id=1, source_target_pairs={{4,0},{8,4},{12,8},{16,12},{20,16},{24,20},{28,24},{32,28},{36,32}... | collective-permute-start | bytes 294920 | tf_op jit(solution)/shard_map/ppermute | solution.py:272
  111.2 31.2 %copy-start.7 = (f32[2,32,512]{2,1,0:T(8,128)S(1)}, f32[2,32,512]{2,1,0:T(8,128)}, u32[]{:S(2)}) copy-start(f32[2,32,512]{2,1,0:T(8,128)} %param.22) | copy-start | bytes 393220
  116.3 45.2 %copy-start.29 = (s32[64]{0:T(128)S(1)}, s32[64]{0:T(128)}, u32[]{:S(2)}) copy-start(s32[64]{0:T(128)} %param.42) | copy-start | bytes 772
  127.6 34.4 %copy-start.3 = (bf16[32,512]{1,0:T(8,128)(2,1)S(1)}, bf16[32,512]{1,0:T(8,128)(2,1)}, u32[]{:S(2)}) copy-start(bf16[32,512]{1,0:T(8,128)(2,1)} %param.23) | copy-start | bytes 98308
  127.6 34.4 %copy-start.4 = (bf16[32,512]{1,0:T(8,128)(2,1)S(1)}, bf16[32,512]{1,0:T(8,128)(2,1)}, u32[]{:S(2)}) copy-start(bf16[32,512]{1,0:T(8,128)(2,1)} %param.24) | copy-start | bytes 98308
  127.6 32.1 %all-to-all-start.1 = ((f32[128,2,128]{2,1,0:T(2,128)}), f32[128,2,128]{2,1,0:T(2,128)S(1)}, u32[]{:S(2)}, u32[]{:S(2)}) async-start(f32[128,2,128]{2,1,0:T(2,128)} %copy.44), calls=%async_computation.1 | async-start | bytes 262144 | tf_op jit(solution)/shard_map/all_to_all | solution.py:283
  162.4 6.6 %collective-permute-start.8 = (f32[10,4,512]{2,1,0:T(4,128)S(1)}, f32[10,4,512]{2,1,0:T(4,128)S(1)}, u32[]{:S(2)}, u32[]{:S(2)}) collective-permute-start(f32[10,4,512]{2,1,0:T(4,128)S(1)} %get-tuple-element.43), channel_id=1, source_target_pairs={{0,4},{4,8},{8,12},{12,16},{16,20},{20,24},{24,28},{28,32},{32,36}... | collective-permute-start | bytes 245768 | tf_op jit(solution)/shard_map/ppermute | solution.py:28
  166.3 5.8 %collective-permute-start.9 = (f32[10,4,512]{2,1,0:T(4,128)S(1)}, f32[10,4,512]{2,1,0:T(4,128)S(1)}, u32[]{:S(2)}, u32[]{:S(2)}) collective-permute-start(f32[10,4,512]{2,1,0:T(4,128)S(1)} %get-tuple-element.44), channel_id=1, source_target_pairs={{4,0},{8,4},{12,8},{16,12},{20,16},{24,20},{28,24},{32,28},{36,32}... | collective-permute-start | bytes 245768 | tf_op jit(solution)/shard_map/ppermute | solution.py:29
  (21 other events, 104.0 us)

commit v6 on v4

--- a/solution.py
+++ b/solution.py
@@ -63,12 +63,9 @@
     return (growth[:, None] * push_term, inflow)
 
 
-def split3(x):
+def split2(x):
     hi = lax.reduce_precision(x, exponent_bits=8, mantissa_bits=7)
-    rest = x - hi
-    mid = lax.reduce_precision(rest, exponent_bits=8, mantissa_bits=7)
-    lo = rest - mid
-    return hi.astype(jnp.bfloat16), mid.astype(jnp.bfloat16), lo.astype(jnp.bfloat16)
+    return hi.astype(jnp.bfloat16), (x - hi).astype(jnp.bfloat16)
 
 
 def sweep_kernel(
@@ -81,14 +78,14 @@
         + [energy_ref[:, 128 * t : 128 * t + 128] for t in range(tiles)]
         + [right_ref[...]]
     )
-    pieces = [split3(block) for block in blocks]
+    pieces = [split2(block) for block in blocks]
     for t in range(tiles):
         parts = jnp.concatenate(
-            [jnp.concatenate([pieces[t + b][p] for b in range(3)], axis=1) for p in range(3)],
+            [jnp.concatenate([pieces[t + b][p] for b in range(3)], axis=1) for p in range(2)],
             axis=0,
         )
         picked = jnp.dot(parts, sel_ref[t], preferred_element_type=jnp.float32)
-        gathered = picked[:bands] + picked[bands : 2 * bands] + picked[2 * bands :]
+        gathered = picked[:bands] + picked[bands:]
         cols = slice(128 * t, 128 * t + 128)
         energy = blocks[t + 1]
         arriving = inflow_ref[0, :, cols] * gathered[:, 0:128]
@@ -105,7 +102,7 @@
 def wave_sweep(left, energy, right, sel, inflow, rate, alive):
     bands, nodes = rate.shape
     vmem = pl.BlockSpec(memory_space=pltpu.VMEM)
-    flops = 2 * 3 * bands * 384 * nodes * NBRS
+    flops = 2 * 2 * bands * 384 * nodes * NBRS
     moved = 4 * (2 * left.size + inflow.size + 3 * rate.size) + 2 * sel.size
     edge = jax.ShapeDtypeStruct((bands, 128), jnp.float32)
     return pl.pallas_call(

time: 173 us -> 171 us (0.988)
  Pallas kernels: 18.2 us -> 16.4 us
    pallas_call x4, Pallas kernels: 18.2 us -> 16.4 us  [wave_sweep(): pl.pallas_call(sweep_kernel, out_shape=(jax.ShapeDtypeStruct((bands, node...]
where the time goes in v6:
time: 171 us
  starting transfers between devices  60.3 us (35%)
  waiting for transfers between devices  58.9 us (34%)
  Pallas kernels  16.4 us (10%)
  other arithmetic  11.8 us (7%)
  blocking collectives  8.71 us (5%)
  local copies, waits for them, and re-layouts  8.38 us (5%)
  matrix products  4.72 us (3%)
    all_to_all x1, waiting for transfers between devices, per_device(): lax.all_to_all(send_rows, ('sec', 'tile'), split_axis=0, concat_axis=0, t...  25.8 us
    all_to_all x1, starting transfers between devices, per_device(): lax.all_to_all(send_rows, ('sec', 'tile'), split_axis=0, concat_axis=0, t...  20.4 us
    all_to_all x1, waiting for transfers between devices, per_device(): lax.all_to_all(back_rows, ('sec', 'tile'), split_axis=0, concat_axis=0, t...  17.2 us
    pallas_call x4, Pallas kernels, wave_sweep(): pl.pallas_call(sweep_kernel, out_shape=(jax.ShapeDtypeStruct((bands, node...  16.4 us
    all_to_all x1, starting transfers between devices, per_device(): lax.all_to_all(back_rows, ('sec', 'tile'), split_axis=0, concat_axis=0, t...  14.8 us
    ppermute x4, waiting for transfers between devices, per_device(): right = lax.ppermute(first, wave_axis, down)  12.7 us
    ppermute x4, starting transfers between devices, per_device(): left = lax.ppermute(last, wave_axis, up)  10.2 us
    ppermute x4, starting transfers between devices, per_device(): right = lax.ppermute(first, wave_axis, down)  9.01 us
  transfers between devices with their start and end apart: 12, of which 7 were waited for; matrix products, arithmetic and copies ran while one was open for 3% of the time, Pallas kernels for 0%

profile of v6, /device:TPU:1, one launch (start us, length us, event | category | flops | bytes accessed | tf_op | source)
XLA Modules:
  0.0 170.6 jit_solution(10464916840331087487)
XLA Ops:
  9.0 20.4 %all-to-all-start = ((f32[128,2,257]{2,1,0:T(2,128)}), f32[128,2,257]{2,1,0:T(2,128)S(1)}, u32[]{:S(2)}, u32[]{:S(2)}) async-start(f32[128,2,257]{2,1,0:T(2,128)} %all_to_all.14), calls=%async_computation | async-start | bytes 786432 | tf_op jit(solution)/shard_map/all_to_all | solution.py:215
  31.4 25.8 %all-to-all-done = f32[128,2,257]{2,1,0:T(2,128)S(1)} async-done(((f32[128,2,257]{2,1,0:T(2,128)}), f32[128,2,257]{2,1,0:T(2,128)S(1)}, u32[]{:S(2)}, u32[]{:S(2)}) %all-to-all-start) | async-done | bytes 263200 | tf_op jit(solution)/shard_map/all_to_all | solution.py:215
  58.6 4.4 %collective-permute-start = (f32[192,128]{1,0:T(8,128)S(1)}, f32[192,128]{1,0:T(8,128)S(1)}, u32[]{:S(2)}, u32[]{:S(2)}) collective-permute-start(f32[192,128]{1,0:T(8,128)S(1)} %get-tuple-element.48), channel_id=1, source_target_pairs={{0,4},{4,8},{8,12},{12,16},{16,20},{20,24},{24,28},{28,32},{32,36}... | collective-permute-start | bytes 294920 | tf_op jit(solution)/shard_map/ppermute | solution.py:238
  63.0 1.9 %collective-permute-start.1 = (f32[192,128]{1,0:T(8,128)S(1)}, f32[192,128]{1,0:T(8,128)S(1)}, u32[]{:S(2)}, u32[]{:S(2)}) collective-permute-start(f32[192,128]{1,0:T(8,128)S(1)} %get-tuple-element.47), channel_id=1, source_target_pairs={{4,0},{8,4},{12,8},{16,12},{20,16},{24,20},{28,24},{32,28},{36,32}... | collective-permute-start | bytes 294920 | tf_op jit(solution)/shard_map/ppermute | solution.py:239
  64.9 2.4 %fusion.43 = (f32[192,512]{1,0:T(8,128)}, f32[4,192,512]{2,1,0:T(8,128)}) fusion(f32[4,512]{1,0:T(4,128)S(1)} %get-tuple-element.58, f32[192]{0:T(256)S(1)} %get-tuple-element.64, f32[4,512]{1,0:T(4,128)S(1)} %get-tuple-element.57, f32[192]{0:T(256)S(1)} %get-tuple-element.63, f32[192,512]{1,0:T(8,128)S(1)} %get-tuple-element.59), kind=kLoop, calls=%fused_computation.113 | loop fusion | flops 2654208 | bytes 2377216 | tf_op jit(solution)/shard_map/reduce_sum | solution.py:230
  69.6 4.1 %shard_map.221 = (f32[192,512]{1,0:T(8,128)}, f32[192,128]{1,0:T(8,128)}, f32[192,128]{1,0:T(8,128)}) custom-call(f32[192,128]{1,0:T(8,128)} %copy-done.10, f32[192,512]{1,0:T(8,128)} %copy-done.1, f32[192,128]{1,0:T(8,128)} %copy-done.11, bf16[4,384,512]{2,1,0:T(8,128)(2,1)} %fusion.sel_ref, f32[4,192,512]{2,1,0:T(8,128)} %get-tuple-element.46.inflow_ref, ...), custom_call_target="tpu_custom_call" | custom-call | flops 603979776 | bytes 4521984 | tf_op jit(solution)/shard_map/pallas_call | solution.py:108
  73.7 2.0 %collective-permute-start.2 = (f32[192,128]{1,0:T(8,128)}, f32[192,128]{1,0:T(8,128)S(1)}, u32[]{:S(2)}, u32[]{:S(2)}) collective-permute-start(f32[192,128]{1,0:T(8,128)} %get-tuple-element.12), channel_id=1, source_target_pairs={{0,4},{4,8},{8,12},{12,16},{16,20},{20,24},{24,28},{28,32},{32,36}... | collective-permute-start | bytes 294920 | tf_op jit(solution)/shard_map/ppermute | solution.py:238
  75.7 2.3 %collective-permute-start.3 = (f32[192,128]{1,0:T(8,128)}, f32[192,128]{1,0:T(8,128)S(1)}, u32[]{:S(2)}, u32[]{:S(2)}) collective-permute-start(f32[192,128]{1,0:T(8,128)} %get-tuple-element.14), channel_id=1, source_target_pairs={{4,0},{8,4},{12,8},{16,12},{20,16},{24,20},{28,24},{32,28},{36,32}... | collective-permute-start | bytes 294920 | tf_op jit(solution)/shard_map/ppermute | solution.py:239
  78.0 3.8 %collective-permute-done.3.right_ref = f32[192,128]{1,0:T(8,128)S(1)} collective-permute-done((f32[192,128]{1,0:T(8,128)}, f32[192,128]{1,0:T(8,128)S(1)}, u32[]{:S(2)}, u32[]{:S(2)}) %collective-permute-start.3) | collective-permute-done | bytes 98336 | tf_op jit(solution)/shard_map/ppermute | solution.py:239
  82.5 4.1 %shard_map.222 = (f32[192,512]{1,0:T(8,128)}, f32[192,128]{1,0:T(8,128)}, f32[192,128]{1,0:T(8,128)}) custom-call(f32[192,128]{1,0:T(8,128)} %copy-done.12, f32[192,512]{1,0:T(8,128)} %get-tuple-element.13.energy_ref, f32[192,128]{1,0:T(8,128)} %copy-done.14, bf16[4,384,512]{2,1,0:T(8,128)(2,1)} %fusion.sel_ref, ...), custom_call_target="tpu_custom_call" | custom-call | flops 603979776 | bytes 4521984 | tf_op jit(solution)/shard_map/pallas_call | solution.py:108
  86.6 1.9 %collective-permute-start.4 = (f32[192,128]{1,0:T(8,128)}, f32[192,128]{1,0:T(8,128)S(1)}, u32[]{:S(2)}, u32[]{:S(2)}) collective-permute-start(f32[192,128]{1,0:T(8,128)} %get-tuple-element.15), channel_id=1, source_target_pairs={{0,4},{4,8},{8,12},{12,16},{16,20},{20,24},{24,28},{28,32},{32,36}... | collective-permute-start | bytes 294920 | tf_op jit(solution)/shard_map/ppermute | solution.py:238
  88.5 2.4 %collective-permute-start.5 = (f32[192,128]{1,0:T(8,128)}, f32[192,128]{1,0:T(8,128)S(1)}, u32[]{:S(2)}, u32[]{:S(2)}) collective-permute-start(f32[192,128]{1,0:T(8,128)} %get-tuple-element.17), channel_id=1, source_target_pairs={{4,0},{8,4},{12,8},{16,12},{20,16},{24,20},{28,24},{32,28},{36,32}... | collective-permute-start | bytes 294920 | tf_op jit(solution)/shard_map/ppermute | solution.py:239
  90.9 3.7 %collective-permute-done.5.right_ref = f32[192,128]{1,0:T(8,128)S(1)} collective-permute-done((f32[192,128]{1,0:T(8,128)}, f32[192,128]{1,0:T(8,128)S(1)}, u32[]{:S(2)}, u32[]{:S(2)}) %collective-permute-start.5) | collective-permute-done | bytes 98336 | tf_op jit(solution)/shard_map/ppermute | solution.py:239
  95.3 4.1 %shard_map.223 = (f32[192,512]{1,0:T(8,128)}, f32[192,128]{1,0:T(8,128)}, f32[192,128]{1,0:T(8,128)}) custom-call(f32[192,128]{1,0:T(8,128)} %copy-done.13, f32[192,512]{1,0:T(8,128)} %get-tuple-element.16.energy_ref, f32[192,128]{1,0:T(8,128)} %copy-done.15, bf16[4,384,512]{2,1,0:T(8,128)(2,1)} %fusion.sel_ref, ...), custom_call_target="tpu_custom_call" | custom-call | flops 603979776 | bytes 4521984 | tf_op jit(solution)/shard_map/pallas_call | solution.py:108
  99.4 1.9 %collective-permute-start.6 = (f32[192,128]{1,0:T(8,128)}, f32[192,128]{1,0:T(8,128)S(1)}, u32[]{:S(2)}, u32[]{:S(2)}) collective-permute-start(f32[192,128]{1,0:T(8,128)} %get-tuple-element.18), channel_id=1, source_target_pairs={{0,4},{4,8},{8,12},{12,16},{16,20},{20,24},{24,28},{28,32},{32,36}... | collective-permute-start | bytes 294920 | tf_op jit(solution)/shard_map/ppermute | solution.py:238
  101.3 2.4 %collective-permute-start.7 = (f32[192,128]{1,0:T(8,128)}, f32[192,128]{1,0:T(8,128)S(1)}, u32[]{:S(2)}, u32[]{:S(2)}) collective-permute-start(f32[192,128]{1,0:T(8,128)} %get-tuple-element.20), channel_id=1, source_target_pairs={{4,0},{8,4},{12,8},{16,12},{20,16},{24,20},{28,24},{32,28},{36,32}... | collective-permute-start | bytes 294920 | tf_op jit(solution)/shard_map/ppermute | solution.py:239
  103.9 3.5 %collective-permute-done.7.right_ref = f32[192,128]{1,0:T(8,128)S(1)} collective-permute-done((f32[192,128]{1,0:T(8,128)}, f32[192,128]{1,0:T(8,128)S(1)}, u32[]{:S(2)}, u32[]{:S(2)}) %collective-permute-start.7) | collective-permute-done | bytes 98336 | tf_op jit(solution)/shard_map/ppermute | solution.py:239
  108.1 4.1 %shard_map.224 = (f32[192,512]{1,0:T(8,128)}, f32[192,128]{1,0:T(8,128)}, f32[192,128]{1,0:T(8,128)}) custom-call(f32[192,128]{1,0:T(8,128)} %copy-done.8, f32[192,512]{1,0:T(8,128)} %get-tuple-element.19.energy_ref, f32[192,128]{1,0:T(8,128)} %copy-done.9, bf16[4,384,512]{2,1,0:T(8,128)(2,1)} %fusion.sel_ref, f32[4,192,512]{2,1,0:T(8,128)} %get-tuple-element.46.inflow_ref, ...), custom_call_target="tpu_custom_call" | custom-call | flops 603979776 | bytes 4521984 | tf_op jit(solution)/shard_map/pallas_call | solution.py:108
  113.7 8.7 %psum.7 = f32[8,128]{1,0:T(8,128)S(1)} all-reduce(f32[8,128]{1,0:T(8,128)S(1)} %reshape.181), channel_id=1, replica_groups=mesh['sec'=4,'tile'=32,'lev'=4] {'lev'}, use_global_device_ids=true, to_apply=%region_4.5 | all-reduce | flops 1024 | bytes 8192 | tf_op jit(solution)/shard_map/psum | solution.py:245
  123.5 14.8 %all-to-all-start.1 = ((f32[128,2,128]{2,1,0:T(2,128)}), f32[128,2,128]{2,1,0:T(2,128)S(1)}, u32[]{:S(2)}, u32[]{:S(2)}) async-start(f32[128,2,128]{2,1,0:T(2,128)} %copy.44), calls=%async_computation.1 | async-start | bytes 262144 | tf_op jit(solution)/shard_map/all_to_all | solution.py:250
  138.3 17.2 %all-to-all-done.1 = f32[128,2,128]{2,1,0:T(2,128)S(1)} async-done(((f32[128,2,128]{2,1,0:T(2,128)}), f32[128,2,128]{2,1,0:T(2,128)S(1)}, u32[]{:S(2)}, u32[]{:S(2)}) %all-to-all-start.1) | async-done | bytes 131104 | tf_op jit(solution)/shard_map/all_to_all | solution.py:250
  158.3 3.9 %collective-permute-start.8 = (f32[10,4,512]{2,1,0:T(4,128)S(1)}, f32[10,4,512]{2,1,0:T(4,128)S(1)}, u32[]{:S(2)}, u32[]{:S(2)}) collective-permute-start(f32[10,4,512]{2,1,0:T(4,128)S(1)} %get-tuple-element.43), channel_id=1, source_target_pairs={{0,4},{4,8},{8,12},{12,16},{16,20},{20,24},{24,28},{28,32},{32,36}... | collective-permute-start | bytes 245768 | tf_op jit(solution)/shard_map/ppermute | solution.py:28
  162.3 1.9 %collective-permute-start.9 = (f32[10,4,512]{2,1,0:T(4,128)S(1)}, f32[10,4,512]{2,1,0:T(4,128)S(1)}, u32[]{:S(2)}, u32[]{:S(2)}) collective-permute-start(f32[10,4,512]{2,1,0:T(4,128)S(1)} %get-tuple-element.44), channel_id=1, source_target_pairs={{4,0},{8,4},{12,8},{16,12},{20,16},{24,20},{28,24},{32,28},{36,32}... | collective-permute-start | bytes 245768 | tf_op jit(solution)/shard_map/ppermute | solution.py:29
  164.9 3.1 %collective-permute-done.9 = f32[10,4,512]{2,1,0:T(4,128)S(1)} collective-permute-done((f32[10,4,512]{2,1,0:T(4,128)S(1)}, f32[10,4,512]{2,1,0:T(4,128)S(1)}, u32[]{:S(2)}, u32[]{:S(2)}) %collective-permute-start.9) | collective-permute-done | bytes 81952 | tf_op jit(solution)/shard_map/ppermute | solution.py:29
  (157 shorter events, 24.2 us)
Async XLA Ops:
  4.7 24.7 %copy-start.24 = (s32[512]{0:T(512)S(1)}, s32[512]{0:T(512)}, u32[]{:S(2)}) copy-start(s32[512]{0:T(512)} %param.39) | copy-start | bytes 6148
  4.7 24.7 %copy-start.22 = (s32[4,512]{1,0:T(4,128)S(1)}, s32[4,512]{1,0:T(4,128)}, u32[]{:S(2)}) copy-start(s32[4,512]{1,0:T(4,128)} %param.37) | copy-start | bytes 24580
  6.4 23.0 %copy-start.25 = (f32[192]{0:T(256)S(1)}, f32[192]{0:T(256)}, u32[]{:S(2)}) copy-start(f32[192]{0:T(256)} %param.33) | copy-start | bytes 2308
  6.5 23.1 %copy-start.26 = (f32[192]{0:T(256)S(1)}, f32[192]{0:T(256)}, u32[]{:S(2)}) copy-start(f32[192]{0:T(256)} %param.34) | copy-start | bytes 2308
  6.5 23.2 %copy-start.21 = (f32[4,512]{1,0:T(4,128)S(1)}, f32[4,512]{1,0:T(4,128)}, u32[]{:S(2)}) copy-start(f32[4,512]{1,0:T(4,128)} %param.38) | copy-start | bytes 24580
  9.0 48.2 %all-to-all-start = ((f32[128,2,257]{2,1,0:T(2,128)}), f32[128,2,257]{2,1,0:T(2,128)S(1)}, u32[]{:S(2)}, u32[]{:S(2)}) async-start(f32[128,2,257]{2,1,0:T(2,128)} %all_to_all.14), calls=%async_computation | async-start | bytes 786432 | tf_op jit(solution)/shard_map/all_to_all | solution.py:215
  29.4 28.9 %copy-start.5 = (bf16[192,512]{1,0:T(8,128)(2,1)S(1)}, bf16[192,512]{1,0:T(8,128)(2,1)}, u32[]{:S(2)}) copy-start(bf16[192,512]{1,0:T(8,128)(2,1)} %param.32) | copy-start | bytes 589828
  29.4 28.9 %copy-start.28 = (f32[192]{0:T(256)S(1)}, f32[192]{0:T(256)}, u32[]{:S(2)}) copy-start(f32[192]{0:T(256)} %param.35) | copy-start | bytes 2308
  29.4 29.1 %copy-start.16 = (f32[512]{0:T(512)}, f32[512]{0:T(512)S(1)}, u32[]{:S(2)}) copy-start(f32[512]{0:T(512)S(1)} %convert_element_type.87) | copy-start | bytes 6148
  58.6 8.7 %collective-permute-start = (f32[192,128]{1,0:T(8,128)S(1)}, f32[192,128]{1,0:T(8,128)S(1)}, u32[]{:S(2)}, u32[]{:S(2)}) collective-permute-start(f32[192,128]{1,0:T(8,128)S(1)} %get-tuple-element.48), channel_id=1, source_target_pairs={{0,4},{4,8},{8,12},{12,16},{16,20},{20,24},{24,28},{28,32},{32,36}... | collective-permute-start | bytes 294920 | tf_op jit(solution)/shard_map/ppermute | solution.py:238
  63.0 5.9 %collective-permute-start.1 = (f32[192,128]{1,0:T(8,128)S(1)}, f32[192,128]{1,0:T(8,128)S(1)}, u32[]{:S(2)}, u32[]{:S(2)}) collective-permute-start(f32[192,128]{1,0:T(8,128)S(1)} %get-tuple-element.47), channel_id=1, source_target_pairs={{4,0},{8,4},{12,8},{16,12},{20,16},{24,20},{28,24},{32,28},{36,32}... | collective-permute-start | bytes 294920 | tf_op jit(solution)/shard_map/ppermute | solution.py:239
  73.7 4.3 %collective-permute-start.2 = (f32[192,128]{1,0:T(8,128)}, f32[192,128]{1,0:T(8,128)S(1)}, u32[]{:S(2)}, u32[]{:S(2)}) collective-permute-start(f32[192,128]{1,0:T(8,128)} %get-tuple-element.12), channel_id=1, source_target_pairs={{0,4},{4,8},{8,12},{12,16},{16,20},{20,24},{24,28},{28,32},{32,36}... | collective-permute-start | bytes 294920 | tf_op jit(solution)/shard_map/ppermute | solution.py:238
  75.7 6.1 %collective-permute-start.3 = (f32[192,128]{1,0:T(8,128)}, f32[192,128]{1,0:T(8,128)S(1)}, u32[]{:S(2)}, u32[]{:S(2)}) collective-permute-start(f32[192,128]{1,0:T(8,128)} %get-tuple-element.14), channel_id=1, source_target_pairs={{4,0},{8,4},{12,8},{16,12},{20,16},{24,20},{28,24},{32,28},{36,32}... | collective-permute-start | bytes 294920 | tf_op jit(solution)/shard_map/ppermute | solution.py:239
  86.6 4.3 %collective-permute-start.4 = (f32[192,128]{1,0:T(8,128)}, f32[192,128]{1,0:T(8,128)S(1)}, u32[]{:S(2)}, u32[]{:S(2)}) collective-permute-start(f32[192,128]{1,0:T(8,128)} %get-tuple-element.15), channel_id=1, source_target_pairs={{0,4},{4,8},{8,12},{12,16},{16,20},{20,24},{24,28},{28,32},{32,36}... | collective-permute-start | bytes 294920 | tf_op jit(solution)/shard_map/ppermute | solution.py:238
  88.5 6.1 %collective-permute-start.5 = (f32[192,128]{1,0:T(8,128)}, f32[192,128]{1,0:T(8,128)S(1)}, u32[]{:S(2)}, u32[]{:S(2)}) collective-permute-start(f32[192,128]{1,0:T(8,128)} %get-tuple-element.17), channel_id=1, source_target_pairs={{4,0},{8,4},{12,8},{16,12},{20,16},{24,20},{28,24},{32,28},{36,32}... | collective-permute-start | bytes 294920 | tf_op jit(solution)/shard_map/ppermute | solution.py:239
  99.4 4.6 %collective-permute-start.6 = (f32[192,128]{1,0:T(8,128)}, f32[192,128]{1,0:T(8,128)S(1)}, u32[]{:S(2)}, u32[]{:S(2)}) collective-permute-start(f32[192,128]{1,0:T(8,128)} %get-tuple-element.18), channel_id=1, source_target_pairs={{0,4},{4,8},{8,12},{12,16},{16,20},{20,24},{24,28},{28,32},{32,36}... | collective-permute-start | bytes 294920 | tf_op jit(solution)/shard_map/ppermute | solution.py:238
  101.3 6.1 %collective-permute-start.7 = (f32[192,128]{1,0:T(8,128)}, f32[192,128]{1,0:T(8,128)S(1)}, u32[]{:S(2)}, u32[]{:S(2)}) collective-permute-start(f32[192,128]{1,0:T(8,128)} %get-tuple-element.20), channel_id=1, source_target_pairs={{4,0},{8,4},{12,8},{16,12},{20,16},{24,20},{28,24},{32,28},{36,32}... | collective-permute-start | bytes 294920 | tf_op jit(solution)/shard_map/ppermute | solution.py:239
  108.1 30.2 %copy-start.7 = (f32[2,32,512]{2,1,0:T(8,128)S(1)}, f32[2,32,512]{2,1,0:T(8,128)}, u32[]{:S(2)}) copy-start(f32[2,32,512]{2,1,0:T(8,128)} %param.22) | copy-start | bytes 393220
  112.2 45.2 %copy-start.29 = (s32[64]{0:T(128)S(1)}, s32[64]{0:T(128)}, u32[]{:S(2)}) copy-start(s32[64]{0:T(128)} %param.42) | copy-start | bytes 772
  123.5 34.5 %copy-start.3 = (bf16[32,512]{1,0:T(8,128)(2,1)S(1)}, bf16[32,512]{1,0:T(8,128)(2,1)}, u32[]{:S(2)}) copy-start(bf16[32,512]{1,0:T(8,128)(2,1)} %param.23) | copy-start | bytes 98308
  123.5 34.5 %copy-start.4 = (bf16[32,512]{1,0:T(8,128)(2,1)S(1)}, bf16[32,512]{1,0:T(8,128)(2,1)}, u32[]{:S(2)}) copy-start(bf16[32,512]{1,0:T(8,128)(2,1)} %param.24) | copy-start | bytes 98308
  123.5 32.1 %all-to-all-start.1 = ((f32[128,2,128]{2,1,0:T(2,128)}), f32[128,2,128]{2,1,0:T(2,128)S(1)}, u32[]{:S(2)}, u32[]{:S(2)}) async-start(f32[128,2,128]{2,1,0:T(2,128)} %copy.44), calls=%async_computation.1 | async-start | bytes 262144 | tf_op jit(solution)/shard_map/all_to_all | solution.py:250
  158.3 6.6 %collective-permute-start.8 = (f32[10,4,512]{2,1,0:T(4,128)S(1)}, f32[10,4,512]{2,1,0:T(4,128)S(1)}, u32[]{:S(2)}, u32[]{:S(2)}) collective-permute-start(f32[10,4,512]{2,1,0:T(4,128)S(1)} %get-tuple-element.43), channel_id=1, source_target_pairs={{0,4},{4,8},{8,12},{12,16},{16,20},{20,24},{24,28},{28,32},{32,36}... | collective-permute-start | bytes 245768 | tf_op jit(solution)/shard_map/ppermute | solution.py:28
  162.3 5.8 %collective-permute-start.9 = (f32[10,4,512]{2,1,0:T(4,128)S(1)}, f32[10,4,512]{2,1,0:T(4,128)S(1)}, u32[]{:S(2)}, u32[]{:S(2)}) collective-permute-start(f32[10,4,512]{2,1,0:T(4,128)S(1)} %get-tuple-element.44), channel_id=1, source_target_pairs={{4,0},{8,4},{12,8},{16,12},{20,16},{24,20},{28,24},{32,28},{36,32}... | collective-permute-start | bytes 245768 | tf_op jit(solution)/shard_map/ppermute | solution.py:29
  (21 other events, 103.0 us)

commit v7 on v6

--- a/solution.py
+++ b/solution.py
@@ -212,7 +212,9 @@
     position = owners * capacity + ranking
     tagged = jnp.concatenate([pieces, remap_slot.astype(jnp.float32)[:, None]], axis=1)
     send_rows = jnp.full((slot_count, 257), -1.0, jnp.float32).at[position].set(tagged)
-    got = lax.all_to_all(send_rows, ("sec", "tile"), split_axis=0, concat_axis=0, tiled=True)
+    packed = send_rows.reshape(peer_count, capacity * 257)
+    got = lax.all_to_all(packed, ("sec", "tile"), split_axis=0, concat_axis=0, tiled=True)
+    got = got.reshape(slot_count, 257)
     got_rows = got[:, :256]
     got_ids = got[:, 256].astype(jnp.int32)
     block_index = jnp.arange(block_count, dtype=jnp.int32)

time: 171 us -> 169 us (0.988)
  waiting for transfers between devices: 58.9 us -> 56.4 us
    all_to_all x1, waiting for transfers between devices: 25.8 us -> 23.3 us  [per_device(): lax.all_to_all(packed, ('sec', 'tile'), split_axis=0, concat_axis=0, tile...]
where the time goes in v7:
time: 169 us
  starting transfers between devices  60 us (36%)
  waiting for transfers between devices  56.4 us (33%)
  Pallas kernels  16.4 us (10%)
  other arithmetic  12.6 us (7%)
  blocking collectives  8.72 us (5%)
  local copies, waits for them, and re-layouts  8.43 us (5%)
  matrix products  4.73 us (3%)
    all_to_all x1, waiting for transfers between devices, per_device(): lax.all_to_all(packed, ('sec', 'tile'), split_axis=0, concat_axis=0, tile...  23.3 us
    all_to_all x1, starting transfers between devices, per_device(): lax.all_to_all(packed, ('sec', 'tile'), split_axis=0, concat_axis=0, tile...  20.4 us
    all_to_all x1, waiting for transfers between devices, per_device(): lax.all_to_all(back_rows, ('sec', 'tile'), split_axis=0, concat_axis=0, t...  17.2 us
    pallas_call x4, Pallas kernels, wave_sweep(): pl.pallas_call(sweep_kernel, out_shape=(jax.ShapeDtypeStruct((bands, node...  16.4 us
    all_to_all x1, starting transfers between devices, per_device(): lax.all_to_all(back_rows, ('sec', 'tile'), split_axis=0, concat_axis=0, t...  14.7 us
    ppermute x4, waiting for transfers between devices, per_device(): right = lax.ppermute(first, wave_axis, down)  12.7 us
    ppermute x4, starting transfers between devices, per_device(): left = lax.ppermute(last, wave_axis, up)  9.98 us
    ppermute x4, starting transfers between devices, per_device(): right = lax.ppermute(first, wave_axis, down)  9.01 us
  transfers between devices with their start and end apart: 12, of which 7 were waited for; matrix products, arithmetic and copies ran while one was open for 3% of the time, Pallas kernels for 0%

profile of v7, /device:TPU:1, one launch (start us, length us, event | category | flops | bytes accessed | tf_op | source)
XLA Modules:
  0.0 168.6 jit_solution(13238319860129836828)
XLA Ops:
  9.2 20.4 %all-to-all-start = ((f32[128,1,514]{2,1,0:T(1,128)}), f32[128,1,514]{2,1,0:T(1,128)S(1)}, u32[]{:S(2)}, u32[]{:S(2)}) async-start(f32[128,1,514]{2,1,0:T(1,128)} %all_to_all.16), calls=%async_computation | async-start | bytes 655360 | tf_op jit(solution)/shard_map/all_to_all | solution.py:216
  31.7 23.3 %all-to-all-done = f32[128,1,514]{2,1,0:T(1,128)S(1)} async-done(((f32[128,1,514]{2,1,0:T(1,128)}), f32[128,1,514]{2,1,0:T(1,128)S(1)}, u32[]{:S(2)}, u32[]{:S(2)}) %all-to-all-start) | async-done | bytes 263200 | tf_op jit(solution)/shard_map/all_to_all | solution.py:216
  57.0 4.1 %collective-permute-start = (f32[192,128]{1,0:T(8,128)S(1)}, f32[192,128]{1,0:T(8,128)S(1)}, u32[]{:S(2)}, u32[]{:S(2)}) collective-permute-start(f32[192,128]{1,0:T(8,128)S(1)} %get-tuple-element.48), channel_id=1, source_target_pairs={{0,4},{4,8},{8,12},{12,16},{16,20},{20,24},{24,28},{28,32},{32,36}... | collective-permute-start | bytes 294920 | tf_op jit(solution)/shard_map/ppermute | solution.py:240
  61.1 1.9 %collective-permute-start.1 = (f32[192,128]{1,0:T(8,128)S(1)}, f32[192,128]{1,0:T(8,128)S(1)}, u32[]{:S(2)}, u32[]{:S(2)}) collective-permute-start(f32[192,128]{1,0:T(8,128)S(1)} %get-tuple-element.47), channel_id=1, source_target_pairs={{4,0},{8,4},{12,8},{16,12},{20,16},{24,20},{28,24},{32,28},{36,32}... | collective-permute-start | bytes 294920 | tf_op jit(solution)/shard_map/ppermute | solution.py:241
  63.0 2.3 %fusion.43 = (f32[192,512]{1,0:T(8,128)}, f32[4,192,512]{2,1,0:T(8,128)}) fusion(f32[4,512]{1,0:T(4,128)S(1)} %get-tuple-element.58, f32[192]{0:T(256)S(1)} %get-tuple-element.64, f32[4,512]{1,0:T(4,128)S(1)} %get-tuple-element.57, f32[192]{0:T(256)S(1)} %get-tuple-element.63, f32[192,512]{1,0:T(8,128)S(1)} %get-tuple-element.59), kind=kLoop, calls=%fused_computation.113 | loop fusion | flops 2654208 | bytes 2377216 | tf_op jit(solution)/shard_map/reduce_sum | solution.py:232
  67.7 4.1 %shard_map.221 = (f32[192,512]{1,0:T(8,128)}, f32[192,128]{1,0:T(8,128)}, f32[192,128]{1,0:T(8,128)}) custom-call(f32[192,128]{1,0:T(8,128)} %copy-done.10, f32[192,512]{1,0:T(8,128)} %copy-done.1, f32[192,128]{1,0:T(8,128)} %copy-done.11, bf16[4,384,512]{2,1,0:T(8,128)(2,1)} %fusion.sel_ref, f32[4,192,512]{2,1,0:T(8,128)} %get-tuple-element.46.inflow_ref, ...), custom_call_target="tpu_custom_call" | custom-call | flops 603979776 | bytes 4521984 | tf_op jit(solution)/shard_map/pallas_call | solution.py:108
  71.8 2.0 %collective-permute-start.2 = (f32[192,128]{1,0:T(8,128)}, f32[192,128]{1,0:T(8,128)S(1)}, u32[]{:S(2)}, u32[]{:S(2)}) collective-permute-start(f32[192,128]{1,0:T(8,128)} %get-tuple-element.12), channel_id=1, source_target_pairs={{0,4},{4,8},{8,12},{12,16},{16,20},{20,24},{24,28},{28,32},{32,36}... | collective-permute-start | bytes 294920 | tf_op jit(solution)/shard_map/ppermute | solution.py:240
  73.8 2.3 %collective-permute-start.3 = (f32[192,128]{1,0:T(8,128)}, f32[192,128]{1,0:T(8,128)S(1)}, u32[]{:S(2)}, u32[]{:S(2)}) collective-permute-start(f32[192,128]{1,0:T(8,128)} %get-tuple-element.14), channel_id=1, source_target_pairs={{4,0},{8,4},{12,8},{16,12},{20,16},{24,20},{28,24},{32,28},{36,32}... | collective-permute-start | bytes 294920 | tf_op jit(solution)/shard_map/ppermute | solution.py:241
  76.1 3.8 %collective-permute-done.3.right_ref = f32[192,128]{1,0:T(8,128)S(1)} collective-permute-done((f32[192,128]{1,0:T(8,128)}, f32[192,128]{1,0:T(8,128)S(1)}, u32[]{:S(2)}, u32[]{:S(2)}) %collective-permute-start.3) | collective-permute-done | bytes 98336 | tf_op jit(solution)/shard_map/ppermute | solution.py:241
  80.6 4.1 %shard_map.222 = (f32[192,512]{1,0:T(8,128)}, f32[192,128]{1,0:T(8,128)}, f32[192,128]{1,0:T(8,128)}) custom-call(f32[192,128]{1,0:T(8,128)} %copy-done.12, f32[192,512]{1,0:T(8,128)} %get-tuple-element.13.energy_ref, f32[192,128]{1,0:T(8,128)} %copy-done.14, bf16[4,384,512]{2,1,0:T(8,128)(2,1)} %fusion.sel_ref, ...), custom_call_target="tpu_custom_call" | custom-call | flops 603979776 | bytes 4521984 | tf_op jit(solution)/shard_map/pallas_call | solution.py:108
  84.7 1.9 %collective-permute-start.4 = (f32[192,128]{1,0:T(8,128)}, f32[192,128]{1,0:T(8,128)S(1)}, u32[]{:S(2)}, u32[]{:S(2)}) collective-permute-start(f32[192,128]{1,0:T(8,128)} %get-tuple-element.15), channel_id=1, source_target_pairs={{0,4},{4,8},{8,12},{12,16},{16,20},{20,24},{24,28},{28,32},{32,36}... | collective-permute-start | bytes 294920 | tf_op jit(solution)/shard_map/ppermute | solution.py:240
  86.6 2.4 %collective-permute-start.5 = (f32[192,128]{1,0:T(8,128)}, f32[192,128]{1,0:T(8,128)S(1)}, u32[]{:S(2)}, u32[]{:S(2)}) collective-permute-start(f32[192,128]{1,0:T(8,128)} %get-tuple-element.17), channel_id=1, source_target_pairs={{4,0},{8,4},{12,8},{16,12},{20,16},{24,20},{28,24},{32,28},{36,32}... | collective-permute-start | bytes 294920 | tf_op jit(solution)/shard_map/ppermute | solution.py:241
  89.0 3.7 %collective-permute-done.5.right_ref = f32[192,128]{1,0:T(8,128)S(1)} collective-permute-done((f32[192,128]{1,0:T(8,128)}, f32[192,128]{1,0:T(8,128)S(1)}, u32[]{:S(2)}, u32[]{:S(2)}) %collective-permute-start.5) | collective-permute-done | bytes 98336 | tf_op jit(solution)/shard_map/ppermute | solution.py:241
  93.4 4.1 %shard_map.223 = (f32[192,512]{1,0:T(8,128)}, f32[192,128]{1,0:T(8,128)}, f32[192,128]{1,0:T(8,128)}) custom-call(f32[192,128]{1,0:T(8,128)} %copy-done.13, f32[192,512]{1,0:T(8,128)} %get-tuple-element.16.energy_ref, f32[192,128]{1,0:T(8,128)} %copy-done.15, bf16[4,384,512]{2,1,0:T(8,128)(2,1)} %fusion.sel_ref, ...), custom_call_target="tpu_custom_call" | custom-call | flops 603979776 | bytes 4521984 | tf_op jit(solution)/shard_map/pallas_call | solution.py:108
  97.5 1.9 %collective-permute-start.6 = (f32[192,128]{1,0:T(8,128)}, f32[192,128]{1,0:T(8,128)S(1)}, u32[]{:S(2)}, u32[]{:S(2)}) collective-permute-start(f32[192,128]{1,0:T(8,128)} %get-tuple-element.18), channel_id=1, source_target_pairs={{0,4},{4,8},{8,12},{12,16},{16,20},{20,24},{24,28},{28,32},{32,36}... | collective-permute-start | bytes 294920 | tf_op jit(solution)/shard_map/ppermute | solution.py:240
  99.4 2.4 %collective-permute-start.7 = (f32[192,128]{1,0:T(8,128)}, f32[192,128]{1,0:T(8,128)S(1)}, u32[]{:S(2)}, u32[]{:S(2)}) collective-permute-start(f32[192,128]{1,0:T(8,128)} %get-tuple-element.20), channel_id=1, source_target_pairs={{4,0},{8,4},{12,8},{16,12},{20,16},{24,20},{28,24},{32,28},{36,32}... | collective-permute-start | bytes 294920 | tf_op jit(solution)/shard_map/ppermute | solution.py:241
  102.0 3.5 %collective-permute-done.7.right_ref = f32[192,128]{1,0:T(8,128)S(1)} collective-permute-done((f32[192,128]{1,0:T(8,128)}, f32[192,128]{1,0:T(8,128)S(1)}, u32[]{:S(2)}, u32[]{:S(2)}) %collective-permute-start.7) | collective-permute-done | bytes 98336 | tf_op jit(solution)/shard_map/ppermute | solution.py:241
  106.2 4.1 %shard_map.224 = (f32[192,512]{1,0:T(8,128)}, f32[192,128]{1,0:T(8,128)}, f32[192,128]{1,0:T(8,128)}) custom-call(f32[192,128]{1,0:T(8,128)} %copy-done.8, f32[192,512]{1,0:T(8,128)} %get-tuple-element.19.energy_ref, f32[192,128]{1,0:T(8,128)} %copy-done.9, bf16[4,384,512]{2,1,0:T(8,128)(2,1)} %fusion.sel_ref, f32[4,192,512]{2,1,0:T(8,128)} %get-tuple-element.46.inflow_ref, ...), custom_call_target="tpu_custom_call" | custom-call | flops 603979776 | bytes 4521984 | tf_op jit(solution)/shard_map/pallas_call | solution.py:108
  111.8 8.7 %psum.7 = f32[8,128]{1,0:T(8,128)S(1)} all-reduce(f32[8,128]{1,0:T(8,128)S(1)} %reshape.188), channel_id=1, replica_groups=mesh['sec'=4,'tile'=32,'lev'=4] {'lev'}, use_global_device_ids=true, to_apply=%region_4.5 | all-reduce | flops 1024 | bytes 8192 | tf_op jit(solution)/shard_map/psum | solution.py:247
  121.6 14.7 %all-to-all-start.1 = ((f32[128,2,128]{2,1,0:T(2,128)}), f32[128,2,128]{2,1,0:T(2,128)S(1)}, u32[]{:S(2)}, u32[]{:S(2)}) async-start(f32[128,2,128]{2,1,0:T(2,128)} %copy.45), calls=%async_computation.1 | async-start | bytes 262144 | tf_op jit(solution)/shard_map/all_to_all | solution.py:252
  136.4 17.2 %all-to-all-done.1 = f32[128,2,128]{2,1,0:T(2,128)S(1)} async-done(((f32[128,2,128]{2,1,0:T(2,128)}), f32[128,2,128]{2,1,0:T(2,128)S(1)}, u32[]{:S(2)}, u32[]{:S(2)}) %all-to-all-start.1) | async-done | bytes 131104 | tf_op jit(solution)/shard_map/all_to_all | solution.py:252
  156.3 3.9 %collective-permute-start.8 = (f32[10,4,512]{2,1,0:T(4,128)S(1)}, f32[10,4,512]{2,1,0:T(4,128)S(1)}, u32[]{:S(2)}, u32[]{:S(2)}) collective-permute-start(f32[10,4,512]{2,1,0:T(4,128)S(1)} %get-tuple-element.43), channel_id=1, source_target_pairs={{0,4},{4,8},{8,12},{12,16},{16,20},{20,24},{24,28},{28,32},{32,36}... | collective-permute-start | bytes 245768 | tf_op jit(solution)/shard_map/ppermute | solution.py:28
  160.3 1.9 %collective-permute-start.9 = (f32[10,4,512]{2,1,0:T(4,128)S(1)}, f32[10,4,512]{2,1,0:T(4,128)S(1)}, u32[]{:S(2)}, u32[]{:S(2)}) collective-permute-start(f32[10,4,512]{2,1,0:T(4,128)S(1)} %get-tuple-element.44), channel_id=1, source_target_pairs={{4,0},{8,4},{12,8},{16,12},{20,16},{24,20},{28,24},{32,28},{36,32}... | collective-permute-start | bytes 245768 | tf_op jit(solution)/shard_map/ppermute | solution.py:29
  162.9 3.1 %collective-permute-done.9 = f32[10,4,512]{2,1,0:T(4,128)S(1)} collective-permute-done((f32[10,4,512]{2,1,0:T(4,128)S(1)}, f32[10,4,512]{2,1,0:T(4,128)S(1)}, u32[]{:S(2)}, u32[]{:S(2)}) %collective-permute-start.9) | collective-permute-done | bytes 81952 | tf_op jit(solution)/shard_map/ppermute | solution.py:29
  (158 shorter events, 25.1 us)
Async XLA Ops:
  4.7 24.9 %copy-start.24 = (s32[512]{0:T(512)S(1)}, s32[512]{0:T(512)}, u32[]{:S(2)}) copy-start(s32[512]{0:T(512)} %param.39) | copy-start | bytes 6148
  4.7 24.9 %copy-start.22 = (s32[4,512]{1,0:T(4,128)S(1)}, s32[4,512]{1,0:T(4,128)}, u32[]{:S(2)}) copy-start(s32[4,512]{1,0:T(4,128)} %param.37) | copy-start | bytes 24580
  4.7 25.0 %copy-start.25 = (f32[192]{0:T(256)S(1)}, f32[192]{0:T(256)}, u32[]{:S(2)}) copy-start(f32[192]{0:T(256)} %param.33) | copy-start | bytes 2308
  4.7 25.0 %copy-start.26 = (f32[192]{0:T(256)S(1)}, f32[192]{0:T(256)}, u32[]{:S(2)}) copy-start(f32[192]{0:T(256)} %param.34) | copy-start | bytes 2308
  4.8 25.1 %copy-start.21 = (f32[4,512]{1,0:T(4,128)S(1)}, f32[4,512]{1,0:T(4,128)}, u32[]{:S(2)}) copy-start(f32[4,512]{1,0:T(4,128)} %param.38) | copy-start | bytes 24580
  9.2 45.8 %all-to-all-start = ((f32[128,1,514]{2,1,0:T(1,128)}), f32[128,1,514]{2,1,0:T(1,128)S(1)}, u32[]{:S(2)}, u32[]{:S(2)}) async-start(f32[128,1,514]{2,1,0:T(1,128)} %all_to_all.16), calls=%async_computation | async-start | bytes 655360 | tf_op jit(solution)/shard_map/all_to_all | solution.py:216
  29.6 27.0 %copy-start.16 = (f32[512]{0:T(512)}, f32[512]{0:T(512)S(1)}, u32[]{:S(2)}) copy-start(f32[512]{0:T(512)S(1)} %convert_element_type.87) | copy-start | bytes 6148
  29.9 26.7 %copy-start.5 = (bf16[192,512]{1,0:T(8,128)(2,1)S(1)}, bf16[192,512]{1,0:T(8,128)(2,1)}, u32[]{:S(2)}) copy-start(bf16[192,512]{1,0:T(8,128)(2,1)} %param.32) | copy-start | bytes 589828
  29.9 26.7 %copy-start.28 = (f32[192]{0:T(256)S(1)}, f32[192]{0:T(256)}, u32[]{:S(2)}) copy-start(f32[192]{0:T(256)} %param.35) | copy-start | bytes 2308
  57.0 8.4 %collective-permute-start = (f32[192,128]{1,0:T(8,128)S(1)}, f32[192,128]{1,0:T(8,128)S(1)}, u32[]{:S(2)}, u32[]{:S(2)}) collective-permute-start(f32[192,128]{1,0:T(8,128)S(1)} %get-tuple-element.48), channel_id=1, source_target_pairs={{0,4},{4,8},{8,12},{12,16},{16,20},{20,24},{24,28},{28,32},{32,36}... | collective-permute-start | bytes 294920 | tf_op jit(solution)/shard_map/ppermute | solution.py:240
  61.1 5.9 %collective-permute-start.1 = (f32[192,128]{1,0:T(8,128)S(1)}, f32[192,128]{1,0:T(8,128)S(1)}, u32[]{:S(2)}, u32[]{:S(2)}) collective-permute-start(f32[192,128]{1,0:T(8,128)S(1)} %get-tuple-element.47), channel_id=1, source_target_pairs={{4,0},{8,4},{12,8},{16,12},{20,16},{24,20},{28,24},{32,28},{36,32}... | collective-permute-start | bytes 294920 | tf_op jit(solution)/shard_map/ppermute | solution.py:241
  71.8 4.3 %collective-permute-start.2 = (f32[192,128]{1,0:T(8,128)}, f32[192,128]{1,0:T(8,128)S(1)}, u32[]{:S(2)}, u32[]{:S(2)}) collective-permute-start(f32[192,128]{1,0:T(8,128)} %get-tuple-element.12), channel_id=1, source_target_pairs={{0,4},{4,8},{8,12},{12,16},{16,20},{20,24},{24,28},{28,32},{32,36}... | collective-permute-start | bytes 294920 | tf_op jit(solution)/shard_map/ppermute | solution.py:240
  73.8 6.1 %collective-permute-start.3 = (f32[192,128]{1,0:T(8,128)}, f32[192,128]{1,0:T(8,128)S(1)}, u32[]{:S(2)}, u32[]{:S(2)}) collective-permute-start(f32[192,128]{1,0:T(8,128)} %get-tuple-element.14), channel_id=1, source_target_pairs={{4,0},{8,4},{12,8},{16,12},{20,16},{24,20},{28,24},{32,28},{36,32}... | collective-permute-start | bytes 294920 | tf_op jit(solution)/shard_map/ppermute | solution.py:241
  84.7 4.3 %collective-permute-start.4 = (f32[192,128]{1,0:T(8,128)}, f32[192,128]{1,0:T(8,128)S(1)}, u32[]{:S(2)}, u32[]{:S(2)}) collective-permute-start(f32[192,128]{1,0:T(8,128)} %get-tuple-element.15), channel_id=1, source_target_pairs={{0,4},{4,8},{8,12},{12,16},{16,20},{20,24},{24,28},{28,32},{32,36}... | collective-permute-start | bytes 294920 | tf_op jit(solution)/shard_map/ppermute | solution.py:240
  86.6 6.1 %collective-permute-start.5 = (f32[192,128]{1,0:T(8,128)}, f32[192,128]{1,0:T(8,128)S(1)}, u32[]{:S(2)}, u32[]{:S(2)}) collective-permute-start(f32[192,128]{1,0:T(8,128)} %get-tuple-element.17), channel_id=1, source_target_pairs={{4,0},{8,4},{12,8},{16,12},{20,16},{24,20},{28,24},{32,28},{36,32}... | collective-permute-start | bytes 294920 | tf_op jit(solution)/shard_map/ppermute | solution.py:241
  97.5 4.6 %collective-permute-start.6 = (f32[192,128]{1,0:T(8,128)}, f32[192,128]{1,0:T(8,128)S(1)}, u32[]{:S(2)}, u32[]{:S(2)}) collective-permute-start(f32[192,128]{1,0:T(8,128)} %get-tuple-element.18), channel_id=1, source_target_pairs={{0,4},{4,8},{8,12},{12,16},{16,20},{20,24},{24,28},{28,32},{32,36}... | collective-permute-start | bytes 294920 | tf_op jit(solution)/shard_map/ppermute | solution.py:240
  99.4 6.1 %collective-permute-start.7 = (f32[192,128]{1,0:T(8,128)}, f32[192,128]{1,0:T(8,128)S(1)}, u32[]{:S(2)}, u32[]{:S(2)}) collective-permute-start(f32[192,128]{1,0:T(8,128)} %get-tuple-element.20), channel_id=1, source_target_pairs={{4,0},{8,4},{12,8},{16,12},{20,16},{24,20},{28,24},{32,28},{36,32}... | collective-permute-start | bytes 294920 | tf_op jit(solution)/shard_map/ppermute | solution.py:241
  106.2 30.2 %copy-start.7 = (f32[2,32,512]{2,1,0:T(8,128)S(1)}, f32[2,32,512]{2,1,0:T(8,128)}, u32[]{:S(2)}) copy-start(f32[2,32,512]{2,1,0:T(8,128)} %param.22) | copy-start | bytes 393220
  110.3 45.2 %copy-start.29 = (s32[64]{0:T(128)S(1)}, s32[64]{0:T(128)}, u32[]{:S(2)}) copy-start(s32[64]{0:T(128)} %param.42) | copy-start | bytes 772
  121.6 34.4 %copy-start.3 = (bf16[32,512]{1,0:T(8,128)(2,1)S(1)}, bf16[32,512]{1,0:T(8,128)(2,1)}, u32[]{:S(2)}) copy-start(bf16[32,512]{1,0:T(8,128)(2,1)} %param.23) | copy-start | bytes 98308
  121.6 34.4 %copy-start.4 = (bf16[32,512]{1,0:T(8,128)(2,1)S(1)}, bf16[32,512]{1,0:T(8,128)(2,1)}, u32[]{:S(2)}) copy-start(bf16[32,512]{1,0:T(8,128)(2,1)} %param.24) | copy-start | bytes 98308
  121.6 32.0 %all-to-all-start.1 = ((f32[128,2,128]{2,1,0:T(2,128)}), f32[128,2,128]{2,1,0:T(2,128)S(1)}, u32[]{:S(2)}, u32[]{:S(2)}) async-start(f32[128,2,128]{2,1,0:T(2,128)} %copy.45), calls=%async_computation.1 | async-start | bytes 262144 | tf_op jit(solution)/shard_map/all_to_all | solution.py:252
  156.3 6.6 %collective-permute-start.8 = (f32[10,4,512]{2,1,0:T(4,128)S(1)}, f32[10,4,512]{2,1,0:T(4,128)S(1)}, u32[]{:S(2)}, u32[]{:S(2)}) collective-permute-start(f32[10,4,512]{2,1,0:T(4,128)S(1)} %get-tuple-element.43), channel_id=1, source_target_pairs={{0,4},{4,8},{8,12},{12,16},{16,20},{20,24},{24,28},{28,32},{32,36}... | collective-permute-start | bytes 245768 | tf_op jit(solution)/shard_map/ppermute | solution.py:28
  160.3 5.8 %collective-permute-start.9 = (f32[10,4,512]{2,1,0:T(4,128)S(1)}, f32[10,4,512]{2,1,0:T(4,128)S(1)}, u32[]{:S(2)}, u32[]{:S(2)}) collective-permute-start(f32[10,4,512]{2,1,0:T(4,128)S(1)} %get-tuple-element.44), channel_id=1, source_target_pairs={{4,0},{8,4},{12,8},{16,12},{20,16},{24,20},{28,24},{32,28},{36,32}... | collective-permute-start | bytes 245768 | tf_op jit(solution)/shard_map/ppermute | solution.py:29
  (21 other events, 102.8 us)

commit v8 on v7

--- a/solution.py
+++ b/solution.py
@@ -1,3 +1,5 @@
+import functools
+
 import jax
 import jax.numpy as jnp
 from jax import lax
@@ -68,50 +70,44 @@
     return hi.astype(jnp.bfloat16), (x - hi).astype(jnp.bfloat16)
 
 
-def sweep_kernel(
-    left_ref, energy_ref, right_ref, sel_ref, inflow_ref, rate_ref, alive_ref, out_ref, first_ref, last_ref
-):
-    bands = out_ref.shape[0]
-    tiles = sel_ref.shape[0]
-    blocks = (
-        [left_ref[...]]
-        + [energy_ref[:, 128 * t : 128 * t + 128] for t in range(tiles)]
-        + [right_ref[...]]
-    )
+def tile_kernel(count, *refs):
+    blocks = [ref[...] for ref in refs[: 3 * count]]
+    sel_refs = refs[3 * count : 4 * count]
+    inflow_refs = refs[4 * count : 5 * count]
+    rate_refs = refs[5 * count : 6 * count]
+    alive_refs = refs[6 * count : 7 * count]
+    out_refs = refs[7 * count :]
+    bands = blocks[0].shape[0]
     pieces = [split2(block) for block in blocks]
-    for t in range(tiles):
+    for i in range(count):
         parts = jnp.concatenate(
-            [jnp.concatenate([pieces[t + b][p] for b in range(3)], axis=1) for p in range(2)],
+            [jnp.concatenate([pieces[3 * i + b][p] for b in range(3)], axis=1) for p in range(2)],
             axis=0,
         )
-        picked = jnp.dot(parts, sel_ref[t], preferred_element_type=jnp.float32)
+        picked = jnp.dot(parts, sel_refs[i][...], preferred_element_type=jnp.float32)
         gathered = picked[:bands] + picked[bands:]
-        cols = slice(128 * t, 128 * t + 128)
-        energy = blocks[t + 1]
-        arriving = inflow_ref[0, :, cols] * gathered[:, 0:128]
+        energy = blocks[3 * i + 1]
+        arriving = inflow_refs[i][0] * gathered[:, 0:128]
         for k in range(1, NBRS):
-            arriving = arriving + inflow_ref[k, :, cols] * gathered[:, 128 * k : 128 * k + 128]
-        fresh = (energy + arriving - rate_ref[:, cols] * energy) * alive_ref[:, cols]
-        out_ref[:, cols] = fresh
-        if t == 0:
-            first_ref[...] = fresh
-        if t == tiles - 1:
-            last_ref[...] = fresh
-
-
-def wave_sweep(left, energy, right, sel, inflow, rate, alive):
-    bands, nodes = rate.shape
+            arriving = arriving + inflow_refs[i][k] * gathered[:, 128 * k : 128 * k + 128]
+        out_refs[i][...] = (energy + arriving - rate_refs[i][...] * energy) * alive_refs[i][...]
+
+
+def sweep_tiles(windows, sels, inflows, rates, alives):
+    count = len(sels)
+    bands = windows[0].shape[0]
     vmem = pl.BlockSpec(memory_space=pltpu.VMEM)
-    flops = 2 * 2 * bands * 384 * nodes * NBRS
-    moved = 4 * (2 * left.size + inflow.size + 3 * rate.size) + 2 * sel.size
+    operands = list(windows) + list(sels) + list(inflows) + list(rates) + list(alives)
+    flops = 2 * 2 * bands * 384 * 128 * NBRS * count
+    moved = sum(4 * x.size for x in windows + inflows + rates) + sum(2 * x.size for x in sels)
     edge = jax.ShapeDtypeStruct((bands, 128), jnp.float32)
     return pl.pallas_call(
-        sweep_kernel,
-        out_shape=(jax.ShapeDtypeStruct((bands, nodes), jnp.float32), edge, edge),
-        in_specs=[vmem] * 7,
-        out_specs=(vmem, vmem, vmem),
+        functools.partial(tile_kernel, count),
+        out_shape=tuple([edge] * count),
+        in_specs=[vmem] * len(operands),
+        out_specs=tuple([vmem] * count),
         cost_estimate=pl.CostEstimate(flops=flops, bytes_accessed=moved, transcendentals=0),
-    )(left, energy, right, sel, inflow, rate, alive)
+    )(*operands)
 
 
 def selection(local_index):
@@ -235,11 +231,34 @@
     wave_axis = ("sec", "tile")
     up = [(i, i + 1) for i in range(lax.axis_size(wave_axis) - 1)]
     down = [(j, i) for i, j in up]
-    first, last = energy[:, :128], energy[:, -128:]
+    tiles = node_count // 128
+    cut = lambda x, t: x[..., 128 * t : 128 * t + 128]
+    sels = [sel[t] for t in range(tiles)]
+    inflows = [cut(inflow, t) for t in range(tiles)]
+    rates = [cut(total_rate, t) for t in range(tiles)]
+    alives = [cut(alive_mask, t) for t in range(tiles)]
+    blocks = [cut(energy, t) for t in range(tiles)]
+    inner = list(range(1, tiles - 1))
     for sweep in range(WSTEPS):
-        left = lax.ppermute(last, wave_axis, up)
-        right = lax.ppermute(first, wave_axis, down)
-        energy, first, last = wave_sweep(left, energy, right, sel, inflow, total_rate, alive_mask)
+        left = lax.ppermute(blocks[-1], wave_axis, up)
+        right = lax.ppermute(blocks[0], wave_axis, down)
+        middle = sweep_tiles(
+            [block for t in inner for block in blocks[t - 1 : t + 2]],
+            [sels[t] for t in inner],
+            [inflows[t] for t in inner],
+            [rates[t] for t in inner],
+            [alives[t] for t in inner],
+        )
+        ends = (0, tiles - 1)
+        first, last = sweep_tiles(
+            [left] + blocks[:2] + blocks[-2:] + [right],
+            [sels[t] for t in ends],
+            [inflows[t] for t in ends],
+            [rates[t] for t in ends],
+            [alives[t] for t in ends],
+        )
+        blocks = [first] + list(middle) + [last]
+    energy = jnp.concatenate(blocks, axis=1)
     waves_out = energy.astype(jnp.bfloat16)
     coefficient = jnp.stack(
         [band_orbital * jnp.cos(band_angle), band_orbital * jnp.sin(band_angle)]

time: 169 us -> 173 us (1.024)
  waiting for transfers between devices: 56.4 us -> 48.5 us
  local copies, waits for them, and re-layouts: 8.43 us -> 15.2 us
  Pallas kernels: 16.4 us -> 23 us
  other arithmetic: 12.6 us -> 9.48 us
    ppermute x8, waiting for transfers between devices: 12.7 us -> 5.35 us  [the longest x4 5.34 us: per_device(): right = lax.ppermute(blocks[0], wave_axis, down)]
    pallas_call x4 -> x8, Pallas kernels: 16.4 us -> 23 us  [sweep_tiles(): pl.pallas_call(functools.partial(tile_kernel, count), out_shape=tuple([ed...]
    slice x1 -> x4, local copies, waits for them, and re-layouts: 0.02 us -> 3.25 us  [per_device(): cut = lambda x, t: x[..., 128 * t:128 * t + 128]]
    reduce_sum x1, other arithmetic: 2.35 us -> 0.43 us  [per_device(): total_rate = jnp.sum(inflow, axis=0)]
    unnamed x67 -> x72, local copies, waits for them, and re-layouts: 3.02 us -> 4.54 us
  transfers between devices with their start and end apart: 12 -> 12, of which waited for: 7 -> 6; matrix products, arithmetic and copies ran while one was open for 3% -> 2% of each run, Pallas kernels for 0% -> 7%
where the time goes in v8:
time: 173 us; the launch traced here: 172 us
  starting transfers between devices  61.6 us (36%)
  waiting for transfers between devices  48.5 us (28%)
  Pallas kernels  23 us (13%)
  local copies, waits for them, and re-layouts  15.2 us (9%)
  other arithmetic  9.48 us (5%)
  blocking collectives  8.84 us (5%)
  matrix products  3.72 us (2%)
    pallas_call x8, Pallas kernels, sweep_tiles(): pl.pallas_call(functools.partial(tile_kernel, count), out_shape=tuple([ed...  23 us
    all_to_all x1, waiting for transfers between devices, per_device(): lax.all_to_all(packed, ('sec', 'tile'), split_axis=0, concat_axis=0, tile...  22.8 us
    all_to_all x1, starting transfers between devices, per_device(): lax.all_to_all(packed, ('sec', 'tile'), split_axis=0, concat_axis=0, tile...  20.4 us
    all_to_all x1, waiting for transfers between devices, per_device(): lax.all_to_all(back_rows, ('sec', 'tile'), split_axis=0, concat_axis=0, t...  17.2 us
    all_to_all x1, starting transfers between devices, per_device(): lax.all_to_all(back_rows, ('sec', 'tile'), split_axis=0, concat_axis=0, t...  16.2 us
    ppermute x4, starting transfers between devices, per_device(): left = lax.ppermute(blocks[-1], wave_axis, up)  10.7 us
    psum x1, blocking collectives, per_device(): orbital = lax.psum(jnp.dot(coefficient, energy, precision=HIGHEST), 'lev')  8.84 us
    ppermute x4, starting transfers between devices, per_device(): right = lax.ppermute(blocks[0], wave_axis, down)  8.48 us
  transfers between devices with their start and end apart: 12, of which 6 were waited for; matrix products, arithmetic and copies ran while one was open for 2% of the time, Pallas kernels for 7%

profile of v8, /device:TPU:1, one launch (start us, length us, event | category | flops | bytes accessed | tf_op | source)
XLA Modules:
  0.0 171.8 jit_solution(10708509778415854017)
XLA Ops:
  9.2 20.4 %all-to-all-start = ((f32[128,1,514]{2,1,0:T(1,128)}), f32[128,1,514]{2,1,0:T(1,128)S(1)}, u32[]{:S(2)}, u32[]{:S(2)}) async-start(f32[128,1,514]{2,1,0:T(1,128)} %all_to_all.16), calls=%async_computation | async-start | bytes 655360 | tf_op jit(solution)/shard_map/all_to_all | solution.py:212
  32.2 22.8 %all-to-all-done = f32[128,1,514]{2,1,0:T(1,128)S(1)} async-done(((f32[128,1,514]{2,1,0:T(1,128)}), f32[128,1,514]{2,1,0:T(1,128)S(1)}, u32[]{:S(2)}, u32[]{:S(2)}) %all-to-all-start) | async-done | bytes 263200 | tf_op jit(solution)/shard_map/all_to_all | solution.py:212
  59.2 4.1 %collective-permute-start = (f32[192,128]{1,0:T(8,128)S(1)}, f32[192,128]{1,0:T(8,128)S(1)}, u32[]{:S(2)}, u32[]{:S(2)}) collective-permute-start(f32[192,128]{1,0:T(8,128)S(1)} %get-tuple-element.74.refs_4_.refs_5_), channel_id=1, source_target_pairs={{0,4},{4,8},{8,12},{12,16},{16,20},{20,24},{24,28},{28,32},{32,36}... | collective-permute-start | bytes 294920 | tf_op jit(solution)/shard_map/ppermute | solution.py:243
  63.4 1.9 %collective-permute-start.1 = (f32[192,128]{1,0:T(8,128)S(1)}, f32[192,128]{1,0:T(8,128)S(1)}, u32[]{:S(2)}, u32[]{:S(2)}) collective-permute-start(f32[192,128]{1,0:T(8,128)S(1)} %get-tuple-element.73.refs_1_.refs_0_), channel_id=1, source_target_pairs={{4,0},{8,4},{12,8},{16,12},{20,16},{24,20},{28,24},{32,28},{36,32}... | collective-permute-start | bytes 294920 | tf_op jit(solution)/shard_map/ppermute | solution.py:244
  66.1 3.2 %collective-permute-done.1.refs_5_ = f32[192,128]{1,0:T(8,128)S(1)} collective-permute-done((f32[192,128]{1,0:T(8,128)S(1)}, f32[192,128]{1,0:T(8,128)S(1)}, u32[]{:S(2)}, u32[]{:S(2)}) %collective-permute-start.1) | collective-permute-done | bytes 98336 | tf_op jit(solution)/shard_map/ppermute | solution.py:244
  69.9 2.9 %shard_map.221 = (f32[192,128]{1,0:T(8,128)}, f32[192,128]{1,0:T(8,128)}) custom-call(f32[192,128]{1,0:T(8,128)} %copy-done.13, f32[192,128]{1,0:T(8,128)} %copy-done.1, f32[192,128]{1,0:T(8,128)} %get-tuple-element.72.refs_2_.refs_1_.refs_3_, f32[192,128]{1,0:T(8,128)} %get-tuple-element.71.refs_3_.refs_2_.refs_4_, f32[192,128]{1,0:T(8,128)} %copy-done.2, ...), custom_call_target="tpu_custom_call" | custom-call | flops 301989888 | bytes 2359296 | tf_op jit(solution)/shard_map/pallas_call | solution.py:104
  74.7 2.4 %collective-permute-start.3 = (f32[192,128]{1,0:T(8,128)}, f32[192,128]{1,0:T(8,128)S(1)}, u32[]{:S(2)}, u32[]{:S(2)}) collective-permute-start(f32[192,128]{1,0:T(8,128)} %get-tuple-element.19.refs_1_.refs_0_), channel_id=1, source_target_pairs={{4,0},{8,4},{12,8},{16,12},{20,16},{24,20},{28,24},{32,28},{36,32}... | collective-permute-start | bytes 294920 | tf_op jit(solution)/shard_map/ppermute | solution.py:244
  77.1 2.9 %shard_map.222 = (f32[192,128]{1,0:T(8,128)}, f32[192,128]{1,0:T(8,128)}) custom-call(f32[192,128]{1,0:T(8,128)} %copy-done.1, f32[192,128]{1,0:T(8,128)} %get-tuple-element.72.refs_2_.refs_1_.refs_3_, f32[192,128]{1,0:T(8,128)} %get-tuple-element.71.refs_3_.refs_2_.refs_4_, f32[192,128]{1,0:T(8,128)} %get-tuple-element.72.refs_2_.refs_1_.refs_3_, ...), custom_call_target="tpu_custom_call" | custom-call | flops 301989888 | bytes 2359296 | tf_op jit(solution)/shard_map/pallas_call | solution.py:104
  81.5 2.9 %shard_map.223 = (f32[192,128]{1,0:T(8,128)}, f32[192,128]{1,0:T(8,128)}) custom-call(f32[192,128]{1,0:T(8,128)} %copy-done.10, f32[192,128]{1,0:T(8,128)} %get-tuple-element.19.refs_1_.refs_0_, f32[192,128]{1,0:T(8,128)} %get-tuple-element.20.refs_2_.refs_1_.refs_3_, f32[192,128]{1,0:T(8,128)} %get-tuple-element.21.refs_3_.refs_2_.refs_4_, ...), custom_call_target="tpu_custom_call" | custom-call | flops 301989888 | bytes 2359296 | tf_op jit(solution)/shard_map/pallas_call | solution.py:104
  84.4 2.3 %collective-permute-start.4 = (f32[192,128]{1,0:T(8,128)}, f32[192,128]{1,0:T(8,128)S(1)}, u32[]{:S(2)}, u32[]{:S(2)}) collective-permute-start(f32[192,128]{1,0:T(8,128)} %get-tuple-element.22.refs_4_.refs_5_), channel_id=1, source_target_pairs={{0,4},{4,8},{8,12},{12,16},{16,20},{20,24},{24,28},{28,32},{32,36}... | collective-permute-start | bytes 294920 | tf_op jit(solution)/shard_map/ppermute | solution.py:243
  86.7 2.0 %collective-permute-start.5 = (f32[192,128]{1,0:T(8,128)}, f32[192,128]{1,0:T(8,128)S(1)}, u32[]{:S(2)}, u32[]{:S(2)}) collective-permute-start(f32[192,128]{1,0:T(8,128)} %get-tuple-element.23.refs_1_.refs_0_), channel_id=1, source_target_pairs={{4,0},{8,4},{12,8},{16,12},{20,16},{24,20},{28,24},{32,28},{36,32}... | collective-permute-start | bytes 294920 | tf_op jit(solution)/shard_map/ppermute | solution.py:244
  88.7 2.9 %shard_map.224 = (f32[192,128]{1,0:T(8,128)}, f32[192,128]{1,0:T(8,128)}) custom-call(f32[192,128]{1,0:T(8,128)} %get-tuple-element.19.refs_1_.refs_0_, f32[192,128]{1,0:T(8,128)} %get-tuple-element.20.refs_2_.refs_1_.refs_3_, f32[192,128]{1,0:T(8,128)} %get-tuple-element.21.refs_3_.refs_2_.refs_4_, f32[192,128]{1,0:T(8,128)} %get-tuple-element.20.refs_2_.refs_1_.refs_3_, ...), custom_call_target="tpu_custom_call" | custom-call | flops 301989888 | bytes 2359296 | tf_op jit(solution)/shard_map/pallas_call | solution.py:104
  93.5 2.9 %shard_map.225 = (f32[192,128]{1,0:T(8,128)}, f32[192,128]{1,0:T(8,128)}) custom-call(f32[192,128]{1,0:T(8,128)} %copy-done.12, f32[192,128]{1,0:T(8,128)} %get-tuple-element.23.refs_1_.refs_0_, f32[192,128]{1,0:T(8,128)} %get-tuple-element.24.refs_2_.refs_1_.refs_3_, f32[192,128]{1,0:T(8,128)} %get-tuple-element.25.refs_3_.refs_2_.refs_4_, ...), custom_call_target="tpu_custom_call" | custom-call | flops 301989888 | bytes 2359296 | tf_op jit(solution)/shard_map/pallas_call | solution.py:104
  96.3 2.3 %collective-permute-start.6 = (f32[192,128]{1,0:T(8,128)}, f32[192,128]{1,0:T(8,128)S(1)}, u32[]{:S(2)}, u32[]{:S(2)}) collective-permute-start(f32[192,128]{1,0:T(8,128)} %get-tuple-element.26.refs_4_.refs_5_), channel_id=1, source_target_pairs={{0,4},{4,8},{8,12},{12,16},{16,20},{20,24},{24,28},{28,32},{32,36}... | collective-permute-start | bytes 294920 | tf_op jit(solution)/shard_map/ppermute | solution.py:243
  98.7 2.2 %collective-permute-start.7 = (f32[192,128]{1,0:T(8,128)}, f32[192,128]{1,0:T(8,128)S(1)}, u32[]{:S(2)}, u32[]{:S(2)}) collective-permute-start(f32[192,128]{1,0:T(8,128)} %get-tuple-element.27.refs_1_.refs_0_), channel_id=1, source_target_pairs={{4,0},{8,4},{12,8},{16,12},{20,16},{24,20},{28,24},{32,28},{36,32}... | collective-permute-start | bytes 294920 | tf_op jit(solution)/shard_map/ppermute | solution.py:244
  101.1 2.9 %shard_map.226 = (f32[192,128]{1,0:T(8,128)}, f32[192,128]{1,0:T(8,128)}) custom-call(f32[192,128]{1,0:T(8,128)} %get-tuple-element.23.refs_1_.refs_0_, f32[192,128]{1,0:T(8,128)} %get-tuple-element.24.refs_2_.refs_1_.refs_3_, f32[192,128]{1,0:T(8,128)} %get-tuple-element.25.refs_3_.refs_2_.refs_4_, f32[192,128]{1,0:T(8,128)} %get-tuple-element.24.refs_2_.refs_1_.refs_3_, ...), custom_call_target="tpu_custom_call" | custom-call | flops 301989888 | bytes 2359296 | tf_op jit(solution)/shard_map/pallas_call | solution.py:104
  104.0 2.9 %shard_map.228 = (f32[192,128]{1,0:T(8,128)}, f32[192,128]{1,0:T(8,128)}) custom-call(f32[192,128]{1,0:T(8,128)} %get-tuple-element.27.refs_1_.refs_0_, f32[192,128]{1,0:T(8,128)} %get-tuple-element.28.refs_2_.refs_1_.refs_3_, f32[192,128]{1,0:T(8,128)} %get-tuple-element.29.refs_3_.refs_2_.refs_4_, f32[192,128]{1,0:T(8,128)} %get-tuple-element.28.refs_2_.refs_1_.refs_3_, ...), custom_call_target="tpu_custom_call" | custom-call | flops 301989888 | bytes 2359296 | tf_op jit(solution)/shard_map/pallas_call | solution.py:104
  108.2 2.9 %shard_map.227 = (f32[192,128]{1,0:T(8,128)}, f32[192,128]{1,0:T(8,128)}) custom-call(f32[192,128]{1,0:T(8,128)} %copy-done.8, f32[192,128]{1,0:T(8,128)} %get-tuple-element.27.refs_1_.refs_0_, f32[192,128]{1,0:T(8,128)} %get-tuple-element.28.refs_2_.refs_1_.refs_3_, f32[192,128]{1,0:T(8,128)} %get-tuple-element.29.refs_3_.refs_2_.refs_4_, ...), custom_call_target="tpu_custom_call" | custom-call | flops 301989888 | bytes 2359296 | tf_op jit(solution)/shard_map/pallas_call | solution.py:104
  113.4 8.8 %psum.7 = f32[8,128]{1,0:T(8,128)S(1)} all-reduce(f32[8,128]{1,0:T(8,128)S(1)} %reshape.188), channel_id=1, replica_groups=mesh['sec'=4,'tile'=32,'lev'=4] {'lev'}, use_global_device_ids=true, to_apply=%region_4.5 | all-reduce | flops 1024 | bytes 8192 | tf_op jit(solution)/shard_map/psum | solution.py:266
  123.3 16.2 %all-to-all-start.1 = ((f32[128,2,128]{2,1,0:T(2,128)}), f32[128,2,128]{2,1,0:T(2,128)S(1)}, u32[]{:S(2)}, u32[]{:S(2)}) async-start(f32[128,2,128]{2,1,0:T(2,128)} %copy.45), calls=%async_computation.1 | async-start | bytes 262144 | tf_op jit(solution)/shard_map/all_to_all | solution.py:271
  139.6 17.2 %all-to-all-done.1 = f32[128,2,128]{2,1,0:T(2,128)S(1)} async-done(((f32[128,2,128]{2,1,0:T(2,128)}), f32[128,2,128]{2,1,0:T(2,128)S(1)}, u32[]{:S(2)}, u32[]{:S(2)}) %all-to-all-start.1) | async-done | bytes 131104 | tf_op jit(solution)/shard_map/all_to_all | solution.py:271
  159.5 3.9 %collective-permute-start.8 = (f32[10,4,512]{2,1,0:T(4,128)S(1)}, f32[10,4,512]{2,1,0:T(4,128)S(1)}, u32[]{:S(2)}, u32[]{:S(2)}) collective-permute-start(f32[10,4,512]{2,1,0:T(4,128)S(1)} %get-tuple-element.63), channel_id=1, source_target_pairs={{0,4},{4,8},{8,12},{12,16},{16,20},{20,24},{24,28},{28,32},{32,36}... | collective-permute-start | bytes 245768 | tf_op jit(solution)/shard_map/ppermute | solution.py:30
  163.5 1.9 %collective-permute-start.9 = (f32[10,4,512]{2,1,0:T(4,128)S(1)}, f32[10,4,512]{2,1,0:T(4,128)S(1)}, u32[]{:S(2)}, u32[]{:S(2)}) collective-permute-start(f32[10,4,512]{2,1,0:T(4,128)S(1)} %get-tuple-element.64), channel_id=1, source_target_pairs={{4,0},{8,4},{12,8},{16,12},{20,16},{24,20},{28,24},{32,28},{36,32}... | collective-permute-start | bytes 245768 | tf_op jit(solution)/shard_map/ppermute | solution.py:31
  166.1 3.1 %collective-permute-done.9 = f32[10,4,512]{2,1,0:T(4,128)S(1)} collective-permute-done((f32[10,4,512]{2,1,0:T(4,128)S(1)}, f32[10,4,512]{2,1,0:T(4,128)S(1)}, u32[]{:S(2)}, u32[]{:S(2)}) %collective-permute-start.9) | collective-permute-done | bytes 81952 | tf_op jit(solution)/shard_map/ppermute | solution.py:31
  (172 shorter events, 32.5 us)
Async XLA Ops:
  4.7 24.9 %copy-start.25 = (s32[512]{0:T(512)S(1)}, s32[512]{0:T(512)}, u32[]{:S(2)}) copy-start(s32[512]{0:T(512)} %param.39) | copy-start | bytes 6148
  4.7 24.9 %copy-start.23 = (s32[4,512]{1,0:T(4,128)S(1)}, s32[4,512]{1,0:T(4,128)}, u32[]{:S(2)}) copy-start(s32[4,512]{1,0:T(4,128)} %param.37) | copy-start | bytes 24580
  4.7 25.5 %copy-start.26 = (f32[192]{0:T(256)S(1)}, f32[192]{0:T(256)}, u32[]{:S(2)}) copy-start(f32[192]{0:T(256)} %param.33) | copy-start | bytes 2308
  4.7 25.5 %copy-start.27 = (f32[192]{0:T(256)S(1)}, f32[192]{0:T(256)}, u32[]{:S(2)}) copy-start(f32[192]{0:T(256)} %param.34) | copy-start | bytes 2308
  4.8 25.6 %copy-start.22 = (f32[4,512]{1,0:T(4,128)S(1)}, f32[4,512]{1,0:T(4,128)}, u32[]{:S(2)}) copy-start(f32[4,512]{1,0:T(4,128)} %param.38) | copy-start | bytes 24580
  9.2 45.8 %all-to-all-start = ((f32[128,1,514]{2,1,0:T(1,128)}), f32[128,1,514]{2,1,0:T(1,128)S(1)}, u32[]{:S(2)}, u32[]{:S(2)}) async-start(f32[128,1,514]{2,1,0:T(1,128)} %all_to_all.16), calls=%async_computation | async-start | bytes 655360 | tf_op jit(solution)/shard_map/all_to_all | solution.py:212
  32.2 24.4 %copy-start.5 = (bf16[192,512]{1,0:T(8,128)(2,1)S(1)}, bf16[192,512]{1,0:T(8,128)(2,1)}, u32[]{:S(2)}) copy-start(bf16[192,512]{1,0:T(8,128)(2,1)} %param.32) | copy-start | bytes 589828
  32.2 24.4 %copy-start.29 = (f32[192]{0:T(256)S(1)}, f32[192]{0:T(256)}, u32[]{:S(2)}) copy-start(f32[192]{0:T(256)} %param.35) | copy-start | bytes 2308
  59.2 6.8 %collective-permute-start = (f32[192,128]{1,0:T(8,128)S(1)}, f32[192,128]{1,0:T(8,128)S(1)}, u32[]{:S(2)}, u32[]{:S(2)}) collective-permute-start(f32[192,128]{1,0:T(8,128)S(1)} %get-tuple-element.74.refs_4_.refs_5_), channel_id=1, source_target_pairs={{0,4},{4,8},{8,12},{12,16},{16,20},{20,24},{24,28},{28,32},{32,36}... | collective-permute-start | bytes 294920 | tf_op jit(solution)/shard_map/ppermute | solution.py:243
  63.4 5.9 %collective-permute-start.1 = (f32[192,128]{1,0:T(8,128)S(1)}, f32[192,128]{1,0:T(8,128)S(1)}, u32[]{:S(2)}, u32[]{:S(2)}) collective-permute-start(f32[192,128]{1,0:T(8,128)S(1)} %get-tuple-element.73.refs_1_.refs_0_), channel_id=1, source_target_pairs={{4,0},{8,4},{12,8},{16,12},{20,16},{24,20},{28,24},{32,28},{36,32}... | collective-permute-start | bytes 294920 | tf_op jit(solution)/shard_map/ppermute | solution.py:244
  72.8 7.2 %collective-permute-start.2 = (f32[192,128]{1,0:T(8,128)}, f32[192,128]{1,0:T(8,128)S(1)}, u32[]{:S(2)}, u32[]{:S(2)}) collective-permute-start(f32[192,128]{1,0:T(8,128)} %get-tuple-element.18.refs_4_.refs_5_), channel_id=1, source_target_pairs={{0,4},{4,8},{8,12},{12,16},{16,20},{20,24},{24,28},{28,32},{32,36}... | collective-permute-start | bytes 294920 | tf_op jit(solution)/shard_map/ppermute | solution.py:243
  74.7 6.1 %collective-permute-start.3 = (f32[192,128]{1,0:T(8,128)}, f32[192,128]{1,0:T(8,128)S(1)}, u32[]{:S(2)}, u32[]{:S(2)}) collective-permute-start(f32[192,128]{1,0:T(8,128)} %get-tuple-element.19.refs_1_.refs_0_), channel_id=1, source_target_pairs={{4,0},{8,4},{12,8},{16,12},{20,16},{24,20},{28,24},{32,28},{36,32}... | collective-permute-start | bytes 294920 | tf_op jit(solution)/shard_map/ppermute | solution.py:244
  84.4 7.2 %collective-permute-start.4 = (f32[192,128]{1,0:T(8,128)}, f32[192,128]{1,0:T(8,128)S(1)}, u32[]{:S(2)}, u32[]{:S(2)}) collective-permute-start(f32[192,128]{1,0:T(8,128)} %get-tuple-element.22.refs_4_.refs_5_), channel_id=1, source_target_pairs={{0,4},{4,8},{8,12},{12,16},{16,20},{20,24},{24,28},{28,32},{32,36}... | collective-permute-start | bytes 294920 | tf_op jit(solution)/shard_map/ppermute | solution.py:243
  86.7 6.1 %collective-permute-start.5 = (f32[192,128]{1,0:T(8,128)}, f32[192,128]{1,0:T(8,128)S(1)}, u32[]{:S(2)}, u32[]{:S(2)}) collective-permute-start(f32[192,128]{1,0:T(8,128)} %get-tuple-element.23.refs_1_.refs_0_), channel_id=1, source_target_pairs={{4,0},{8,4},{12,8},{16,12},{20,16},{24,20},{28,24},{32,28},{36,32}... | collective-permute-start | bytes 294920 | tf_op jit(solution)/shard_map/ppermute | solution.py:244
  96.3 10.5 %collective-permute-start.6 = (f32[192,128]{1,0:T(8,128)}, f32[192,128]{1,0:T(8,128)S(1)}, u32[]{:S(2)}, u32[]{:S(2)}) collective-permute-start(f32[192,128]{1,0:T(8,128)} %get-tuple-element.26.refs_4_.refs_5_), channel_id=1, source_target_pairs={{0,4},{4,8},{8,12},{12,16},{16,20},{20,24},{24,28},{28,32},{32,36}... | collective-permute-start | bytes 294920 | tf_op jit(solution)/shard_map/ppermute | solution.py:243
  98.7 8.2 %collective-permute-start.7 = (f32[192,128]{1,0:T(8,128)}, f32[192,128]{1,0:T(8,128)S(1)}, u32[]{:S(2)}, u32[]{:S(2)}) collective-permute-start(f32[192,128]{1,0:T(8,128)} %get-tuple-element.27.refs_1_.refs_0_), channel_id=1, source_target_pairs={{4,0},{8,4},{12,8},{16,12},{20,16},{24,20},{28,24},{32,28},{36,32}... | collective-permute-start | bytes 294920 | tf_op jit(solution)/shard_map/ppermute | solution.py:244
  106.9 32.7 %copy-start.7 = (f32[2,32,512]{2,1,0:T(8,128)S(1)}, f32[2,32,512]{2,1,0:T(8,128)}, u32[]{:S(2)}) copy-start(f32[2,32,512]{2,1,0:T(8,128)} %param.22) | copy-start | bytes 393220
  112.9 45.8 %copy-start.30 = (s32[64]{0:T(128)S(1)}, s32[64]{0:T(128)}, u32[]{:S(2)}) copy-start(s32[64]{0:T(128)} %param.42) | copy-start | bytes 772
  123.3 35.9 %copy-start.3 = (bf16[32,512]{1,0:T(8,128)(2,1)S(1)}, bf16[32,512]{1,0:T(8,128)(2,1)}, u32[]{:S(2)}) copy-start(bf16[32,512]{1,0:T(8,128)(2,1)} %param.23) | copy-start | bytes 98308
  123.3 35.9 %copy-start.4 = (bf16[32,512]{1,0:T(8,128)(2,1)S(1)}, bf16[32,512]{1,0:T(8,128)(2,1)}, u32[]{:S(2)}) copy-start(bf16[32,512]{1,0:T(8,128)(2,1)} %param.24) | copy-start | bytes 98308
  123.3 33.5 %all-to-all-start.1 = ((f32[128,2,128]{2,1,0:T(2,128)}), f32[128,2,128]{2,1,0:T(2,128)S(1)}, u32[]{:S(2)}, u32[]{:S(2)}) async-start(f32[128,2,128]{2,1,0:T(2,128)} %copy.45), calls=%async_computation.1 | async-start | bytes 262144 | tf_op jit(solution)/shard_map/all_to_all | solution.py:271
  139.5 19.7 %copy-start.31 = (f32[2]{0:T(128)S(1)}, f32[2]{0:T(128)}, u32[]{:S(2)}) copy-start(f32[2]{0:T(128)} %param.30) | copy-start | bytes 28
  159.5 6.6 %collective-permute-start.8 = (f32[10,4,512]{2,1,0:T(4,128)S(1)}, f32[10,4,512]{2,1,0:T(4,128)S(1)}, u32[]{:S(2)}, u32[]{:S(2)}) collective-permute-start(f32[10,4,512]{2,1,0:T(4,128)S(1)} %get-tuple-element.63), channel_id=1, source_target_pairs={{0,4},{4,8},{8,12},{12,16},{16,20},{20,24},{24,28},{28,32},{32,36}... | collective-permute-start | bytes 245768 | tf_op jit(solution)/shard_map/ppermute | solution.py:30
  163.5 5.8 %collective-permute-start.9 = (f32[10,4,512]{2,1,0:T(4,128)S(1)}, f32[10,4,512]{2,1,0:T(4,128)S(1)}, u32[]{:S(2)}, u32[]{:S(2)}) collective-permute-start(f32[10,4,512]{2,1,0:T(4,128)S(1)} %get-tuple-element.64), channel_id=1, source_target_pairs={{4,0},{8,4},{12,8},{16,12},{20,16},{24,20},{28,24},{32,28},{36,32}... | collective-permute-start | bytes 245768 | tf_op jit(solution)/shard_map/ppermute | solution.py:31
  (22 other events, 89.5 us)

commit v9 on v7

--- a/solution.py
+++ b/solution.py
@@ -69,10 +69,32 @@
 
 
 def sweep_kernel(
-    left_ref, energy_ref, right_ref, sel_ref, inflow_ref, rate_ref, alive_ref, out_ref, first_ref, last_ref
+    left_ref,
+    energy_ref,
+    right_ref,
+    sel_hbm,
+    inflow_hbm,
+    rate_ref,
+    alive_ref,
+    out_ref,
+    first_ref,
+    last_ref,
+    sel_ref,
+    inflow_ref,
+    sems,
 ):
     bands = out_ref.shape[0]
     tiles = sel_ref.shape[0]
+    copies = []
+    for t in range(tiles):
+        span = pl.ds(128 * t, 128)
+        pair = (
+            pltpu.make_async_copy(sel_hbm.at[t], sel_ref.at[t], sems.at[0, t]),
+            pltpu.make_async_copy(inflow_hbm.at[:, :, span], inflow_ref.at[:, :, span], sems.at[1, t]),
+        )
+        pair[0].start()
+        pair[1].start()
+        copies.append(pair)
     blocks = (
         [left_ref[...]]
         + [energy_ref[:, 128 * t : 128 * t + 128] for t in range(tiles)]
@@ -84,7 +106,9 @@
             [jnp.concatenate([pieces[t + b][p] for b in range(3)], axis=1) for p in range(2)],
             axis=0,
         )
+        copies[t][0].wait()
         picked = jnp.dot(parts, sel_ref[t], preferred_element_type=jnp.float32)
+        copies[t][1].wait()
         gathered = picked[:bands] + picked[bands:]
         cols = slice(128 * t, 128 * t + 128)
         energy = blocks[t + 1]
@@ -108,8 +132,13 @@
     return pl.pallas_call(
         sweep_kernel,
         out_shape=(jax.ShapeDtypeStruct((bands, nodes), jnp.float32), edge, edge),
-        in_specs=[vmem] * 7,
+        in_specs=[vmem] * 3 + [pl.BlockSpec(memory_space=pl.ANY)] * 2 + [vmem] * 2,
         out_specs=(vmem, vmem, vmem),
+        scratch_shapes=[
+            pltpu.VMEM(sel.shape, sel.dtype),
+            pltpu.VMEM(inflow.shape, inflow.dtype),
+            pltpu.SemaphoreType.DMA((2, sel.shape[0])),
+        ],
         cost_estimate=pl.CostEstimate(flops=flops, bytes_accessed=moved, transcendentals=0),
     )(left, energy, right, sel, inflow, rate, alive)
 

time: 169 us -> 172 us (1.018)
  Pallas kernels: 16.4 us -> 19.2 us
    pallas_call x4, Pallas kernels: 16.4 us -> 19.2 us  [wave_sweep(): pl.pallas_call(sweep_kernel, out_shape=(jax.ShapeDtypeStruct((bands, node...]
where the time goes in v9:
time: 172 us
  starting transfers between devices  60.2 us (35%)
  waiting for transfers between devices  56.2 us (33%)
  Pallas kernels  19.2 us (11%)
  other arithmetic  12.6 us (7%)
  blocking collectives  8.69 us (5%)
  local copies, waits for them, and re-layouts  8.43 us (5%)
  matrix products  4.71 us (3%)
    all_to_all x1, waiting for transfers between devices, per_device(): lax.all_to_all(packed, ('sec', 'tile'), split_axis=0, concat_axis=0, tile...  23.3 us
    all_to_all x1, starting transfers between devices, per_device(): lax.all_to_all(packed, ('sec', 'tile'), split_axis=0, concat_axis=0, tile...  20.4 us
    pallas_call x4, Pallas kernels, wave_sweep(): pl.pallas_call(sweep_kernel, out_shape=(jax.ShapeDtypeStruct((bands, node...  19.2 us
    all_to_all x1, waiting for transfers between devices, per_device(): lax.all_to_all(back_rows, ('sec', 'tile'), split_axis=0, concat_axis=0, t...  17.2 us
    all_to_all x1, starting transfers between devices, per_device(): lax.all_to_all(back_rows, ('sec', 'tile'), split_axis=0, concat_axis=0, t...  14.7 us
    ppermute x4, waiting for transfers between devices, per_device(): right = lax.ppermute(first, wave_axis, down)  12.5 us
    ppermute x4, starting transfers between devices, per_device(): left = lax.ppermute(last, wave_axis, up)  10 us
    ppermute x4, starting transfers between devices, per_device(): right = lax.ppermute(first, wave_axis, down)  9.2 us
  transfers between devices with their start and end apart: 12, of which 7 were waited for; matrix products, arithmetic and copies ran while one was open for 3% of the time, Pallas kernels for 0%

profile of v9, /device:TPU:1, one launch (start us, length us, event | category | flops | bytes accessed | tf_op | source)
XLA Modules:
  0.0 171.5 jit_solution(433520149484556712)
XLA Ops:
  9.2 20.4 %all-to-all-start = ((f32[128,1,514]{2,1,0:T(1,128)}), f32[128,1,514]{2,1,0:T(1,128)S(1)}, u32[]{:S(2)}, u32[]{:S(2)}) async-start(f32[128,1,514]{2,1,0:T(1,128)} %all_to_all.16), calls=%async_computation | async-start | bytes 655360 | tf_op jit(solution)/shard_map/all_to_all | solution.py:245
  31.7 23.3 %all-to-all-done = f32[128,1,514]{2,1,0:T(1,128)S(1)} async-done(((f32[128,1,514]{2,1,0:T(1,128)}), f32[128,1,514]{2,1,0:T(1,128)S(1)}, u32[]{:S(2)}, u32[]{:S(2)}) %all-to-all-start) | async-done | bytes 263200 | tf_op jit(solution)/shard_map/all_to_all | solution.py:245
  57.0 4.1 %collective-permute-start = (f32[192,128]{1,0:T(8,128)S(1)}, f32[192,128]{1,0:T(8,128)S(1)}, u32[]{:S(2)}, u32[]{:S(2)}) collective-permute-start(f32[192,128]{1,0:T(8,128)S(1)} %get-tuple-element.48), channel_id=1, source_target_pairs={{0,4},{4,8},{8,12},{12,16},{16,20},{20,24},{24,28},{28,32},{32,36}... | collective-permute-start | bytes 294920 | tf_op jit(solution)/shard_map/ppermute | solution.py:269
  61.1 1.9 %collective-permute-start.1 = (f32[192,128]{1,0:T(8,128)S(1)}, f32[192,128]{1,0:T(8,128)S(1)}, u32[]{:S(2)}, u32[]{:S(2)}) collective-permute-start(f32[192,128]{1,0:T(8,128)S(1)} %get-tuple-element.47), channel_id=1, source_target_pairs={{4,0},{8,4},{12,8},{16,12},{20,16},{24,20},{28,24},{32,28},{36,32}... | collective-permute-start | bytes 294920 | tf_op jit(solution)/shard_map/ppermute | solution.py:270
  63.0 2.3 %fusion.43 = (f32[192,512]{1,0:T(8,128)}, f32[4,192,512]{2,1,0:T(8,128)}) fusion(f32[4,512]{1,0:T(4,128)S(1)} %get-tuple-element.58, f32[192]{0:T(256)S(1)} %get-tuple-element.64, f32[4,512]{1,0:T(4,128)S(1)} %get-tuple-element.57, f32[192]{0:T(256)S(1)} %get-tuple-element.63, f32[192,512]{1,0:T(8,128)S(1)} %get-tuple-element.59), kind=kLoop, calls=%fused_computation.113 | loop fusion | flops 2654208 | bytes 2377216 | tf_op jit(solution)/shard_map/reduce_sum | solution.py:261
  67.7 4.8 %shard_map.221 = (f32[192,512]{1,0:T(8,128)}, f32[192,128]{1,0:T(8,128)}, f32[192,128]{1,0:T(8,128)}) custom-call(f32[192,128]{1,0:T(8,128)} %copy-done.10, f32[192,512]{1,0:T(8,128)} %copy-done.1, f32[192,128]{1,0:T(8,128)} %copy-done.11, bf16[4,384,512]{2,1,0:T(8,128)(2,1)} %fusion.sel_hbm, f32[4,192,512]{2,1,0:T(8,128)} %get-tuple-element.46.inflow_hbm, ...), custom_call_target="tpu_custom_call" | custom-call | flops 603979776 | bytes 4521984 | tf_op jit(solution)/shard_map/pallas_call | solution.py:132
  72.5 2.0 %collective-permute-start.2 = (f32[192,128]{1,0:T(8,128)}, f32[192,128]{1,0:T(8,128)S(1)}, u32[]{:S(2)}, u32[]{:S(2)}) collective-permute-start(f32[192,128]{1,0:T(8,128)} %get-tuple-element.12), channel_id=1, source_target_pairs={{0,4},{4,8},{8,12},{12,16},{16,20},{20,24},{24,28},{28,32},{32,36}... | collective-permute-start | bytes 294920 | tf_op jit(solution)/shard_map/ppermute | solution.py:269
  74.5 2.3 %collective-permute-start.3 = (f32[192,128]{1,0:T(8,128)}, f32[192,128]{1,0:T(8,128)S(1)}, u32[]{:S(2)}, u32[]{:S(2)}) collective-permute-start(f32[192,128]{1,0:T(8,128)} %get-tuple-element.14), channel_id=1, source_target_pairs={{4,0},{8,4},{12,8},{16,12},{20,16},{24,20},{28,24},{32,28},{36,32}... | collective-permute-start | bytes 294920 | tf_op jit(solution)/shard_map/ppermute | solution.py:270
  76.8 3.8 %collective-permute-done.3.right_ref = f32[192,128]{1,0:T(8,128)S(1)} collective-permute-done((f32[192,128]{1,0:T(8,128)}, f32[192,128]{1,0:T(8,128)S(1)}, u32[]{:S(2)}, u32[]{:S(2)}) %collective-permute-start.3) | collective-permute-done | bytes 98336 | tf_op jit(solution)/shard_map/ppermute | solution.py:270
  81.3 4.8 %shard_map.222 = (f32[192,512]{1,0:T(8,128)}, f32[192,128]{1,0:T(8,128)}, f32[192,128]{1,0:T(8,128)}) custom-call(f32[192,128]{1,0:T(8,128)} %copy-done.12, f32[192,512]{1,0:T(8,128)} %get-tuple-element.13.energy_ref, f32[192,128]{1,0:T(8,128)} %copy-done.14, bf16[4,384,512]{2,1,0:T(8,128)(2,1)} %fusion.sel_hbm, ...), custom_call_target="tpu_custom_call" | custom-call | flops 603979776 | bytes 4521984 | tf_op jit(solution)/shard_map/pallas_call | solution.py:132
  86.1 1.9 %collective-permute-start.4 = (f32[192,128]{1,0:T(8,128)}, f32[192,128]{1,0:T(8,128)S(1)}, u32[]{:S(2)}, u32[]{:S(2)}) collective-permute-start(f32[192,128]{1,0:T(8,128)} %get-tuple-element.15), channel_id=1, source_target_pairs={{0,4},{4,8},{8,12},{12,16},{16,20},{20,24},{24,28},{28,32},{32,36}... | collective-permute-start | bytes 294920 | tf_op jit(solution)/shard_map/ppermute | solution.py:269
  88.0 2.4 %collective-permute-start.5 = (f32[192,128]{1,0:T(8,128)}, f32[192,128]{1,0:T(8,128)S(1)}, u32[]{:S(2)}, u32[]{:S(2)}) collective-permute-start(f32[192,128]{1,0:T(8,128)} %get-tuple-element.17), channel_id=1, source_target_pairs={{4,0},{8,4},{12,8},{16,12},{20,16},{24,20},{28,24},{32,28},{36,32}... | collective-permute-start | bytes 294920 | tf_op jit(solution)/shard_map/ppermute | solution.py:270
  90.5 3.7 %collective-permute-done.5.right_ref = f32[192,128]{1,0:T(8,128)S(1)} collective-permute-done((f32[192,128]{1,0:T(8,128)}, f32[192,128]{1,0:T(8,128)S(1)}, u32[]{:S(2)}, u32[]{:S(2)}) %collective-permute-start.5) | collective-permute-done | bytes 98336 | tf_op jit(solution)/shard_map/ppermute | solution.py:270
  94.8 4.8 %shard_map.223 = (f32[192,512]{1,0:T(8,128)}, f32[192,128]{1,0:T(8,128)}, f32[192,128]{1,0:T(8,128)}) custom-call(f32[192,128]{1,0:T(8,128)} %copy-done.13, f32[192,512]{1,0:T(8,128)} %get-tuple-element.16.energy_ref, f32[192,128]{1,0:T(8,128)} %copy-done.15, bf16[4,384,512]{2,1,0:T(8,128)(2,1)} %fusion.sel_hbm, ...), custom_call_target="tpu_custom_call" | custom-call | flops 603979776 | bytes 4521984 | tf_op jit(solution)/shard_map/pallas_call | solution.py:132
  99.6 1.9 %collective-permute-start.6 = (f32[192,128]{1,0:T(8,128)}, f32[192,128]{1,0:T(8,128)S(1)}, u32[]{:S(2)}, u32[]{:S(2)}) collective-permute-start(f32[192,128]{1,0:T(8,128)} %get-tuple-element.18), channel_id=1, source_target_pairs={{0,4},{4,8},{8,12},{12,16},{16,20},{20,24},{24,28},{28,32},{32,36}... | collective-permute-start | bytes 294920 | tf_op jit(solution)/shard_map/ppermute | solution.py:269
  101.6 2.6 %collective-permute-start.7 = (f32[192,128]{1,0:T(8,128)}, f32[192,128]{1,0:T(8,128)S(1)}, u32[]{:S(2)}, u32[]{:S(2)}) collective-permute-start(f32[192,128]{1,0:T(8,128)} %get-tuple-element.20), channel_id=1, source_target_pairs={{4,0},{8,4},{12,8},{16,12},{20,16},{24,20},{28,24},{32,28},{36,32}... | collective-permute-start | bytes 294920 | tf_op jit(solution)/shard_map/ppermute | solution.py:270
  104.4 3.3 %collective-permute-done.7.right_ref = f32[192,128]{1,0:T(8,128)S(1)} collective-permute-done((f32[192,128]{1,0:T(8,128)}, f32[192,128]{1,0:T(8,128)S(1)}, u32[]{:S(2)}, u32[]{:S(2)}) %collective-permute-start.7) | collective-permute-done | bytes 98336 | tf_op jit(solution)/shard_map/ppermute | solution.py:270
  108.4 4.8 %shard_map.224 = (f32[192,512]{1,0:T(8,128)}, f32[192,128]{1,0:T(8,128)}, f32[192,128]{1,0:T(8,128)}) custom-call(f32[192,128]{1,0:T(8,128)} %copy-done.8, f32[192,512]{1,0:T(8,128)} %get-tuple-element.19.energy_ref, f32[192,128]{1,0:T(8,128)} %copy-done.9, bf16[4,384,512]{2,1,0:T(8,128)(2,1)} %fusion.sel_hbm, f32[4,192,512]{2,1,0:T(8,128)} %get-tuple-element.46.inflow_hbm, ...), custom_call_target="tpu_custom_call" | custom-call | flops 603979776 | bytes 4521984 | tf_op jit(solution)/shard_map/pallas_call | solution.py:132
  114.7 8.7 %psum.7 = f32[8,128]{1,0:T(8,128)S(1)} all-reduce(f32[8,128]{1,0:T(8,128)S(1)} %reshape.188), channel_id=1, replica_groups=mesh['sec'=4,'tile'=32,'lev'=4] {'lev'}, use_global_device_ids=true, to_apply=%region_4.5 | all-reduce | flops 1024 | bytes 8192 | tf_op jit(solution)/shard_map/psum | solution.py:276
  124.5 14.7 %all-to-all-start.1 = ((f32[128,2,128]{2,1,0:T(2,128)}), f32[128,2,128]{2,1,0:T(2,128)S(1)}, u32[]{:S(2)}, u32[]{:S(2)}) async-start(f32[128,2,128]{2,1,0:T(2,128)} %copy.45), calls=%async_computation.1 | async-start | bytes 262144 | tf_op jit(solution)/shard_map/all_to_all | solution.py:281
  139.3 17.2 %all-to-all-done.1 = f32[128,2,128]{2,1,0:T(2,128)S(1)} async-done(((f32[128,2,128]{2,1,0:T(2,128)}), f32[128,2,128]{2,1,0:T(2,128)S(1)}, u32[]{:S(2)}, u32[]{:S(2)}) %all-to-all-start.1) | async-done | bytes 131104 | tf_op jit(solution)/shard_map/all_to_all | solution.py:281
  159.2 3.9 %collective-permute-start.8 = (f32[10,4,512]{2,1,0:T(4,128)S(1)}, f32[10,4,512]{2,1,0:T(4,128)S(1)}, u32[]{:S(2)}, u32[]{:S(2)}) collective-permute-start(f32[10,4,512]{2,1,0:T(4,128)S(1)} %get-tuple-element.43), channel_id=1, source_target_pairs={{0,4},{4,8},{8,12},{12,16},{16,20},{20,24},{24,28},{28,32},{32,36}... | collective-permute-start | bytes 245768 | tf_op jit(solution)/shard_map/ppermute | solution.py:28
  163.2 1.9 %collective-permute-start.9 = (f32[10,4,512]{2,1,0:T(4,128)S(1)}, f32[10,4,512]{2,1,0:T(4,128)S(1)}, u32[]{:S(2)}, u32[]{:S(2)}) collective-permute-start(f32[10,4,512]{2,1,0:T(4,128)S(1)} %get-tuple-element.44), channel_id=1, source_target_pairs={{4,0},{8,4},{12,8},{16,12},{20,16},{24,20},{28,24},{32,28},{36,32}... | collective-permute-start | bytes 245768 | tf_op jit(solution)/shard_map/ppermute | solution.py:29
  165.8 3.1 %collective-permute-done.9 = f32[10,4,512]{2,1,0:T(4,128)S(1)} collective-permute-done((f32[10,4,512]{2,1,0:T(4,128)S(1)}, f32[10,4,512]{2,1,0:T(4,128)S(1)}, u32[]{:S(2)}, u32[]{:S(2)}) %collective-permute-start.9) | collective-permute-done | bytes 81952 | tf_op jit(solution)/shard_map/ppermute | solution.py:29
  (158 shorter events, 25.1 us)
Async XLA Ops:
  4.7 24.9 %copy-start.24 = (s32[512]{0:T(512)S(1)}, s32[512]{0:T(512)}, u32[]{:S(2)}) copy-start(s32[512]{0:T(512)} %param.39) | copy-start | bytes 6148
  4.7 24.9 %copy-start.22 = (s32[4,512]{1,0:T(4,128)S(1)}, s32[4,512]{1,0:T(4,128)}, u32[]{:S(2)}) copy-start(s32[4,512]{1,0:T(4,128)} %param.37) | copy-start | bytes 24580
  4.7 25.0 %copy-start.25 = (f32[192]{0:T(256)S(1)}, f32[192]{0:T(256)}, u32[]{:S(2)}) copy-start(f32[192]{0:T(256)} %param.33) | copy-start | bytes 2308
  4.7 25.0 %copy-start.26 = (f32[192]{0:T(256)S(1)}, f32[192]{0:T(256)}, u32[]{:S(2)}) copy-start(f32[192]{0:T(256)} %param.34) | copy-start | bytes 2308
  4.8 25.1 %copy-start.21 = (f32[4,512]{1,0:T(4,128)S(1)}, f32[4,512]{1,0:T(4,128)}, u32[]{:S(2)}) copy-start(f32[4,512]{1,0:T(4,128)} %param.38) | copy-start | bytes 24580
  9.2 45.8 %all-to-all-start = ((f32[128,1,514]{2,1,0:T(1,128)}), f32[128,1,514]{2,1,0:T(1,128)S(1)}, u32[]{:S(2)}, u32[]{:S(2)}) async-start(f32[128,1,514]{2,1,0:T(1,128)} %all_to_all.16), calls=%async_computation | async-start | bytes 655360 | tf_op jit(solution)/shard_map/all_to_all | solution.py:245
  29.6 27.0 %copy-start.16 = (f32[512]{0:T(512)}, f32[512]{0:T(512)S(1)}, u32[]{:S(2)}) copy-start(f32[512]{0:T(512)S(1)} %convert_element_type.87) | copy-start | bytes 6148
  29.9 26.7 %copy-start.5 = (bf16[192,512]{1,0:T(8,128)(2,1)S(1)}, bf16[192,512]{1,0:T(8,128)(2,1)}, u32[]{:S(2)}) copy-start(bf16[192,512]{1,0:T(8,128)(2,1)} %param.32) | copy-start | bytes 589828
  29.9 26.7 %copy-start.28 = (f32[192]{0:T(256)S(1)}, f32[192]{0:T(256)}, u32[]{:S(2)}) copy-start(f32[192]{0:T(256)} %param.35) | copy-start | bytes 2308
  57.0 8.4 %collective-permute-start = (f32[192,128]{1,0:T(8,128)S(1)}, f32[192,128]{1,0:T(8,128)S(1)}, u32[]{:S(2)}, u32[]{:S(2)}) collective-permute-start(f32[192,128]{1,0:T(8,128)S(1)} %get-tuple-element.48), channel_id=1, source_target_pairs={{0,4},{4,8},{8,12},{12,16},{16,20},{20,24},{24,28},{28,32},{32,36}... | collective-permute-start | bytes 294920 | tf_op jit(solution)/shard_map/ppermute | solution.py:269
  61.1 5.9 %collective-permute-start.1 = (f32[192,128]{1,0:T(8,128)S(1)}, f32[192,128]{1,0:T(8,128)S(1)}, u32[]{:S(2)}, u32[]{:S(2)}) collective-permute-start(f32[192,128]{1,0:T(8,128)S(1)} %get-tuple-element.47), channel_id=1, source_target_pairs={{4,0},{8,4},{12,8},{16,12},{20,16},{24,20},{28,24},{32,28},{36,32}... | collective-permute-start | bytes 294920 | tf_op jit(solution)/shard_map/ppermute | solution.py:270
  72.5 4.3 %collective-permute-start.2 = (f32[192,128]{1,0:T(8,128)}, f32[192,128]{1,0:T(8,128)S(1)}, u32[]{:S(2)}, u32[]{:S(2)}) collective-permute-start(f32[192,128]{1,0:T(8,128)} %get-tuple-element.12), channel_id=1, source_target_pairs={{0,4},{4,8},{8,12},{12,16},{16,20},{20,24},{24,28},{28,32},{32,36}... | collective-permute-start | bytes 294920 | tf_op jit(solution)/shard_map/ppermute | solution.py:269
  74.5 6.1 %collective-permute-start.3 = (f32[192,128]{1,0:T(8,128)}, f32[192,128]{1,0:T(8,128)S(1)}, u32[]{:S(2)}, u32[]{:S(2)}) collective-permute-start(f32[192,128]{1,0:T(8,128)} %get-tuple-element.14), channel_id=1, source_target_pairs={{4,0},{8,4},{12,8},{16,12},{20,16},{24,20},{28,24},{32,28},{36,32}... | collective-permute-start | bytes 294920 | tf_op jit(solution)/shard_map/ppermute | solution.py:270
  86.1 4.3 %collective-permute-start.4 = (f32[192,128]{1,0:T(8,128)}, f32[192,128]{1,0:T(8,128)S(1)}, u32[]{:S(2)}, u32[]{:S(2)}) collective-permute-start(f32[192,128]{1,0:T(8,128)} %get-tuple-element.15), channel_id=1, source_target_pairs={{0,4},{4,8},{8,12},{12,16},{16,20},{20,24},{24,28},{28,32},{32,36}... | collective-permute-start | bytes 294920 | tf_op jit(solution)/shard_map/ppermute | solution.py:269
  88.0 6.1 %collective-permute-start.5 = (f32[192,128]{1,0:T(8,128)}, f32[192,128]{1,0:T(8,128)S(1)}, u32[]{:S(2)}, u32[]{:S(2)}) collective-permute-start(f32[192,128]{1,0:T(8,128)} %get-tuple-element.17), channel_id=1, source_target_pairs={{4,0},{8,4},{12,8},{16,12},{20,16},{24,20},{28,24},{32,28},{36,32}... | collective-permute-start | bytes 294920 | tf_op jit(solution)/shard_map/ppermute | solution.py:270
  99.6 4.8 %collective-permute-start.6 = (f32[192,128]{1,0:T(8,128)}, f32[192,128]{1,0:T(8,128)S(1)}, u32[]{:S(2)}, u32[]{:S(2)}) collective-permute-start(f32[192,128]{1,0:T(8,128)} %get-tuple-element.18), channel_id=1, source_target_pairs={{0,4},{4,8},{8,12},{12,16},{16,20},{20,24},{24,28},{28,32},{32,36}... | collective-permute-start | bytes 294920 | tf_op jit(solution)/shard_map/ppermute | solution.py:269
  101.6 6.1 %collective-permute-start.7 = (f32[192,128]{1,0:T(8,128)}, f32[192,128]{1,0:T(8,128)S(1)}, u32[]{:S(2)}, u32[]{:S(2)}) collective-permute-start(f32[192,128]{1,0:T(8,128)} %get-tuple-element.20), channel_id=1, source_target_pairs={{4,0},{8,4},{12,8},{16,12},{20,16},{24,20},{28,24},{32,28},{36,32}... | collective-permute-start | bytes 294920 | tf_op jit(solution)/shard_map/ppermute | solution.py:270
  108.4 30.9 %copy-start.7 = (f32[2,32,512]{2,1,0:T(8,128)S(1)}, f32[2,32,512]{2,1,0:T(8,128)}, u32[]{:S(2)}) copy-start(f32[2,32,512]{2,1,0:T(8,128)} %param.22) | copy-start | bytes 393220
  113.2 45.2 %copy-start.29 = (s32[64]{0:T(128)S(1)}, s32[64]{0:T(128)}, u32[]{:S(2)}) copy-start(s32[64]{0:T(128)} %param.42) | copy-start | bytes 772
  124.5 34.4 %copy-start.3 = (bf16[32,512]{1,0:T(8,128)(2,1)S(1)}, bf16[32,512]{1,0:T(8,128)(2,1)}, u32[]{:S(2)}) copy-start(bf16[32,512]{1,0:T(8,128)(2,1)} %param.23) | copy-start | bytes 98308
  124.5 34.4 %copy-start.4 = (bf16[32,512]{1,0:T(8,128)(2,1)S(1)}, bf16[32,512]{1,0:T(8,128)(2,1)}, u32[]{:S(2)}) copy-start(bf16[32,512]{1,0:T(8,128)(2,1)} %param.24) | copy-start | bytes 98308
  124.5 32.0 %all-to-all-start.1 = ((f32[128,2,128]{2,1,0:T(2,128)}), f32[128,2,128]{2,1,0:T(2,128)S(1)}, u32[]{:S(2)}, u32[]{:S(2)}) async-start(f32[128,2,128]{2,1,0:T(2,128)} %copy.45), calls=%async_computation.1 | async-start | bytes 262144 | tf_op jit(solution)/shard_map/all_to_all | solution.py:281
  159.2 6.6 %collective-permute-start.8 = (f32[10,4,512]{2,1,0:T(4,128)S(1)}, f32[10,4,512]{2,1,0:T(4,128)S(1)}, u32[]{:S(2)}, u32[]{:S(2)}) collective-permute-start(f32[10,4,512]{2,1,0:T(4,128)S(1)} %get-tuple-element.43), channel_id=1, source_target_pairs={{0,4},{4,8},{8,12},{12,16},{16,20},{20,24},{24,28},{28,32},{32,36}... | collective-permute-start | bytes 245768 | tf_op jit(solution)/shard_map/ppermute | solution.py:28
  163.2 5.8 %collective-permute-start.9 = (f32[10,4,512]{2,1,0:T(4,128)S(1)}, f32[10,4,512]{2,1,0:T(4,128)S(1)}, u32[]{:S(2)}, u32[]{:S(2)}) collective-permute-start(f32[10,4,512]{2,1,0:T(4,128)S(1)} %get-tuple-element.44), channel_id=1, source_target_pairs={{4,0},{8,4},{12,8},{16,12},{20,16},{24,20},{28,24},{32,28},{36,32}... | collective-permute-start | bytes 245768 | tf_op jit(solution)/shard_map/ppermute | solution.py:29
  (21 other events, 103.5 us)

commit v10 on v7

--- a/solution.py
+++ b/solution.py
@@ -91,7 +91,7 @@
         arriving = inflow_ref[0, :, cols] * gathered[:, 0:128]
         for k in range(1, NBRS):
             arriving = arriving + inflow_ref[k, :, cols] * gathered[:, 128 * k : 128 * k + 128]
-        fresh = (energy + arriving - rate_ref[:, cols] * energy) * alive_ref[:, cols]
+        fresh = energy + arriving - rate_ref[:, cols] * energy
         out_ref[:, cols] = fresh
         if t == 0:
             first_ref[...] = fresh
@@ -236,10 +236,12 @@
     up = [(i, i + 1) for i in range(lax.axis_size(wave_axis) - 1)]
     down = [(j, i) for i, j in up]
     first, last = energy[:, :128], energy[:, -128:]
+    live_inflow = inflow * alive_mask[None]
+    live_rate = total_rate * alive_mask
     for sweep in range(WSTEPS):
         left = lax.ppermute(last, wave_axis, up)
         right = lax.ppermute(first, wave_axis, down)
-        energy, first, last = wave_sweep(left, energy, right, sel, inflow, total_rate, alive_mask)
+        energy, first, last = wave_sweep(left, energy, right, sel, live_inflow, live_rate, alive_mask)
     waves_out = energy.astype(jnp.bfloat16)
     coefficient = jnp.stack(
         [band_orbital * jnp.cos(band_angle), band_orbital * jnp.sin(band_angle)]

time: 169 us -> 172 us (1.018)
  waiting for transfers between devices: 56.4 us -> 58.7 us
    all_to_all x1, waiting for transfers between devices: 23.3 us -> 25.1 us  [per_device(): lax.all_to_all(packed, ('sec', 'tile'), split_axis=0, concat_axis=0, tile...]
  transfers between devices with their start and end apart: 12 -> 12, of which waited for: 7 -> 7; matrix products, arithmetic and copies ran while one was open for 3% -> 2% of each run, Pallas kernels for 0% -> 0%
where the time goes in v10:
time: 172 us; the launch traced here: 171 us
  starting transfers between devices  60 us (35%)
  waiting for transfers between devices  58.7 us (34%)
  Pallas kernels  16.4 us (10%)
  other arithmetic  12.8 us (7%)
  blocking collectives  8.69 us (5%)
  local copies, waits for them, and re-layouts  8.39 us (5%)
  matrix products  4.72 us (3%)
    all_to_all x1, waiting for transfers between devices, per_device(): lax.all_to_all(packed, ('sec', 'tile'), split_axis=0, concat_axis=0, tile...  25.1 us
    all_to_all x1, starting transfers between devices, per_device(): lax.all_to_all(packed, ('sec', 'tile'), split_axis=0, concat_axis=0, tile...  20.4 us
    all_to_all x1, waiting for transfers between devices, per_device(): lax.all_to_all(back_rows, ('sec', 'tile'), split_axis=0, concat_axis=0, t...  17.2 us
    pallas_call x4, Pallas kernels, wave_sweep(): pl.pallas_call(sweep_kernel, out_shape=(jax.ShapeDtypeStruct((bands, node...  16.4 us
    all_to_all x1, starting transfers between devices, per_device(): lax.all_to_all(back_rows, ('sec', 'tile'), split_axis=0, concat_axis=0, t...  14.7 us
    ppermute x4, waiting for transfers between devices, per_device(): right = lax.ppermute(first, wave_axis, down)  13.2 us
    ppermute x4, starting transfers between devices, per_device(): left = lax.ppermute(last, wave_axis, up)  9.86 us
    ppermute x4, starting transfers between devices, per_device(): right = lax.ppermute(first, wave_axis, down)  9.12 us
  transfers between devices with their start and end apart: 12, of which 7 were waited for; matrix products, arithmetic and copies ran while one was open for 2% of the time, Pallas kernels for 0%

profile of v10, /device:TPU:1, one launch (start us, length us, event | category | flops | bytes accessed | tf_op | source)
XLA Modules:
  0.0 171.0 jit_solution(2406862465830588873)
XLA Ops:
  9.2 20.4 %all-to-all-start = ((f32[128,1,514]{2,1,0:T(1,128)}), f32[128,1,514]{2,1,0:T(1,128)S(1)}, u32[]{:S(2)}, u32[]{:S(2)}) async-start(f32[128,1,514]{2,1,0:T(1,128)} %all_to_all.16), calls=%async_computation | async-start | bytes 655360 | tf_op jit(solution)/shard_map/all_to_all | solution.py:216
  29.9 25.1 %all-to-all-done = f32[128,1,514]{2,1,0:T(1,128)S(1)} async-done(((f32[128,1,514]{2,1,0:T(1,128)}), f32[128,1,514]{2,1,0:T(1,128)S(1)}, u32[]{:S(2)}, u32[]{:S(2)}) %all-to-all-start) | async-done | bytes 263200 | tf_op jit(solution)/shard_map/all_to_all | solution.py:216
  59.5 4.1 %collective-permute-start = (f32[192,128]{1,0:T(8,128)S(1)}, f32[192,128]{1,0:T(8,128)S(1)}, u32[]{:S(2)}, u32[]{:S(2)}) collective-permute-start(f32[192,128]{1,0:T(8,128)S(1)} %get-tuple-element.48), channel_id=1, source_target_pairs={{0,4},{4,8},{8,12},{12,16},{16,20},{20,24},{24,28},{28,32},{32,36}... | collective-permute-start | bytes 294920 | tf_op jit(solution)/shard_map/ppermute | solution.py:242
  63.6 1.9 %collective-permute-start.1 = (f32[192,128]{1,0:T(8,128)S(1)}, f32[192,128]{1,0:T(8,128)S(1)}, u32[]{:S(2)}, u32[]{:S(2)}) collective-permute-start(f32[192,128]{1,0:T(8,128)S(1)} %get-tuple-element.47), channel_id=1, source_target_pairs={{4,0},{8,4},{12,8},{16,12},{20,16},{24,20},{28,24},{32,28},{36,32}... | collective-permute-start | bytes 294920 | tf_op jit(solution)/shard_map/ppermute | solution.py:243
  67.2 2.3 %collective-permute-done.1.right_ref = f32[192,128]{1,0:T(8,128)S(1)} collective-permute-done((f32[192,128]{1,0:T(8,128)S(1)}, f32[192,128]{1,0:T(8,128)S(1)}, u32[]{:S(2)}, u32[]{:S(2)}) %collective-permute-start.1) | collective-permute-done | bytes 98336 | tf_op jit(solution)/shard_map/ppermute | solution.py:243
  70.2 4.1 %shard_map.221 = (f32[192,512]{1,0:T(8,128)}, f32[192,128]{1,0:T(8,128)}, f32[192,128]{1,0:T(8,128)}) custom-call(f32[192,128]{1,0:T(8,128)} %copy-done.11, f32[192,512]{1,0:T(8,128)} %copy-done.1, f32[192,128]{1,0:T(8,128)} %copy-done.12, bf16[4,384,512]{2,1,0:T(8,128)(2,1)} %fusion.sel_ref, f32[4,192,512]{2,1,0:T(8,128)} %get-tuple-element.46.inflow_ref, ...), custom_call_target="tpu_custom_call" | custom-call | flops 603979776 | bytes 4521984 | tf_op jit(solution)/shard_map/pallas_call | solution.py:108
  74.3 1.9 %collective-permute-start.2 = (f32[192,128]{1,0:T(8,128)}, f32[192,128]{1,0:T(8,128)S(1)}, u32[]{:S(2)}, u32[]{:S(2)}) collective-permute-start(f32[192,128]{1,0:T(8,128)} %get-tuple-element.12), channel_id=1, source_target_pairs={{0,4},{4,8},{8,12},{12,16},{16,20},{20,24},{24,28},{28,32},{32,36}... | collective-permute-start | bytes 294920 | tf_op jit(solution)/shard_map/ppermute | solution.py:242
  76.2 2.4 %collective-permute-start.3 = (f32[192,128]{1,0:T(8,128)}, f32[192,128]{1,0:T(8,128)S(1)}, u32[]{:S(2)}, u32[]{:S(2)}) collective-permute-start(f32[192,128]{1,0:T(8,128)} %get-tuple-element.14), channel_id=1, source_target_pairs={{4,0},{8,4},{12,8},{16,12},{20,16},{24,20},{28,24},{32,28},{36,32}... | collective-permute-start | bytes 294920 | tf_op jit(solution)/shard_map/ppermute | solution.py:243
  78.6 3.7 %collective-permute-done.3.right_ref = f32[192,128]{1,0:T(8,128)S(1)} collective-permute-done((f32[192,128]{1,0:T(8,128)}, f32[192,128]{1,0:T(8,128)S(1)}, u32[]{:S(2)}, u32[]{:S(2)}) %collective-permute-start.3) | collective-permute-done | bytes 98336 | tf_op jit(solution)/shard_map/ppermute | solution.py:243
  83.0 4.1 %shard_map.222 = (f32[192,512]{1,0:T(8,128)}, f32[192,128]{1,0:T(8,128)}, f32[192,128]{1,0:T(8,128)}) custom-call(f32[192,128]{1,0:T(8,128)} %copy-done.13, f32[192,512]{1,0:T(8,128)} %get-tuple-element.13.energy_ref, f32[192,128]{1,0:T(8,128)} %copy-done.15, bf16[4,384,512]{2,1,0:T(8,128)(2,1)} %fusion.sel_ref, ...), custom_call_target="tpu_custom_call" | custom-call | flops 603979776 | bytes 4521984 | tf_op jit(solution)/shard_map/pallas_call | solution.py:108
  87.1 1.9 %collective-permute-start.4 = (f32[192,128]{1,0:T(8,128)}, f32[192,128]{1,0:T(8,128)S(1)}, u32[]{:S(2)}, u32[]{:S(2)}) collective-permute-start(f32[192,128]{1,0:T(8,128)} %get-tuple-element.15), channel_id=1, source_target_pairs={{0,4},{4,8},{8,12},{12,16},{16,20},{20,24},{24,28},{28,32},{32,36}... | collective-permute-start | bytes 294920 | tf_op jit(solution)/shard_map/ppermute | solution.py:242
  89.0 2.4 %collective-permute-start.5 = (f32[192,128]{1,0:T(8,128)}, f32[192,128]{1,0:T(8,128)S(1)}, u32[]{:S(2)}, u32[]{:S(2)}) collective-permute-start(f32[192,128]{1,0:T(8,128)} %get-tuple-element.17), channel_id=1, source_target_pairs={{4,0},{8,4},{12,8},{16,12},{20,16},{24,20},{28,24},{32,28},{36,32}... | collective-permute-start | bytes 294920 | tf_op jit(solution)/shard_map/ppermute | solution.py:243
  91.4 3.7 %collective-permute-done.5.right_ref = f32[192,128]{1,0:T(8,128)S(1)} collective-permute-done((f32[192,128]{1,0:T(8,128)}, f32[192,128]{1,0:T(8,128)S(1)}, u32[]{:S(2)}, u32[]{:S(2)}) %collective-permute-start.5) | collective-permute-done | bytes 98336 | tf_op jit(solution)/shard_map/ppermute | solution.py:243
  95.8 4.1 %shard_map.223 = (f32[192,512]{1,0:T(8,128)}, f32[192,128]{1,0:T(8,128)}, f32[192,128]{1,0:T(8,128)}) custom-call(f32[192,128]{1,0:T(8,128)} %copy-done.14, f32[192,512]{1,0:T(8,128)} %get-tuple-element.16.energy_ref, f32[192,128]{1,0:T(8,128)} %copy-done.16, bf16[4,384,512]{2,1,0:T(8,128)(2,1)} %fusion.sel_ref, ...), custom_call_target="tpu_custom_call" | custom-call | flops 603979776 | bytes 4521984 | tf_op jit(solution)/shard_map/pallas_call | solution.py:108
  99.9 1.9 %collective-permute-start.6 = (f32[192,128]{1,0:T(8,128)}, f32[192,128]{1,0:T(8,128)S(1)}, u32[]{:S(2)}, u32[]{:S(2)}) collective-permute-start(f32[192,128]{1,0:T(8,128)} %get-tuple-element.18), channel_id=1, source_target_pairs={{0,4},{4,8},{8,12},{12,16},{16,20},{20,24},{24,28},{28,32},{32,36}... | collective-permute-start | bytes 294920 | tf_op jit(solution)/shard_map/ppermute | solution.py:242
  101.8 2.4 %collective-permute-start.7 = (f32[192,128]{1,0:T(8,128)}, f32[192,128]{1,0:T(8,128)S(1)}, u32[]{:S(2)}, u32[]{:S(2)}) collective-permute-start(f32[192,128]{1,0:T(8,128)} %get-tuple-element.20), channel_id=1, source_target_pairs={{4,0},{8,4},{12,8},{16,12},{20,16},{24,20},{28,24},{32,28},{36,32}... | collective-permute-start | bytes 294920 | tf_op jit(solution)/shard_map/ppermute | solution.py:243
  104.4 3.5 %collective-permute-done.7.right_ref = f32[192,128]{1,0:T(8,128)S(1)} collective-permute-done((f32[192,128]{1,0:T(8,128)}, f32[192,128]{1,0:T(8,128)S(1)}, u32[]{:S(2)}, u32[]{:S(2)}) %collective-permute-start.7) | collective-permute-done | bytes 98336 | tf_op jit(solution)/shard_map/ppermute | solution.py:243
  108.6 4.1 %shard_map.224 = (f32[192,512]{1,0:T(8,128)}, f32[192,128]{1,0:T(8,128)}, f32[192,128]{1,0:T(8,128)}) custom-call(f32[192,128]{1,0:T(8,128)} %copy-done.9, f32[192,512]{1,0:T(8,128)} %get-tuple-element.19.energy_ref, f32[192,128]{1,0:T(8,128)} %copy-done.10, bf16[4,384,512]{2,1,0:T(8,128)(2,1)} %fusion.sel_ref, f32[4,192,512]{2,1,0:T(8,128)} %get-tuple-element.46.inflow_ref, ...), custom_call_target="tpu_custom_call" | custom-call | flops 603979776 | bytes 4521984 | tf_op jit(solution)/shard_map/pallas_call | solution.py:108
  114.2 8.7 %psum.7 = f32[8,128]{1,0:T(8,128)S(1)} all-reduce(f32[8,128]{1,0:T(8,128)S(1)} %reshape.189), channel_id=1, replica_groups=mesh['sec'=4,'tile'=32,'lev'=4] {'lev'}, use_global_device_ids=true, to_apply=%region_4.5 | all-reduce | flops 1024 | bytes 8192 | tf_op jit(solution)/shard_map/psum | solution.py:249
  124.0 14.7 %all-to-all-start.1 = ((f32[128,2,128]{2,1,0:T(2,128)}), f32[128,2,128]{2,1,0:T(2,128)S(1)}, u32[]{:S(2)}, u32[]{:S(2)}) async-start(f32[128,2,128]{2,1,0:T(2,128)} %copy.45), calls=%async_computation.1 | async-start | bytes 262144 | tf_op jit(solution)/shard_map/all_to_all | solution.py:254
  138.8 17.2 %all-to-all-done.1 = f32[128,2,128]{2,1,0:T(2,128)S(1)} async-done(((f32[128,2,128]{2,1,0:T(2,128)}), f32[128,2,128]{2,1,0:T(2,128)S(1)}, u32[]{:S(2)}, u32[]{:S(2)}) %all-to-all-start.1) | async-done | bytes 131104 | tf_op jit(solution)/shard_map/all_to_all | solution.py:254
  158.7 3.9 %collective-permute-start.8 = (f32[10,4,512]{2,1,0:T(4,128)S(1)}, f32[10,4,512]{2,1,0:T(4,128)S(1)}, u32[]{:S(2)}, u32[]{:S(2)}) collective-permute-start(f32[10,4,512]{2,1,0:T(4,128)S(1)} %get-tuple-element.43), channel_id=1, source_target_pairs={{0,4},{4,8},{8,12},{12,16},{16,20},{20,24},{24,28},{28,32},{32,36}... | collective-permute-start | bytes 245768 | tf_op jit(solution)/shard_map/ppermute | solution.py:28
  162.7 1.9 %collective-permute-start.9 = (f32[10,4,512]{2,1,0:T(4,128)S(1)}, f32[10,4,512]{2,1,0:T(4,128)S(1)}, u32[]{:S(2)}, u32[]{:S(2)}) collective-permute-start(f32[10,4,512]{2,1,0:T(4,128)S(1)} %get-tuple-element.44), channel_id=1, source_target_pairs={{4,0},{8,4},{12,8},{16,12},{20,16},{24,20},{28,24},{32,28},{36,32}... | collective-permute-start | bytes 245768 | tf_op jit(solution)/shard_map/ppermute | solution.py:29
  165.3 3.1 %collective-permute-done.9 = f32[10,4,512]{2,1,0:T(4,128)S(1)} collective-permute-done((f32[10,4,512]{2,1,0:T(4,128)S(1)}, f32[10,4,512]{2,1,0:T(4,128)S(1)}, u32[]{:S(2)}, u32[]{:S(2)}) %collective-permute-start.9) | collective-permute-done | bytes 81952 | tf_op jit(solution)/shard_map/ppermute | solution.py:29
  (159 shorter events, 25.9 us)
Async XLA Ops:
  4.7 24.9 %copy-start.24 = (s32[512]{0:T(512)S(1)}, s32[512]{0:T(512)}, u32[]{:S(2)}) copy-start(s32[512]{0:T(512)} %param.39) | copy-start | bytes 6148
  4.7 24.9 %copy-start.22 = (s32[4,512]{1,0:T(4,128)S(1)}, s32[4,512]{1,0:T(4,128)}, u32[]{:S(2)}) copy-start(s32[4,512]{1,0:T(4,128)} %param.37) | copy-start | bytes 24580
  4.7 24.9 %copy-start.26 = (f32[192]{0:T(256)S(1)}, f32[192]{0:T(256)}, u32[]{:S(2)}) copy-start(f32[192]{0:T(256)} %param.33) | copy-start | bytes 2308
  4.7 24.9 %copy-start.27 = (f32[192]{0:T(256)S(1)}, f32[192]{0:T(256)}, u32[]{:S(2)}) copy-start(f32[192]{0:T(256)} %param.34) | copy-start | bytes 2308
  4.8 25.0 %copy-start.21 = (f32[4,512]{1,0:T(4,128)S(1)}, f32[4,512]{1,0:T(4,128)}, u32[]{:S(2)}) copy-start(f32[4,512]{1,0:T(4,128)} %param.38) | copy-start | bytes 24580
  9.2 45.8 %all-to-all-start = ((f32[128,1,514]{2,1,0:T(1,128)}), f32[128,1,514]{2,1,0:T(1,128)S(1)}, u32[]{:S(2)}, u32[]{:S(2)}) async-start(f32[128,1,514]{2,1,0:T(1,128)} %all_to_all.16), calls=%async_computation | async-start | bytes 655360 | tf_op jit(solution)/shard_map/all_to_all | solution.py:216
  29.6 28.9 %copy-start.8 = (f32[512]{0:T(512)}, f32[512]{0:T(512)S(1)}, u32[]{:S(2)}) copy-start(f32[512]{0:T(512)S(1)} %convert_element_type.87) | copy-start | bytes 6148
  59.5 7.7 %collective-permute-start = (f32[192,128]{1,0:T(8,128)S(1)}, f32[192,128]{1,0:T(8,128)S(1)}, u32[]{:S(2)}, u32[]{:S(2)}) collective-permute-start(f32[192,128]{1,0:T(8,128)S(1)} %get-tuple-element.48), channel_id=1, source_target_pairs={{0,4},{4,8},{8,12},{12,16},{16,20},{20,24},{24,28},{28,32},{32,36}... | collective-permute-start | bytes 294920 | tf_op jit(solution)/shard_map/ppermute | solution.py:242
  63.6 5.9 %collective-permute-start.1 = (f32[192,128]{1,0:T(8,128)S(1)}, f32[192,128]{1,0:T(8,128)S(1)}, u32[]{:S(2)}, u32[]{:S(2)}) collective-permute-start(f32[192,128]{1,0:T(8,128)S(1)} %get-tuple-element.47), channel_id=1, source_target_pairs={{4,0},{8,4},{12,8},{16,12},{20,16},{24,20},{28,24},{32,28},{36,32}... | collective-permute-start | bytes 294920 | tf_op jit(solution)/shard_map/ppermute | solution.py:243
  74.3 4.3 %collective-permute-start.2 = (f32[192,128]{1,0:T(8,128)}, f32[192,128]{1,0:T(8,128)S(1)}, u32[]{:S(2)}, u32[]{:S(2)}) collective-permute-start(f32[192,128]{1,0:T(8,128)} %get-tuple-element.12), channel_id=1, source_target_pairs={{0,4},{4,8},{8,12},{12,16},{16,20},{20,24},{24,28},{28,32},{32,36}... | collective-permute-start | bytes 294920 | tf_op jit(solution)/shard_map/ppermute | solution.py:242
  76.2 6.1 %collective-permute-start.3 = (f32[192,128]{1,0:T(8,128)}, f32[192,128]{1,0:T(8,128)S(1)}, u32[]{:S(2)}, u32[]{:S(2)}) collective-permute-start(f32[192,128]{1,0:T(8,128)} %get-tuple-element.14), channel_id=1, source_target_pairs={{4,0},{8,4},{12,8},{16,12},{20,16},{24,20},{28,24},{32,28},{36,32}... | collective-permute-start | bytes 294920 | tf_op jit(solution)/shard_map/ppermute | solution.py:243
  87.1 4.3 %collective-permute-start.4 = (f32[192,128]{1,0:T(8,128)}, f32[192,128]{1,0:T(8,128)S(1)}, u32[]{:S(2)}, u32[]{:S(2)}) collective-permute-start(f32[192,128]{1,0:T(8,128)} %get-tuple-element.15), channel_id=1, source_target_pairs={{0,4},{4,8},{8,12},{12,16},{16,20},{20,24},{24,28},{28,32},{32,36}... | collective-permute-start | bytes 294920 | tf_op jit(solution)/shard_map/ppermute | solution.py:242
  89.0 6.1 %collective-permute-start.5 = (f32[192,128]{1,0:T(8,128)}, f32[192,128]{1,0:T(8,128)S(1)}, u32[]{:S(2)}, u32[]{:S(2)}) collective-permute-start(f32[192,128]{1,0:T(8,128)} %get-tuple-element.17), channel_id=1, source_target_pairs={{4,0},{8,4},{12,8},{16,12},{20,16},{24,20},{28,24},{32,28},{36,32}... | collective-permute-start | bytes 294920 | tf_op jit(solution)/shard_map/ppermute | solution.py:243
  99.9 4.6 %collective-permute-start.6 = (f32[192,128]{1,0:T(8,128)}, f32[192,128]{1,0:T(8,128)S(1)}, u32[]{:S(2)}, u32[]{:S(2)}) collective-permute-start(f32[192,128]{1,0:T(8,128)} %get-tuple-element.18), channel_id=1, source_target_pairs={{0,4},{4,8},{8,12},{12,16},{16,20},{20,24},{24,28},{28,32},{32,36}... | collective-permute-start | bytes 294920 | tf_op jit(solution)/shard_map/ppermute | solution.py:242
  101.8 6.1 %collective-permute-start.7 = (f32[192,128]{1,0:T(8,128)}, f32[192,128]{1,0:T(8,128)S(1)}, u32[]{:S(2)}, u32[]{:S(2)}) collective-permute-start(f32[192,128]{1,0:T(8,128)} %get-tuple-element.20), channel_id=1, source_target_pairs={{4,0},{8,4},{12,8},{16,12},{20,16},{24,20},{28,24},{32,28},{36,32}... | collective-permute-start | bytes 294920 | tf_op jit(solution)/shard_map/ppermute | solution.py:243
  108.6 30.2 %copy-start.7 = (f32[2,32,512]{2,1,0:T(8,128)S(1)}, f32[2,32,512]{2,1,0:T(8,128)}, u32[]{:S(2)}) copy-start(f32[2,32,512]{2,1,0:T(8,128)} %param.22) | copy-start | bytes 393220
  112.7 45.2 %copy-start.29 = (s32[64]{0:T(128)S(1)}, s32[64]{0:T(128)}, u32[]{:S(2)}) copy-start(s32[64]{0:T(128)} %param.42) | copy-start | bytes 772
  124.0 34.4 %copy-start.3 = (bf16[32,512]{1,0:T(8,128)(2,1)S(1)}, bf16[32,512]{1,0:T(8,128)(2,1)}, u32[]{:S(2)}) copy-start(bf16[32,512]{1,0:T(8,128)(2,1)} %param.23) | copy-start | bytes 98308
  124.0 34.4 %copy-start.4 = (bf16[32,512]{1,0:T(8,128)(2,1)S(1)}, bf16[32,512]{1,0:T(8,128)(2,1)}, u32[]{:S(2)}) copy-start(bf16[32,512]{1,0:T(8,128)(2,1)} %param.24) | copy-start | bytes 98308
  124.0 32.0 %all-to-all-start.1 = ((f32[128,2,128]{2,1,0:T(2,128)}), f32[128,2,128]{2,1,0:T(2,128)S(1)}, u32[]{:S(2)}, u32[]{:S(2)}) async-start(f32[128,2,128]{2,1,0:T(2,128)} %copy.45), calls=%async_computation.1 | async-start | bytes 262144 | tf_op jit(solution)/shard_map/all_to_all | solution.py:254
  138.7 19.7 %copy-start.30 = (f32[2]{0:T(128)S(1)}, f32[2]{0:T(128)}, u32[]{:S(2)}) copy-start(f32[2]{0:T(128)} %param.30) | copy-start | bytes 28
  138.7 19.7 %copy-start.31 = (f32[2]{0:T(128)S(1)}, f32[2]{0:T(128)}, u32[]{:S(2)}) copy-start(f32[2]{0:T(128)} %param.31) | copy-start | bytes 28
  158.7 6.6 %collective-permute-start.8 = (f32[10,4,512]{2,1,0:T(4,128)S(1)}, f32[10,4,512]{2,1,0:T(4,128)S(1)}, u32[]{:S(2)}, u32[]{:S(2)}) collective-permute-start(f32[10,4,512]{2,1,0:T(4,128)S(1)} %get-tuple-element.43), channel_id=1, source_target_pairs={{0,4},{4,8},{8,12},{12,16},{16,20},{20,24},{24,28},{28,32},{32,36}... | collective-permute-start | bytes 245768 | tf_op jit(solution)/shard_map/ppermute | solution.py:28
  162.7 5.8 %collective-permute-start.9 = (f32[10,4,512]{2,1,0:T(4,128)S(1)}, f32[10,4,512]{2,1,0:T(4,128)S(1)}, u32[]{:S(2)}, u32[]{:S(2)}) collective-permute-start(f32[10,4,512]{2,1,0:T(4,128)S(1)} %get-tuple-element.44), channel_id=1, source_target_pairs={{4,0},{8,4},{12,8},{16,12},{20,16},{24,20},{28,24},{32,28},{36,32}... | collective-permute-start | bytes 245768 | tf_op jit(solution)/shard_map/ppermute | solution.py:29
  (21 other events, 69.0 us)
